TPU v7x, 128 devices: a whole 4x4x4 slice. The times are simulated.
128 devices in a mesh: gx: 4 (over z), gy: 16 (over x, y_lo, core), gz: 2 (over y_hi).
Axes of the slice: x: 4, y: 4 (y_hi: 2, y_lo: 2; y = y_hi * 2 + y_lo), z: 4, core: 2. Of those that a mesh axis runs over, the one named last changes fastest.
Arguments:
- right_side: float32 [64, 1024, 512], P('gx', 'gy', 'gz'), may hold values from -4 to 4
- initial_guess: float32 [64, 1024, 512], P('gx', 'gy', 'gz'), may hold values from -3 to 3
- damping: float32 [64, 1024, 512], P('gx', 'gy', 'gz'), may hold values from 0.1 to 4
- group_map: int32 [16, 256, 128], P('gx', 'gy', 'gz'), may hold values from 0 to 1023
- block_inverse: float32 [1024, 1024], P('gy'), may hold values from -0.1875 to 0.1875
Outputs:
- fine_iterate: float32 [64, 1024, 512], P('gx', 'gy', 'gz')
- middle_correction: float32 [32, 512, 256], P('gx', 'gy', 'gz')
- coarse_correction: float32 [16, 256, 128], P('gx', 'gy', 'gz')
- aggregate_solution: float32 [1024], P('gy')
All inputs are finite; a program needn't handle non-finite values.
Results may differ from a plain program's by a relative error of at most 0.0003.
Values sent between devices are 32-bit elements; how exact they have to be, the bound alone decides.
No kernel may reach another device: no remote copies, remote signals or barrier semaphores. Data moves between devices by JAX's collectives and lax.ppermute only.
A program may use at most 192 MiB of HBM per device.

v0:
```python
import math

import jax
import jax.numpy as jnp
from jax import lax
from jax.sharding import PartitionSpec as P

SWEEPS = 4
NAGG = 1024
DIGITS = 32


OMEGA = 0.8


def with_halo(cells, sides, width):
    for axis, dim in sides:
        count = lax.axis_size(axis)
        ends = count - 1
        head = lax.slice_in_dim(cells, 0, width, axis=dim)
        tail = lax.slice_in_dim(cells, cells.shape[dim] - width, cells.shape[dim], axis=dim)
        cells = jnp.concatenate(
            [
                lax.ppermute(tail, axis, [(i, (i + 1) % count) for i in range(ends)]),
                cells,
                lax.ppermute(head, axis, [((i + 1) % count, i) for i in range(ends)]),
            ],
            axis=dim,
        )
    return cells


def neighbours(padded):
    total = padded[2:, 1:-1, 1:-1] + padded[:-2, 1:-1, 1:-1]
    total = total + padded[1:-1, 2:, 1:-1] + padded[1:-1, :-2, 1:-1]
    return total + padded[1:-1, 1:-1, 2:] + padded[1:-1, 1:-1, :-2]


def relax(padded, source, diagonal):
    centre = padded[1:-1, 1:-1, 1:-1]
    return centre + OMEGA * (source - (diagonal * centre - neighbours(padded))) / diagonal


def defect(padded, source, diagonal):
    centre = padded[1:-1, 1:-1, 1:-1]
    return source - (diagonal * centre - neighbours(padded))


def pair_matrix(rows, cols, along):
    row = lax.broadcasted_iota(jnp.int32, (rows, cols), 0)
    col = lax.broadcasted_iota(jnp.int32, (rows, cols), 1)
    if along == 0:
        return (col // 2 == row).astype(jnp.float32)
    return (row // 2 == col).astype(jnp.float32)


def shrink(field):
    extent_a, extent_b, extent_c = field.shape
    halves = field.reshape(extent_a // 2, 2, extent_b, extent_c)
    flat = (halves[:, 0] + halves[:, 1]).reshape(extent_a // 2 * extent_b, extent_c)
    rows = extent_a // 2 * extent_b
    flat = jnp.dot(pair_matrix(rows // 2, rows, 0), flat, precision=lax.Precision.HIGHEST)
    flat = jnp.dot(flat, pair_matrix(extent_c, extent_c // 2, 1), precision=lax.Precision.HIGHEST)
    return flat.reshape(extent_a // 2, extent_b // 2, extent_c // 2) * 0.125


def exchange(stack, width):
    for axis, dim in (("gz", 3), ("gy", 2), ("gx", 1)):
        count = lax.axis_size(axis)
        head = lax.slice_in_dim(stack, 0, width, axis=dim)
        tail = lax.slice_in_dim(stack, stack.shape[dim] - width, stack.shape[dim], axis=dim)
        stack = jnp.concatenate(
            [
                lax.ppermute(tail, axis, [(i, i + 1) for i in range(count - 1)]),
                stack,
                lax.ppermute(head, axis, [(i + 1, i) for i in range(count - 1)]),
            ],
            axis=dim,
        )
    return stack


def inside(shape, width):
    masks = []
    for axis, extent in zip(("gx", "gy", "gz"), shape):
        place = lax.axis_index(axis) * extent - width
        place = place + lax.broadcasted_iota(jnp.int32, (extent + 2 * width,), 0)
        masks.append((place >= 0) & (place < extent * lax.axis_size(axis)))
    return masks[0][:, None, None] & masks[1][None, :, None] & masks[2][None, None, :]


def crop(field, k):
    if k == 0:
        return field
    return field[k:-k, k:-k, k:-k]


def smooth_wide(start, source, diagonal, mask, steps):
    current = start
    for step in range(1, steps + 1):
        current = relax(current, crop(source, step), crop(diagonal, step))
        current = jnp.where(crop(mask, step), current, 0.0)
    return current


def coarser_level(source, damp):
    width = SWEEPS
    wide = exchange(jnp.stack([source, damp]), width)
    wide_source = wide[0]
    wide_diag = 6.0 + wide[1]
    mask = inside(source.shape, width)
    start = jnp.where(mask, OMEGA * wide_source / wide_diag, 0.0)
    current = smooth_wide(start, wide_source, wide_diag, mask, SWEEPS - 1)
    return crop(current, 1), defect(current, source, 6.0 + damp)


def shards(right_side, initial_guess, damping, group_map, block_inverse):
    width = SWEEPS + 1
    wide = exchange(jnp.stack([initial_guess, right_side, damping]), width)
    wide_source = wide[1]
    wide_diag = 6.0 + wide[2]
    mask = inside(right_side.shape, width)
    current = smooth_wide(wide[0], wide_source, wide_diag, mask, SWEEPS)
    iterate = crop(current, 1)
    fine_defect = defect(current, right_side, 6.0 + damping)
    middle_damp = 4.0 * shrink(damping)
    middle_source = 4.0 * shrink(fine_defect)
    middle, middle_defect = coarser_level(middle_source, middle_damp)
    coarse_damp = 4.0 * shrink(middle_damp)
    coarse_source = 4.0 * shrink(middle_defect)
    coarse, coarse_defect = coarser_level(coarse_source, coarse_damp)
    cells = coarse_defect.size
    digits = DIGITS
    owner = group_map.reshape(cells, 1)
    letters = lax.broadcasted_iota(jnp.int32, (cells, digits), 1)
    high = (owner // digits == letters).astype(jnp.float32) * coarse_defect.reshape(cells, 1)
    low = (owner % digits == letters).astype(jnp.float32)
    partial_sums = lax.dot_general(
        high, low, (((0,), (0,)), ((), ())), precision=lax.Precision.HIGHEST
    ).reshape(NAGG)
    summed = lax.psum(partial_sums, "gz")
    summed = lax.psum(summed, "gx")
    splits = ((1, 2), (2, 2), (4, 4)) if lax.axis_size("gy") == 16 else ((1, lax.axis_size("gy")),)
    for stride, span in splits:
        groups = [
            [base + stride * k for k in range(span)]
            for base in range(lax.axis_size("gy"))
            if base % (stride * span) < stride
        ]
        summed = lax.psum(summed, "gy", axis_index_groups=groups)
    group_cells = (
        coarse_source.size * lax.axis_size("gx") * lax.axis_size("gy") * lax.axis_size("gz") // NAGG
    )
    aggregate_source = summed / math.sqrt(group_cells)
    solution = jnp.dot(block_inverse, aggregate_source, precision=lax.Precision.HIGHEST)
    return (iterate, middle, coarse, solution)


def solution(mesh):
    return jax.shard_map(
        shards,
        mesh=mesh,
        in_specs=(
            P("gx", "gy", "gz"),
            P("gx", "gy", "gz"),
            P("gx", "gy", "gz"),
            P("gx", "gy", "gz"),
            P("gy", None),
        ),
        out_specs=(P("gx", "gy", "gz"), P("gx", "gy", "gz"), P("gx", "gy", "gz"), P("gy")),
        check_vma=False,
    )
```

profile of v0, /device:TPU:1, one launch (start us, length us, event | category | flops | bytes accessed | tf_op | source)
XLA Modules:
  0.0 250.5 jit_solution(1123585572657354928)
XLA Ops:
  6.7 6.3 %collective-permute-start = (f32[3,16,64,5]{2,1,3,0:T(8,128)S(1)}, f32[3,16,64,5]{2,1,3,0:T(8,128)}, u32[]{:S(2)}, u32[]{:S(2)}) collective-permute-start(f32[3,16,64,5]{2,1,3,0:T(8,128)S(1)} %copy.45), channel_id=1, source_target_pairs={{0,1},{2,3},{4,5},{6,7},{8,9},{10,11},{12,13},{14,15},{16,17},{18,... | collective-permute-start | bytes 184328 | tf_op jit(solution)/shard_map/ppermute | solution.py:74
  44.3 4.5 %pad_maximum_fusion.8 = (f32[3,5,74,266]{3,2,1,0:T(8,128)}, f32[3,5,74,266]{3,2,1,0:T(8,128)}) fusion(f32[3,16,5,266]{3,2,1,0:T(8,128)S(1)} %copy.52, f32[3,16,5,266]{3,2,1,0:T(8,128)S(1)} %copy.51, f32[3,16,64,5]{3,2,1,0:T(8,128)} %copy.48, f32[3,16,64,5]{3,2,1,0:T(8,128)S(1)} %copy-done.3, f32[1,16,64,256]{3,2,1,0:T(8,128)S(1)} %bitcast.57, ...), kind=kLoop, calls=%fused_computation.56 | loop fusion | flops 3543120 | bytes 6141408 | tf_op jit(solution)/shard_map/slice | solution.py:71
  48.8 4.9 %collective-permute-start.4 = (f32[3,5,74,266]{3,2,1,0:T(8,128)}, f32[3,5,74,266]{3,2,1,0:T(8,128)}, u32[]{:S(2)}, u32[]{:S(2)}) collective-permute-start(f32[3,5,74,266]{3,2,1,0:T(8,128)} %get-tuple-element.21), channel_id=1, source_target_pairs={{0,32},{32,64},{64,96},{1,33},{33,65},{65,97},{2,34},{34,66},{66,9... | collective-permute-start | bytes 3543128 | tf_op jit(solution)/shard_map/ppermute | solution.py:74
  60.8 28.6 %collective-permute-done.4 = f32[3,5,74,266]{3,2,1,0:T(8,128)} collective-permute-done((f32[3,5,74,266]{3,2,1,0:T(8,128)}, f32[3,5,74,266]{3,2,1,0:T(8,128)}, u32[]{:S(2)}, u32[]{:S(2)}) %collective-permute-start.4) | collective-permute-done | bytes 1181072 | tf_op jit(solution)/shard_map/ppermute | solution.py:74
  89.4 5.4 %collective-permute-done.5 = f32[3,5,74,266]{3,2,1,0:T(8,128)} collective-permute-done((f32[3,5,74,266]{3,2,1,0:T(8,128)}, f32[3,5,74,266]{3,2,1,0:T(8,128)}, u32[]{:S(2)}, u32[]{:S(2)}) %collective-permute-start.5) | collective-permute-done | bytes 1181072 | tf_op jit(solution)/shard_map/ppermute | solution.py:76
  94.8 11.5 %pad_maximum_fusion = f32[3,26,74,266]{3,2,1,0:T(8,128)} fusion(f32[3,5,74,266]{3,2,1,0:T(8,128)} %collective-permute-done.5, f32[3,16,5,266]{3,2,1,0:T(8,128)} %copy-done.6, f32[3,16,64,5]{3,2,1,0:T(8,128)} %copy.48, f32[1,16,64,256]{3,2,1,0:T(8,128)S(1)} %bitcast.58, f32[1,16,64,256]{3,2,1,0:T(8,128)S(1)} %bitcast.62, f32[1,16,64,256]{3,2,1,0:T(8,128)S(1)} %bitcast.66, ...), kind=kLoop, calls=%fused_computation | loop fusion | flops 12282816 | bytes 12282816 | tf_op jit(solution)/shard_map/concatenate | solution.py:72
  106.3 4.5 %fusion = (f32[26,74,266]{2,1,0:T(8,128)S(1)}, f32[26,74,266]{2,1,0:T(8,128)S(1)}, f32[26,74,266]{2,1,0:T(8,128)S(1)}) fusion(f32[3,26,74,266]{3,2,1,0:T(8,128)} %pad_maximum_fusion), kind=kLoop, calls=%fused_computation.2 | loop fusion | flops 511784 | bytes 12282816 | tf_op jit(solution)/shard_map/add | solution.py:121
  110.9 7.2 %fusion.6 = f32[24,72,264]{2,1,0:T(8,128)S(1)} fusion(f32[26,74,266]{2,1,0:T(8,128)S(1)} %get-tuple-element.20, f32[26,74,266]{2,1,0:T(8,128)S(1)} %get-tuple-element.19, f32[26,74,266]{2,1,0:T(8,128)S(1)} %get-tuple-element.18, pred[26,74,266]{2,1,0:T(8,128)(4,1)S(1)} %broadcast_and_fusion), kind=kLoop, calls=%fused_computation.12 | loop fusion | flops 5474304 | bytes 18703872 | tf_op jit(solution)/shard_map/jit(_where)/select_n | solution.py:102
  118.0 6.5 %fusion.12 = f32[22,70,262]{2,1,0:T(8,128)S(1)} fusion(f32[24,72,264]{2,1,0:T(8,128)S(1)} %fusion.6, f32[26,74,266]{2,1,0:T(8,128)S(1)} %get-tuple-element.19, f32[26,74,266]{2,1,0:T(8,128)S(1)} %get-tuple-element.18, pred[26,74,266]{2,1,0:T(8,128)(4,1)S(1)} %broadcast_and_fusion), kind=kLoop, calls=%fused_computation.23 | loop fusion | flops 4841760 | bytes 16542680 | tf_op jit(solution)/shard_map/jit(_where)/select_n | solution.py:102
  124.6 6.2 %fusion.18 = f32[20,68,260]{2,1,0:T(8,128)S(1)} fusion(f32[22,70,262]{2,1,0:T(8,128)S(1)} %fusion.12, f32[26,74,266]{2,1,0:T(8,128)S(1)} %get-tuple-element.19, f32[26,74,266]{2,1,0:T(8,128)S(1)} %get-tuple-element.18, pred[26,74,266]{2,1,0:T(8,128)(4,1)S(1)} %broadcast_and_fusion), kind=kLoop, calls=%fused_computation.34 | loop fusion | flops 4243200 | bytes 14497600 | tf_op jit(solution)/shard_map/jit(_where)/select_n | solution.py:102
  130.8 5.4 %fusion.24 = f32[18,66,258]{2,1,0:T(8,128)S(1)} fusion(f32[20,68,260]{2,1,0:T(8,128)S(1)} %fusion.18, f32[26,74,266]{2,1,0:T(8,128)S(1)} %get-tuple-element.19, f32[26,74,266]{2,1,0:T(8,128)S(1)} %get-tuple-element.18, pred[26,74,266]{2,1,0:T(8,128)(4,1)S(1)} %broadcast_and_fusion), kind=kLoop, calls=%fused_computation.45 | loop fusion | flops 3678048 | bytes 12566664 | tf_op jit(solution)/shard_map/jit(_where)/select_n | solution.py:102
  140.2 6.2 %collective-permute-start.6 = (f32[2,8,32,4]{3,2,1,0:T(8,128)S(1)}, f32[2,8,32,4]{3,2,1,0:T(8,128)S(1)}, u32[]{:S(2)}, u32[]{:S(2)}) collective-permute-start(f32[2,8,32,4]{3,2,1,0:T(8,128)S(1)} %get-tuple-element.35), channel_id=1, source_target_pairs={{0,1},{2,3},{4,5},{6,7},{8,9},{10,11},{12,13},{14,15},{16,17},{18,... | collective-permute-start | bytes 24584 | tf_op jit(solution)/shard_map/ppermute | solution.py:74
  149.8 5.6 %collective-permute-done.7 = f32[2,8,32,4]{3,2,1,0:T(8,128)S(1)} collective-permute-done((f32[2,8,32,4]{3,2,1,0:T(8,128)S(1)}, f32[2,8,32,4]{3,2,1,0:T(8,128)S(1)}, u32[]{:S(2)}, u32[]{:S(2)}) %collective-permute-start.7) | collective-permute-done | bytes 8224 | tf_op jit(solution)/shard_map/ppermute | solution.py:76
  155.6 8.5 %collective-permute-start.8 = (f32[2,8,4,136]{3,2,1,0:T(4,128)S(1)}, f32[2,8,4,136]{3,2,1,0:T(4,128)S(1)}, u32[]{:S(2)}, u32[]{:S(2)}) collective-permute-start(f32[2,8,4,136]{3,2,1,0:T(4,128)S(1)} %get-tuple-element.29), channel_id=1, source_target_pairs={{0,2},{2,4},{4,6},{6,8},{8,10},{10,12},{12,14},{14,16},{16,18},{18... | collective-permute-start | bytes 104456 | tf_op jit(solution)/shard_map/ppermute | solution.py:74
  166.1 3.6 %collective-permute-done.9 = f32[2,8,4,136]{3,2,1,0:T(4,128)S(1)} collective-permute-done((f32[2,8,4,136]{3,2,1,0:T(4,128)S(1)}, f32[2,8,4,136]{3,2,1,0:T(4,128)S(1)}, u32[]{:S(2)}, u32[]{:S(2)}) %collective-permute-start.9) | collective-permute-done | bytes 34848 | tf_op jit(solution)/shard_map/ppermute | solution.py:76
  173.9 3.9 %collective-permute-done.10 = f32[2,4,40,136]{3,2,1,0:T(8,128)S(1)} collective-permute-done((f32[2,4,40,136]{3,2,1,0:T(8,128)S(1)}, f32[2,4,40,136]{3,2,1,0:T(8,128)S(1)}, u32[]{:S(2)}, u32[]{:S(2)}) %collective-permute-start.10) | collective-permute-done | bytes 174112 | tf_op jit(solution)/shard_map/ppermute | solution.py:74
  177.8 4.1 %collective-permute-done.11 = f32[2,4,40,136]{3,2,1,0:T(8,128)S(1)} collective-permute-done((f32[2,4,40,136]{3,2,1,0:T(8,128)S(1)}, f32[2,4,40,136]{3,2,1,0:T(8,128)S(1)}, u32[]{:S(2)}, u32[]{:S(2)}) %collective-permute-start.11) | collective-permute-done | bytes 174112 | tf_op jit(solution)/shard_map/ppermute | solution.py:76
  191.6 5.6 %collective-permute-done.13 = f32[2,4,16,4]{3,2,1,0:T(8,128)S(1)} collective-permute-done((f32[2,4,16,4]{3,2,1,0:T(8,128)S(1)}, f32[2,4,16,4]{3,2,1,0:T(8,128)S(1)}, u32[]{:S(2)}, u32[]{:S(2)}) %collective-permute-start.13) | collective-permute-done | bytes 2080 | tf_op jit(solution)/shard_map/ppermute | solution.py:76
  210.9 3.7 %collective-permute-done.17 = f32[2,4,24,72]{3,2,1,0:T(8,128)S(1)} collective-permute-done((f32[2,4,24,72]{3,2,1,0:T(8,128)S(1)}, f32[2,4,24,72]{3,2,1,0:T(8,128)S(1)}, u32[]{:S(2)}, u32[]{:S(2)}) %collective-permute-start.17) | collective-permute-done | bytes 55328 | tf_op jit(solution)/shard_map/ppermute | solution.py:76
  217.2 5.5 %psum.35 = f32[1024]{0:T(1024)S(1)} all-reduce(f32[1024]{0:T(1024)S(1)} %reshape.365), channel_id=1, replica_groups=mesh['gx'=4,'gy'=16,'gz'=2] {'gz'}, use_global_device_ids=true, to_apply=%region_0.1 | all-reduce | flops 1024 | bytes 8192 | tf_op jit(solution)/shard_map/psum | solution.py:141
  222.7 6.1 %psum.36 = f32[1024]{0:T(1024)S(1)} all-reduce(f32[1024]{0:T(1024)S(1)} %psum.35), channel_id=1, replica_groups=mesh['gx'=4,'gy'=16,'gz'=2] {'gx'}, use_global_device_ids=true, to_apply=%region_1.2 | all-reduce | flops 1024 | bytes 8192 | tf_op jit(solution)/shard_map/psum | solution.py:142
  228.8 4.1 %psum.37 = f32[1024]{0:T(1024)S(1)} all-reduce(f32[1024]{0:T(1024)S(1)} %psum.36), channel_id=1, replica_groups={{0,2},{4,6},{8,10},{12,14},{16,18},{20,22},{24,26},{28,30},{1,3},{5,7},..., use_global_device_ids=true, to_apply=%region_2.3 | all-reduce | flops 1024 | bytes 8192 | tf_op jit(solution)/shard_map/psum | solution.py:150
  233.0 7.4 %psum.38 = f32[1024]{0:T(1024)S(1)} all-reduce(f32[1024]{0:T(1024)S(1)} %psum.37), channel_id=1, replica_groups={{0,4},{2,6},{8,12},{10,14},{16,20},{18,22},{24,28},{26,30},{1,5},{3,7},..., use_global_device_ids=true, to_apply=%region_3.4 | all-reduce | flops 1024 | bytes 8192 | tf_op jit(solution)/shard_map/psum | solution.py:150
  240.4 9.3 %psum.39 = f32[1024]{0:T(1024)S(1)} all-reduce(f32[1024]{0:T(1024)S(1)} %psum.38), channel_id=1, replica_groups={{0,8,16,24},{2,10,18,26},{4,12,20,28},{6,14,22,30},{1,9,17,25},{3,11,19..., use_global_device_ids=true, to_apply=%region_4.5 | all-reduce | flops 1024 | bytes 8192 | tf_op jit(solution)/shard_map/psum | solution.py:150
  (139 shorter events, 84.4 us)
Async XLA Ops:
  0.6 249.0 %copy-start = (f32[64,1024]{1,0:T(8,128)S(1)}, f32[64,1024]{1,0:T(8,128)}, u32[]{:S(2)}) copy-start(f32[64,1024]{1,0:T(8,128)} %param.9) | copy-start | bytes 786436
  4.7 12.6 %copy-start.1 = (f32[16,64,256]{2,1,0:T(8,128)S(1)}, f32[16,64,256]{2,1,0:T(8,128)}, u32[]{:S(2)}) copy-start(f32[16,64,256]{2,1,0:T(8,128)} %param.7) | copy-start | bytes 3145732
  6.7 15.6 %collective-permute-start = (f32[3,16,64,5]{2,1,3,0:T(8,128)S(1)}, f32[3,16,64,5]{2,1,3,0:T(8,128)}, u32[]{:S(2)}, u32[]{:S(2)}) collective-permute-start(f32[3,16,64,5]{2,1,3,0:T(8,128)S(1)} %copy.45), channel_id=1, source_target_pairs={{0,1},{2,3},{4,5},{6,7},{8,9},{10,11},{12,13},{14,15},{16,17},{18,... | collective-permute-start | bytes 184328 | tf_op jit(solution)/shard_map/ppermute | solution.py:74
  14.2 10.8 %collective-permute-start.1 = (f32[3,16,64,5]{2,1,3,0:T(8,128)}, f32[3,16,64,5]{2,1,3,0:T(8,128)}, u32[]{:S(2)}, u32[]{:S(2)}) collective-permute-start(f32[3,16,64,5]{2,1,3,0:T(8,128)} %copy.46), channel_id=1, source_target_pairs={{1,0},{3,2},{5,4},{7,6},{9,8},{11,10},{13,12},{15,14},{17,16},{19,... | collective-permute-start | bytes 184328 | tf_op jit(solution)/shard_map/ppermute | solution.py:76
  15.5 12.1 %copy-start.19 = (pred[512]{0:T(512)(128)(4,1)}, pred[512]{0:T(512)(128)(4,1)S(1)}, u32[]{:S(2)}) copy-start(pred[512]{0:T(512)(128)(4,1)S(1)} %fusion.110) | copy-start | bytes 1540
  18.2 9.4 %copy-start.2 = (f32[16,64,256]{2,1,0:T(8,128)S(1)}, f32[16,64,256]{2,1,0:T(8,128)}, u32[]{:S(2)}) copy-start(f32[16,64,256]{2,1,0:T(8,128)} %param.5) | copy-start | bytes 3145732
  18.2 9.4 %copy-start.4 = (f32[16,64,256]{2,1,0:T(8,128)S(1)}, f32[16,64,256]{2,1,0:T(8,128)}, u32[]{:S(2)}) copy-start(f32[16,64,256]{2,1,0:T(8,128)} %param.6) | copy-start | bytes 3145732
  30.1 8.5 %collective-permute-start.2 = (f32[3,16,5,266]{3,1,2,0:T(8,128)}, f32[3,16,5,266]{3,1,2,0:T(8,128)}, u32[]{:S(2)}, u32[]{:S(2)}) collective-permute-start(f32[3,16,5,266]{3,1,2,0:T(8,128)} %copy.49), channel_id=1, source_target_pairs={{0,2},{2,4},{4,6},{6,8},{8,10},{10,12},{12,14},{14,16},{16,18},{18... | collective-permute-start | bytes 766088 | tf_op jit(solution)/shard_map/ppermute | solution.py:74
  34.0 9.1 %collective-permute-start.3 = (f32[3,16,5,266]{3,1,2,0:T(8,128)}, f32[3,16,5,266]{3,1,2,0:T(8,128)}, u32[]{:S(2)}, u32[]{:S(2)}) collective-permute-start(f32[3,16,5,266]{3,1,2,0:T(8,128)} %copy.50), channel_id=1, source_target_pairs={{2,0},{4,2},{6,4},{8,6},{10,8},{12,10},{14,12},{16,14},{18,16},{20... | collective-permute-start | bytes 766088 | tf_op jit(solution)/shard_map/ppermute | solution.py:76
  48.8 40.5 %collective-permute-start.4 = (f32[3,5,74,266]{3,2,1,0:T(8,128)}, f32[3,5,74,266]{3,2,1,0:T(8,128)}, u32[]{:S(2)}, u32[]{:S(2)}) collective-permute-start(f32[3,5,74,266]{3,2,1,0:T(8,128)} %get-tuple-element.21), channel_id=1, source_target_pairs={{0,32},{32,64},{64,96},{1,33},{33,65},{65,97},{2,34},{34,66},{66,9... | collective-permute-start | bytes 3543128 | tf_op jit(solution)/shard_map/ppermute | solution.py:74
  53.7 41.1 %collective-permute-start.5 = (f32[3,5,74,266]{3,2,1,0:T(8,128)}, f32[3,5,74,266]{3,2,1,0:T(8,128)}, u32[]{:S(2)}, u32[]{:S(2)}) collective-permute-start(f32[3,5,74,266]{3,2,1,0:T(8,128)} %get-tuple-element.22), channel_id=1, source_target_pairs={{32,0},{64,32},{96,64},{33,1},{65,33},{97,65},{34,2},{66,34},{98,6... | collective-permute-start | bytes 3543128 | tf_op jit(solution)/shard_map/ppermute | solution.py:76
  138.9 27.1 %copy-start.10 = (s32[4,16,64]{2,1,0:T(8,128)S(1)}, s32[4,16,64]{2,1,0:T(8,128)}, u32[]{:S(2)}) copy-start(s32[4,16,64]{2,1,0:T(8,128)} %param.8) | copy-start | bytes 49156
  140.2 9.7 %collective-permute-start.6 = (f32[2,8,32,4]{3,2,1,0:T(8,128)S(1)}, f32[2,8,32,4]{3,2,1,0:T(8,128)S(1)}, u32[]{:S(2)}, u32[]{:S(2)}) collective-permute-start(f32[2,8,32,4]{3,2,1,0:T(8,128)S(1)} %get-tuple-element.35), channel_id=1, source_target_pairs={{0,1},{2,3},{4,5},{6,7},{8,9},{10,11},{12,13},{14,15},{16,17},{18,... | collective-permute-start | bytes 24584 | tf_op jit(solution)/shard_map/ppermute | solution.py:74
  146.4 9.0 %collective-permute-start.7 = (f32[2,8,32,4]{3,2,1,0:T(8,128)S(1)}, f32[2,8,32,4]{3,2,1,0:T(8,128)S(1)}, u32[]{:S(2)}, u32[]{:S(2)}) collective-permute-start(f32[2,8,32,4]{3,2,1,0:T(8,128)S(1)} %get-tuple-element.36), channel_id=1, source_target_pairs={{1,0},{3,2},{5,4},{7,6},{9,8},{11,10},{13,12},{15,14},{17,16},{19,... | collective-permute-start | bytes 24584 | tf_op jit(solution)/shard_map/ppermute | solution.py:76
  155.6 10.5 %collective-permute-start.8 = (f32[2,8,4,136]{3,2,1,0:T(4,128)S(1)}, f32[2,8,4,136]{3,2,1,0:T(4,128)S(1)}, u32[]{:S(2)}, u32[]{:S(2)}) collective-permute-start(f32[2,8,4,136]{3,2,1,0:T(4,128)S(1)} %get-tuple-element.29), channel_id=1, source_target_pairs={{0,2},{2,4},{4,6},{6,8},{8,10},{10,12},{12,14},{14,16},{16,18},{18... | collective-permute-start | bytes 104456 | tf_op jit(solution)/shard_map/ppermute | solution.py:74
  164.1 5.6 %collective-permute-start.9 = (f32[2,8,4,136]{3,2,1,0:T(4,128)S(1)}, f32[2,8,4,136]{3,2,1,0:T(4,128)S(1)}, u32[]{:S(2)}, u32[]{:S(2)}) collective-permute-start(f32[2,8,4,136]{3,2,1,0:T(4,128)S(1)} %get-tuple-element.30), channel_id=1, source_target_pairs={{2,0},{4,2},{6,4},{8,6},{10,8},{12,10},{14,12},{16,14},{18,16},{20... | collective-permute-start | bytes 104456 | tf_op jit(solution)/shard_map/ppermute | solution.py:76
  170.0 7.8 %collective-permute-start.10 = (f32[2,4,40,136]{3,2,1,0:T(8,128)S(1)}, f32[2,4,40,136]{3,2,1,0:T(8,128)S(1)}, u32[]{:S(2)}, u32[]{:S(2)}) collective-permute-start(f32[2,4,40,136]{3,2,1,0:T(8,128)S(1)} %get-tuple-element.31), channel_id=1, source_target_pairs={{0,32},{32,64},{64,96},{1,33},{33,65},{65,97},{2,34},{34,66},{66,9... | collective-permute-start | bytes 522248 | tf_op jit(solution)/shard_map/ppermute | solution.py:74
  172.3 9.6 %collective-permute-start.11 = (f32[2,4,40,136]{3,2,1,0:T(8,128)S(1)}, f32[2,4,40,136]{3,2,1,0:T(8,128)S(1)}, u32[]{:S(2)}, u32[]{:S(2)}) collective-permute-start(f32[2,4,40,136]{3,2,1,0:T(8,128)S(1)} %get-tuple-element.32), channel_id=1, source_target_pairs={{32,0},{64,32},{96,64},{33,1},{65,33},{97,65},{34,2},{66,34},{98,6... | collective-permute-start | bytes 522248 | tf_op jit(solution)/shard_map/ppermute | solution.py:76
  188.5 3.2 %collective-permute-start.12 = (f32[2,4,16,4]{3,2,1,0:T(8,128)S(1)}, f32[2,4,16,4]{3,2,1,0:T(8,128)S(1)}, u32[]{:S(2)}, u32[]{:S(2)}) collective-permute-start(f32[2,4,16,4]{3,2,1,0:T(8,128)S(1)} %get-tuple-element.39), channel_id=1, source_target_pairs={{0,1},{2,3},{4,5},{6,7},{8,9},{10,11},{12,13},{14,15},{16,17},{18,... | collective-permute-start | bytes 6152 | tf_op jit(solution)/shard_map/ppermute | solution.py:74
  190.2 7.0 %collective-permute-start.13 = (f32[2,4,16,4]{3,2,1,0:T(8,128)S(1)}, f32[2,4,16,4]{3,2,1,0:T(8,128)S(1)}, u32[]{:S(2)}, u32[]{:S(2)}) collective-permute-start(f32[2,4,16,4]{3,2,1,0:T(8,128)S(1)} %get-tuple-element.40), channel_id=1, source_target_pairs={{1,0},{3,2},{5,4},{7,6},{9,8},{11,10},{13,12},{15,14},{17,16},{19,... | collective-permute-start | bytes 6152 | tf_op jit(solution)/shard_map/ppermute | solution.py:76
  197.3 5.5 %collective-permute-start.14 = (f32[2,4,4,72]{3,2,1,0:T(4,128)S(1)}, f32[2,4,4,72]{3,2,1,0:T(4,128)S(1)}, u32[]{:S(2)}, u32[]{:S(2)}) collective-permute-start(f32[2,4,4,72]{3,2,1,0:T(4,128)S(1)} %get-tuple-element.37), channel_id=1, source_target_pairs={{0,2},{2,4},{4,6},{6,8},{8,10},{10,12},{12,14},{14,16},{16,18},{18... | collective-permute-start | bytes 27656 | tf_op jit(solution)/shard_map/ppermute | solution.py:74
  200.9 5.1 %collective-permute-start.15 = (f32[2,4,4,72]{3,2,1,0:T(4,128)S(1)}, f32[2,4,4,72]{3,2,1,0:T(4,128)S(1)}, u32[]{:S(2)}, u32[]{:S(2)}) collective-permute-start(f32[2,4,4,72]{3,2,1,0:T(4,128)S(1)} %get-tuple-element.38), channel_id=1, source_target_pairs={{2,0},{4,2},{6,4},{8,6},{10,8},{12,10},{14,12},{16,14},{18,16},{20... | collective-permute-start | bytes 27656 | tf_op jit(solution)/shard_map/ppermute | solution.py:76
  206.1 4.9 %collective-permute-start.16 = (f32[2,4,24,72]{3,2,1,0:T(8,128)S(1)}, f32[2,4,24,72]{3,2,1,0:T(8,128)S(1)}, u32[]{:S(2)}, u32[]{:S(2)}) collective-permute-start(f32[2,4,24,72]{3,2,1,0:T(8,128)S(1)} %pad_maximum_fusion.18), channel_id=1, source_target_pairs={{0,32},{32,64},{64,96},{1,33},{33,65},{65,97},{2,34},{34,66},{66,9... | collective-permute-start | bytes 165896 | tf_op jit(solution)/shard_map/ppermute | solution.py:74
  209.3 5.4 %collective-permute-start.17 = (f32[2,4,24,72]{3,2,1,0:T(8,128)S(1)}, f32[2,4,24,72]{3,2,1,0:T(8,128)S(1)}, u32[]{:S(2)}, u32[]{:S(2)}) collective-permute-start(f32[2,4,24,72]{3,2,1,0:T(8,128)S(1)} %pad_maximum_fusion.18), channel_id=1, source_target_pairs={{32,0},{64,32},{96,64},{33,1},{65,33},{97,65},{34,2},{66,34},{98,6... | collective-permute-start | bytes 165896 | tf_op jit(solution)/shard_map/ppermute | solution.py:76
  (15 other events, 46.4 us)
where the time goes:
time: 254 us; the launch traced here: 250 us
  waiting for transfers between devices  69.4 us (27%)
  other arithmetic  69.1 us (27%)
  starting transfers between devices  53.7 us (21%)
  blocking collectives  32.4 us (13%)
  local copies, waits for them, and re-layouts  15.2 us (6%)
  matrix products  9.39 us (4%)
    ppermute x9, starting transfers between devices, exchange(): lax.ppermute(tail, axis, [(i, i + 1) for i in range(count - 1)])  39.8 us
    ppermute x9, waiting for transfers between devices, exchange(): lax.ppermute(tail, axis, [(i, i + 1) for i in range(count - 1)])  34.8 us
    ppermute x9, waiting for transfers between devices, exchange(): lax.ppermute(head, axis, [(i + 1, i) for i in range(count - 1)])  34.6 us
    select_n x10, other arithmetic, smooth_wide(): current = jnp.where(crop(mask, step), current, 0.0)  29.9 us
    psum x3, blocking collectives, shards(): summed = lax.psum(summed, 'gy', axis_index_groups=groups)  20.8 us
    ppermute x9, starting transfers between devices, exchange(): lax.ppermute(head, axis, [(i + 1, i) for i in range(count - 1)])  13.9 us
    concatenate x5, other arithmetic, exchange(): jnp.concatenate([lax.ppermute(tail, axis, [(i, i + 1) for i in range(coun...  12.4 us
    slice x4, other arithmetic, exchange(): lax.slice_in_dim(stack, stack.shape[dim] - width, stack.shape[dim], axis=...  6.5 us
  transfers between devices with their start and end apart: 18, of which 12 were waited for; matrix products, arithmetic and copies ran while one was open for 8% of the time, Pallas kernels for 0%

commit v1 on v0

--- a/solution.py
+++ b/solution.py
@@ -65,7 +65,7 @@
 
 
 def exchange(stack, width):
-    for axis, dim in (("gz", 3), ("gy", 2), ("gx", 1)):
+    for axis, dim in (("gx", 1), ("gy", 2), ("gz", 3)):
         count = lax.axis_size(axis)
         head = lax.slice_in_dim(stack, 0, width, axis=dim)
         tail = lax.slice_in_dim(stack, stack.shape[dim] - width, stack.shape[dim], axis=dim)

time: 254 us -> 240 us (0.945)
  waiting for transfers between devices: 69.4 us -> 49.7 us
  local copies, waits for them, and re-layouts: 15.2 us -> 26.1 us
  starting transfers between devices: 53.7 us -> 49.5 us
    ppermute x9, waiting for transfers between devices: 34.8 us -> 14.2 us  [exchange(): lax.ppermute(tail, axis, [(i, i + 1) for i in range(count - 1)])]
    concatenate x5 -> x6, other arithmetic: 12.4 us -> 18.8 us  [exchange(): jnp.concatenate([lax.ppermute(tail, axis, [(i, i + 1) for i in range(coun...]
    ppermute x9, starting transfers between devices: 39.8 us -> 35.6 us  [exchange(): lax.ppermute(tail, axis, [(i, i + 1) for i in range(count - 1)])]
    slice x4 -> x6, local copies, waits for them, and re-layouts: 4.66 us -> 8.85 us  [exchange(): lax.slice_in_dim(stack, stack.shape[dim] - width, stack.shape[dim], axis=...]
    slice x2 -> x3, local copies, waits for them, and re-layouts: 1.98 us -> 4.78 us  [exchange(): head = lax.slice_in_dim(stack, 0, width, axis=dim)]
  transfers between devices with their start and end apart: 18 -> 18, of which waited for: 12 -> 12; matrix products, arithmetic and copies ran while one was open for 8% -> 10% of each run, Pallas kernels for 0% -> 0%
where the time goes in v1:
time: 240 us; the launch traced here: 237 us
  other arithmetic  69.4 us (29%)
  waiting for transfers between devices  49.7 us (21%)
  starting transfers between devices  49.5 us (21%)
  blocking collectives  31.6 us (13%)
  local copies, waits for them, and re-layouts  26.1 us (11%)
  matrix products  8.97 us (4%)
    ppermute x9, starting transfers between devices, exchange(): lax.ppermute(tail, axis, [(i, i + 1) for i in range(count - 1)])  35.6 us
    ppermute x9, waiting for transfers between devices, exchange(): lax.ppermute(head, axis, [(i + 1, i) for i in range(count - 1)])  35.5 us
    select_n x10, other arithmetic, smooth_wide(): current = jnp.where(crop(mask, step), current, 0.0)  29.9 us
    psum x3, blocking collectives, shards(): summed = lax.psum(summed, 'gy', axis_index_groups=groups)  20.3 us
    concatenate x6, other arithmetic, exchange(): jnp.concatenate([lax.ppermute(tail, axis, [(i, i + 1) for i in range(coun...  18.8 us
    ppermute x9, waiting for transfers between devices, exchange(): lax.ppermute(tail, axis, [(i, i + 1) for i in range(count - 1)])  14.2 us
    ppermute x9, starting transfers between devices, exchange(): lax.ppermute(head, axis, [(i + 1, i) for i in range(count - 1)])  13.9 us
    slice x6, local copies, waits for them, and re-layouts, exchange(): lax.slice_in_dim(stack, stack.shape[dim] - width, stack.shape[dim], axis=...  8.85 us
  transfers between devices with their start and end apart: 18, of which 12 were waited for; matrix products, arithmetic and copies ran while one was open for 10% of the time, Pallas kernels for 0%

profile of v1, /device:TPU:1, one launch (start us, length us, event | category | flops | bytes accessed | tf_op | source)
XLA Modules:
  0.0 236.8 jit_solution(16208574465040992324)
XLA Ops:
  3.7 5.5 %collective-permute-start = (f32[3,5,64,256]{3,2,1,0:T(8,128)}, f32[3,5,64,256]{3,2,1,0:T(8,128)}, u32[]{:S(2)}, u32[]{:S(2)}) collective-permute-start(f32[3,5,64,256]{3,2,1,0:T(8,128)} %get-tuple-element.25), channel_id=1, source_target_pairs={{0,32},{32,64},{64,96},{1,33},{33,65},{65,97},{2,34},{34,66},{66,9... | collective-permute-start | bytes 2949128 | tf_op jit(solution)/shard_map/ppermute | solution.py:74
  19.5 9.5 %collective-permute-done = f32[3,5,64,256]{3,2,1,0:T(8,128)} collective-permute-done((f32[3,5,64,256]{3,2,1,0:T(8,128)}, f32[3,5,64,256]{3,2,1,0:T(8,128)}, u32[]{:S(2)}, u32[]{:S(2)}) %collective-permute-start) | collective-permute-done | bytes 983072 | tf_op jit(solution)/shard_map/ppermute | solution.py:74
  29.0 4.8 %collective-permute-done.1 = f32[3,5,64,256]{3,2,1,0:T(8,128)} collective-permute-done((f32[3,5,64,256]{3,2,1,0:T(8,128)}, f32[3,5,64,256]{3,2,1,0:T(8,128)}, u32[]{:S(2)}, u32[]{:S(2)}) %collective-permute-start.1) | collective-permute-done | bytes 983072 | tf_op jit(solution)/shard_map/ppermute | solution.py:76
  36.0 4.9 %collective-permute-start.2 = (f32[3,26,5,256]{3,1,2,0:T(8,128)}, f32[3,26,5,256]{3,1,2,0:T(8,128)}, u32[]{:S(2)}, u32[]{:S(2)}) collective-permute-start(f32[3,26,5,256]{3,1,2,0:T(8,128)} %copy.63), channel_id=1, source_target_pairs={{0,2},{2,4},{4,6},{6,8},{8,10},{10,12},{12,14},{14,16},{16,18},{18... | collective-permute-start | bytes 1198088 | tf_op jit(solution)/shard_map/ppermute | solution.py:74
  48.5 3.8 %collective-permute-done.3 = f32[3,26,5,256]{3,1,2,0:T(8,128)} collective-permute-done((f32[3,26,5,256]{3,1,2,0:T(8,128)}, f32[3,26,5,256]{3,1,2,0:T(8,128)}, u32[]{:S(2)}, u32[]{:S(2)}) %collective-permute-start.3) | collective-permute-done | bytes 399392 | tf_op jit(solution)/shard_map/ppermute | solution.py:76
  64.0 5.2 %collective-permute-start.4 = (f32[3,26,74,5]{2,1,3,0:T(8,128)}, f32[3,26,74,5]{2,1,3,0:T(8,128)}, u32[]{:S(2)}, u32[]{:S(2)}) collective-permute-start(f32[3,26,74,5]{2,1,3,0:T(8,128)} %copy.67), channel_id=1, source_target_pairs={{0,1},{2,3},{4,5},{6,7},{8,9},{10,11},{12,13},{14,15},{16,17},{18,... | collective-permute-start | bytes 346328 | tf_op jit(solution)/shard_map/ppermute | solution.py:74
  84.9 15.3 %pad_maximum_fusion = f32[3,26,74,266]{3,2,1,0:T(8,128)} fusion(f32[3,26,74,5]{3,2,1,0:T(8,128)} %copy.70, f32[3,26,5,256]{3,2,1,0:T(8,128)} %copy-done.6, f32[3,5,64,256]{3,2,1,0:T(8,128)} %collective-permute-done.1, f32[1,16,64,256]{3,2,1,0:T(8,128)S(1)} %bitcast.58, f32[1,16,64,256]{3,2,1,0:T(8,128)S(1)} %bitcast.62, f32[1,16,64,256]{3,2,1,0:T(8,128)S(1)} %bitcast.66, ...), kind=kLoop, calls=%fused_computation | loop fusion | flops 12282816 | bytes 12282816 | tf_op jit(solution)/shard_map/concatenate | solution.py:72
  100.2 4.5 %fusion = (f32[26,74,266]{2,1,0:T(8,128)S(1)}, f32[26,74,266]{2,1,0:T(8,128)S(1)}, f32[26,74,266]{2,1,0:T(8,128)S(1)}) fusion(f32[3,26,74,266]{3,2,1,0:T(8,128)} %pad_maximum_fusion), kind=kLoop, calls=%fused_computation.3 | loop fusion | flops 511784 | bytes 12282816 | tf_op jit(solution)/shard_map/add | solution.py:121
  104.7 7.2 %fusion.6 = f32[24,72,264]{2,1,0:T(8,128)S(1)} fusion(f32[26,74,266]{2,1,0:T(8,128)S(1)} %get-tuple-element.20, f32[26,74,266]{2,1,0:T(8,128)S(1)} %get-tuple-element.19, f32[26,74,266]{2,1,0:T(8,128)S(1)} %get-tuple-element.18, pred[26,74,266]{2,1,0:T(8,128)(4,1)S(1)} %copy-done.4), kind=kLoop, calls=%fused_computation.12 | loop fusion | flops 5474304 | bytes 18703872 | tf_op jit(solution)/shard_map/jit(_where)/select_n | solution.py:102
  111.9 6.8 %fusion.12 = f32[22,70,262]{2,1,0:T(8,128)S(1)} fusion(f32[24,72,264]{2,1,0:T(8,128)S(1)} %fusion.6, f32[26,74,266]{2,1,0:T(8,128)S(1)} %get-tuple-element.19, f32[26,74,266]{2,1,0:T(8,128)S(1)} %get-tuple-element.18, pred[26,74,266]{2,1,0:T(8,128)(4,1)S(1)} %copy-done.4), kind=kLoop, calls=%fused_computation.23 | loop fusion | flops 4841760 | bytes 16542680 | tf_op jit(solution)/shard_map/jit(_where)/select_n | solution.py:102
  118.7 6.0 %fusion.18 = f32[20,68,260]{2,1,0:T(8,128)S(1)} fusion(f32[22,70,262]{2,1,0:T(8,128)S(1)} %fusion.12, f32[26,74,266]{2,1,0:T(8,128)S(1)} %get-tuple-element.19, f32[26,74,266]{2,1,0:T(8,128)S(1)} %get-tuple-element.18, pred[26,74,266]{2,1,0:T(8,128)(4,1)S(1)} %copy-done.4), kind=kLoop, calls=%fused_computation.34 | loop fusion | flops 4243200 | bytes 14497600 | tf_op jit(solution)/shard_map/jit(_where)/select_n | solution.py:102
  124.7 5.4 %fusion.24 = f32[18,66,258]{2,1,0:T(8,128)S(1)} fusion(f32[20,68,260]{2,1,0:T(8,128)S(1)} %fusion.18, f32[26,74,266]{2,1,0:T(8,128)S(1)} %get-tuple-element.19, f32[26,74,266]{2,1,0:T(8,128)S(1)} %get-tuple-element.18, pred[26,74,266]{2,1,0:T(8,128)(4,1)S(1)} %copy-done.4), kind=kLoop, calls=%fused_computation.45 | loop fusion | flops 3678048 | bytes 12566664 | tf_op jit(solution)/shard_map/jit(_where)/select_n | solution.py:102
  138.5 3.8 %collective-permute-done.7 = f32[2,4,32,128]{3,2,1,0:T(8,128)S(1)} collective-permute-done((f32[2,4,32,128]{3,2,1,0:T(8,128)S(1)}, f32[2,4,32,128]{3,2,1,0:T(8,128)S(1)}, u32[]{:S(2)}, u32[]{:S(2)}) %collective-permute-start.7) | collective-permute-done | bytes 131104 | tf_op jit(solution)/shard_map/ppermute | solution.py:76
  142.3 6.3 %collective-permute-start.8 = (f32[2,16,4,128]{3,2,1,0:T(4,128)S(1)}, f32[2,16,4,128]{3,2,1,0:T(4,128)S(1)}, u32[]{:S(2)}, u32[]{:S(2)}) collective-permute-start(f32[2,16,4,128]{3,2,1,0:T(4,128)S(1)} %get-tuple-element.31), channel_id=1, source_target_pairs={{0,2},{2,4},{4,6},{6,8},{8,10},{10,12},{12,14},{14,16},{16,18},{18... | collective-permute-start | bytes 196616 | tf_op jit(solution)/shard_map/ppermute | solution.py:74
  158.3 4.9 %collective-permute-done.11 = f32[2,16,40,4]{2,1,3,0:T(8,128)S(1)} collective-permute-done((f32[2,16,40,4]{2,1,3,0:T(8,128)S(1)}, f32[2,16,40,4]{2,1,3,0:T(8,128)S(1)}, u32[]{:S(2)}, u32[]{:S(2)}) %collective-permute-start.11) | collective-permute-done | bytes 20512 | tf_op jit(solution)/shard_map/ppermute | solution.py:76
  175.0 4.1 %collective-permute-done.13 = f32[2,4,16,64]{3,2,1,0:T(8,128)S(1)} collective-permute-done((f32[2,4,16,64]{3,2,1,0:T(8,128)S(1)}, f32[2,4,16,64]{3,2,1,0:T(8,128)S(1)}, u32[]{:S(2)}, u32[]{:S(2)}) %collective-permute-start.13) | collective-permute-done | bytes 32800 | tf_op jit(solution)/shard_map/ppermute | solution.py:76
  179.1 4.4 %collective-permute-start.14 = (f32[2,12,4,64]{3,2,1,0:T(4,128)S(1)}, f32[2,12,4,64]{3,2,1,0:T(4,128)S(1)}, u32[]{:S(2)}, u32[]{:S(2)}) collective-permute-start(f32[2,12,4,64]{3,2,1,0:T(4,128)S(1)} %get-tuple-element.39), channel_id=1, source_target_pairs={{0,2},{2,4},{4,6},{6,8},{8,10},{10,12},{12,14},{14,16},{16,18},{18... | collective-permute-start | bytes 73736 | tf_op jit(solution)/shard_map/ppermute | solution.py:74
  192.5 4.1 %collective-permute-done.16 = f32[2,12,24,4]{3,2,1,0:T(8,128)S(1)} collective-permute-done((f32[2,12,24,4]{3,2,1,0:T(8,128)S(1)}, f32[2,12,24,4]{3,2,1,0:T(8,128)S(1)}, u32[]{:S(2)}, u32[]{:S(2)}) %collective-permute-start.16) | collective-permute-done | bytes 9248 | tf_op jit(solution)/shard_map/ppermute | solution.py:74
  196.5 5.1 %collective-permute-done.17 = f32[2,12,24,4]{3,2,1,0:T(8,128)S(1)} collective-permute-done((f32[2,12,24,4]{3,2,1,0:T(8,128)S(1)}, f32[2,12,24,4]{3,2,1,0:T(8,128)S(1)}, u32[]{:S(2)}, u32[]{:S(2)}) %collective-permute-start.17) | collective-permute-done | bytes 9248 | tf_op jit(solution)/shard_map/ppermute | solution.py:76
  204.3 5.3 %psum.35 = f32[1024]{0:T(1024)S(1)} all-reduce(f32[1024]{0:T(1024)S(1)} %reshape.365), channel_id=1, replica_groups=mesh['gx'=4,'gy'=16,'gz'=2] {'gz'}, use_global_device_ids=true, to_apply=%region_0.1 | all-reduce | flops 1024 | bytes 8192 | tf_op jit(solution)/shard_map/psum | solution.py:141
  209.6 6.0 %psum.36 = f32[1024]{0:T(1024)S(1)} all-reduce(f32[1024]{0:T(1024)S(1)} %psum.35), channel_id=1, replica_groups=mesh['gx'=4,'gy'=16,'gz'=2] {'gx'}, use_global_device_ids=true, to_apply=%region_1.2 | all-reduce | flops 1024 | bytes 8192 | tf_op jit(solution)/shard_map/psum | solution.py:142
  215.6 4.3 %psum.37 = f32[1024]{0:T(1024)S(1)} all-reduce(f32[1024]{0:T(1024)S(1)} %psum.36), channel_id=1, replica_groups={{0,2},{4,6},{8,10},{12,14},{16,18},{20,22},{24,26},{28,30},{1,3},{5,7},..., use_global_device_ids=true, to_apply=%region_2.3 | all-reduce | flops 1024 | bytes 8192 | tf_op jit(solution)/shard_map/psum | solution.py:150
  220.0 3.9 %psum.38 = f32[1024]{0:T(1024)S(1)} all-reduce(f32[1024]{0:T(1024)S(1)} %psum.37), channel_id=1, replica_groups={{0,4},{2,6},{8,12},{10,14},{16,20},{18,22},{24,28},{26,30},{1,5},{3,7},..., use_global_device_ids=true, to_apply=%region_3.4 | all-reduce | flops 1024 | bytes 8192 | tf_op jit(solution)/shard_map/psum | solution.py:150
  223.9 12.1 %psum.39 = f32[1024]{0:T(1024)S(1)} all-reduce(f32[1024]{0:T(1024)S(1)} %psum.38), channel_id=1, replica_groups={{0,8,16,24},{2,10,18,26},{4,12,20,28},{6,14,22,30},{1,9,17,25},{3,11,19..., use_global_device_ids=true, to_apply=%region_4.5 | all-reduce | flops 1024 | bytes 8192 | tf_op jit(solution)/shard_map/psum | solution.py:150
  (168 shorter events, 92.2 us)
Async XLA Ops:
  0.6 235.3 %copy-start = (f32[64,1024]{1,0:T(8,128)S(1)}, f32[64,1024]{1,0:T(8,128)}, u32[]{:S(2)}) copy-start(f32[64,1024]{1,0:T(8,128)} %param.9) | copy-start | bytes 786436
  3.7 30.1 %copy-start.2 = (f32[16,64,256]{2,1,0:T(8,128)S(1)}, f32[16,64,256]{2,1,0:T(8,128)}, u32[]{:S(2)}) copy-start(f32[16,64,256]{2,1,0:T(8,128)} %param.5) | copy-start | bytes 3145732
  3.7 30.1 %copy-start.3 = (f32[16,64,256]{2,1,0:T(8,128)S(1)}, f32[16,64,256]{2,1,0:T(8,128)}, u32[]{:S(2)}) copy-start(f32[16,64,256]{2,1,0:T(8,128)} %param.6) | copy-start | bytes 3145732
  3.7 25.2 %collective-permute-start = (f32[3,5,64,256]{3,2,1,0:T(8,128)}, f32[3,5,64,256]{3,2,1,0:T(8,128)}, u32[]{:S(2)}, u32[]{:S(2)}) collective-permute-start(f32[3,5,64,256]{3,2,1,0:T(8,128)} %get-tuple-element.25), channel_id=1, source_target_pairs={{0,32},{32,64},{64,96},{1,33},{33,65},{65,97},{2,34},{34,66},{66,9... | collective-permute-start | bytes 2949128 | tf_op jit(solution)/shard_map/ppermute | solution.py:74
  9.2 24.6 %collective-permute-start.1 = (f32[3,5,64,256]{3,2,1,0:T(8,128)}, f32[3,5,64,256]{3,2,1,0:T(8,128)}, u32[]{:S(2)}, u32[]{:S(2)}) collective-permute-start(f32[3,5,64,256]{3,2,1,0:T(8,128)} %get-tuple-element.26), channel_id=1, source_target_pairs={{32,0},{64,32},{96,64},{33,1},{65,33},{97,65},{34,2},{66,34},{98,6... | collective-permute-start | bytes 2949128 | tf_op jit(solution)/shard_map/ppermute | solution.py:76
  10.6 24.4 %copy-start.17 = (s32[256]{0:T(256)}, s32[256]{0:T(256)S(1)}, u32[]{:S(2)}) copy-start(s32[256]{0:T(256)S(1)} %get-tuple-element.49) | copy-start | bytes 3076
  10.6 24.4 %copy-start.19 = (s32[256]{0:T(256)}, s32[256]{0:T(256)S(1)}, u32[]{:S(2)}) copy-start(s32[256]{0:T(256)S(1)} %get-tuple-element.50) | copy-start | bytes 3076
  19.5 24.2 %copy-start.32 = (pred[26]{0:T(512)(128)(4,1)S(1)}, pred[26]{0:T(512)(128)(4,1)}, u32[]{:S(2)}) copy-start(pred[26]{0:T(512)(128)(4,1)} %compare_and_fusion.9) | copy-start | bytes 82
  36.0 11.2 %collective-permute-start.2 = (f32[3,26,5,256]{3,1,2,0:T(8,128)}, f32[3,26,5,256]{3,1,2,0:T(8,128)}, u32[]{:S(2)}, u32[]{:S(2)}) collective-permute-start(f32[3,26,5,256]{3,1,2,0:T(8,128)} %copy.63), channel_id=1, source_target_pairs={{0,2},{2,4},{4,6},{6,8},{8,10},{10,12},{12,14},{14,16},{16,18},{18... | collective-permute-start | bytes 1198088 | tf_op jit(solution)/shard_map/ppermute | solution.py:74
  41.8 10.5 %collective-permute-start.3 = (f32[3,26,5,256]{3,1,2,0:T(8,128)}, f32[3,26,5,256]{3,1,2,0:T(8,128)}, u32[]{:S(2)}, u32[]{:S(2)}) collective-permute-start(f32[3,26,5,256]{3,1,2,0:T(8,128)} %copy.64), channel_id=1, source_target_pairs={{2,0},{4,2},{6,4},{8,6},{10,8},{12,10},{14,12},{16,14},{18,16},{20... | collective-permute-start | bytes 1198088 | tf_op jit(solution)/shard_map/ppermute | solution.py:76
  64.0 11.9 %collective-permute-start.4 = (f32[3,26,74,5]{2,1,3,0:T(8,128)}, f32[3,26,74,5]{2,1,3,0:T(8,128)}, u32[]{:S(2)}, u32[]{:S(2)}) collective-permute-start(f32[3,26,74,5]{2,1,3,0:T(8,128)} %copy.67), channel_id=1, source_target_pairs={{0,1},{2,3},{4,5},{6,7},{8,9},{10,11},{12,13},{14,15},{16,17},{18,... | collective-permute-start | bytes 346328 | tf_op jit(solution)/shard_map/ppermute | solution.py:74
  72.8 8.8 %collective-permute-start.5 = (f32[3,26,74,5]{2,1,3,0:T(8,128)}, f32[3,26,74,5]{2,1,3,0:T(8,128)}, u32[]{:S(2)}, u32[]{:S(2)}) collective-permute-start(f32[3,26,74,5]{2,1,3,0:T(8,128)} %copy.68), channel_id=1, source_target_pairs={{1,0},{3,2},{5,4},{7,6},{9,8},{11,10},{13,12},{15,14},{17,16},{19,... | collective-permute-start | bytes 346328 | tf_op jit(solution)/shard_map/ppermute | solution.py:76
  134.0 4.5 %collective-permute-start.6 = (f32[2,4,32,128]{3,2,1,0:T(8,128)S(1)}, f32[2,4,32,128]{3,2,1,0:T(8,128)S(1)}, u32[]{:S(2)}, u32[]{:S(2)}) collective-permute-start(f32[2,4,32,128]{3,2,1,0:T(8,128)S(1)} %get-tuple-element.37), channel_id=1, source_target_pairs={{0,32},{32,64},{64,96},{1,33},{33,65},{65,97},{2,34},{34,66},{66,9... | collective-permute-start | bytes 393224 | tf_op jit(solution)/shard_map/ppermute | solution.py:74
  136.6 5.7 %collective-permute-start.7 = (f32[2,4,32,128]{3,2,1,0:T(8,128)S(1)}, f32[2,4,32,128]{3,2,1,0:T(8,128)S(1)}, u32[]{:S(2)}, u32[]{:S(2)}) collective-permute-start(f32[2,4,32,128]{3,2,1,0:T(8,128)S(1)} %get-tuple-element.38), channel_id=1, source_target_pairs={{32,0},{64,32},{96,64},{33,1},{65,33},{97,65},{34,2},{66,34},{98,6... | collective-permute-start | bytes 393224 | tf_op jit(solution)/shard_map/ppermute | solution.py:76
  142.3 8.5 %collective-permute-start.8 = (f32[2,16,4,128]{3,2,1,0:T(4,128)S(1)}, f32[2,16,4,128]{3,2,1,0:T(4,128)S(1)}, u32[]{:S(2)}, u32[]{:S(2)}) collective-permute-start(f32[2,16,4,128]{3,2,1,0:T(4,128)S(1)} %get-tuple-element.31), channel_id=1, source_target_pairs={{0,2},{2,4},{4,6},{6,8},{8,10},{10,12},{12,14},{14,16},{16,18},{18... | collective-permute-start | bytes 196616 | tf_op jit(solution)/shard_map/ppermute | solution.py:74
  148.6 5.6 %collective-permute-start.9 = (f32[2,16,4,128]{3,2,1,0:T(4,128)S(1)}, f32[2,16,4,128]{3,2,1,0:T(4,128)S(1)}, u32[]{:S(2)}, u32[]{:S(2)}) collective-permute-start(f32[2,16,4,128]{3,2,1,0:T(4,128)S(1)} %get-tuple-element.32), channel_id=1, source_target_pairs={{2,0},{4,2},{6,4},{8,6},{10,8},{12,10},{14,12},{16,14},{18,16},{20... | collective-permute-start | bytes 196616 | tf_op jit(solution)/shard_map/ppermute | solution.py:76
  154.8 3.2 %collective-permute-start.10 = (f32[2,16,40,4]{2,1,3,0:T(8,128)S(1)}, f32[2,16,40,4]{2,1,3,0:T(8,128)S(1)}, u32[]{:S(2)}, u32[]{:S(2)}) collective-permute-start(f32[2,16,40,4]{2,1,3,0:T(8,128)S(1)} %copy.71), channel_id=1, source_target_pairs={{0,1},{2,3},{4,5},{6,7},{8,9},{10,11},{12,13},{14,15},{16,17},{18,... | collective-permute-start | bytes 61448 | tf_op jit(solution)/shard_map/ppermute | solution.py:74
  156.7 6.5 %collective-permute-start.11 = (f32[2,16,40,4]{2,1,3,0:T(8,128)S(1)}, f32[2,16,40,4]{2,1,3,0:T(8,128)S(1)}, u32[]{:S(2)}, u32[]{:S(2)}) collective-permute-start(f32[2,16,40,4]{2,1,3,0:T(8,128)S(1)} %copy.72), channel_id=1, source_target_pairs={{1,0},{3,2},{5,4},{7,6},{9,8},{11,10},{13,12},{15,14},{17,16},{19,... | collective-permute-start | bytes 61448 | tf_op jit(solution)/shard_map/ppermute | solution.py:76
  170.3 4.6 %collective-permute-start.12 = (f32[2,4,16,64]{3,2,1,0:T(8,128)S(1)}, f32[2,4,16,64]{3,2,1,0:T(8,128)S(1)}, u32[]{:S(2)}, u32[]{:S(2)}) collective-permute-start(f32[2,4,16,64]{3,2,1,0:T(8,128)S(1)} %pad_maximum_fusion.19), channel_id=1, source_target_pairs={{0,32},{32,64},{64,96},{1,33},{33,65},{65,97},{2,34},{34,66},{66,9... | collective-permute-start | bytes 98312 | tf_op jit(solution)/shard_map/ppermute | solution.py:74
  173.6 5.5 %collective-permute-start.13 = (f32[2,4,16,64]{3,2,1,0:T(8,128)S(1)}, f32[2,4,16,64]{3,2,1,0:T(8,128)S(1)}, u32[]{:S(2)}, u32[]{:S(2)}) collective-permute-start(f32[2,4,16,64]{3,2,1,0:T(8,128)S(1)} %pad_maximum_fusion.19), channel_id=1, source_target_pairs={{32,0},{64,32},{96,64},{33,1},{65,33},{97,65},{34,2},{66,34},{98,6... | collective-permute-start | bytes 98312 | tf_op jit(solution)/shard_map/ppermute | solution.py:76
  179.1 6.3 %collective-permute-start.14 = (f32[2,12,4,64]{3,2,1,0:T(4,128)S(1)}, f32[2,12,4,64]{3,2,1,0:T(4,128)S(1)}, u32[]{:S(2)}, u32[]{:S(2)}) collective-permute-start(f32[2,12,4,64]{3,2,1,0:T(4,128)S(1)} %get-tuple-element.39), channel_id=1, source_target_pairs={{0,2},{2,4},{4,6},{6,8},{8,10},{10,12},{12,14},{14,16},{16,18},{18... | collective-permute-start | bytes 73736 | tf_op jit(solution)/shard_map/ppermute | solution.py:74
  183.5 5.4 %collective-permute-start.15 = (f32[2,12,4,64]{3,2,1,0:T(4,128)S(1)}, f32[2,12,4,64]{3,2,1,0:T(4,128)S(1)}, u32[]{:S(2)}, u32[]{:S(2)}) collective-permute-start(f32[2,12,4,64]{3,2,1,0:T(4,128)S(1)} %get-tuple-element.40), channel_id=1, source_target_pairs={{2,0},{4,2},{6,4},{8,6},{10,8},{12,10},{14,12},{16,14},{18,16},{20... | collective-permute-start | bytes 73736 | tf_op jit(solution)/shard_map/ppermute | solution.py:76
  189.1 7.4 %collective-permute-start.16 = (f32[2,12,24,4]{3,2,1,0:T(8,128)S(1)}, f32[2,12,24,4]{3,2,1,0:T(8,128)S(1)}, u32[]{:S(2)}, u32[]{:S(2)}) collective-permute-start(f32[2,12,24,4]{3,2,1,0:T(8,128)S(1)} %get-tuple-element.35), channel_id=1, source_target_pairs={{0,1},{2,3},{4,5},{6,7},{8,9},{10,11},{12,13},{14,15},{16,17},{18,... | collective-permute-start | bytes 27656 | tf_op jit(solution)/shard_map/ppermute | solution.py:74
  191.0 10.6 %collective-permute-start.17 = (f32[2,12,24,4]{3,2,1,0:T(8,128)S(1)}, f32[2,12,24,4]{3,2,1,0:T(8,128)S(1)}, u32[]{:S(2)}, u32[]{:S(2)}) collective-permute-start(f32[2,12,24,4]{3,2,1,0:T(8,128)S(1)} %get-tuple-element.36), channel_id=1, source_target_pairs={{1,0},{3,2},{5,4},{7,6},{9,8},{11,10},{13,12},{15,14},{17,16},{19,... | collective-permute-start | bytes 27656 | tf_op jit(solution)/shard_map/ppermute | solution.py:76
  (27 other events, 179.3 us)

commit v2 on v1

--- a/solution.py
+++ b/solution.py
@@ -65,7 +65,7 @@
 
 
 def exchange(stack, width):
-    for axis, dim in (("gx", 1), ("gy", 2), ("gz", 3)):
+    for axis, dim in (("gz", 3), ("gx", 1), ("gy", 2)):
         count = lax.axis_size(axis)
         head = lax.slice_in_dim(stack, 0, width, axis=dim)
         tail = lax.slice_in_dim(stack, stack.shape[dim] - width, stack.shape[dim], axis=dim)

time: 240 us -> 245 us (1.021)
  waiting for transfers between devices: 49.7 us -> 72.4 us
  local copies, waits for them, and re-layouts: 26.1 us -> 16.8 us
  blocking collectives: 31.6 us -> 25.8 us
  other arithmetic: 69.4 us -> 64.3 us
  starting transfers between devices: 49.5 us -> 53.8 us
    ppermute x9, waiting for transfers between devices: 14.2 us -> 43.9 us  [exchange(): lax.ppermute(tail, axis, [(i, i + 1) for i in range(count - 1)])]
    ppermute x9, waiting for transfers between devices: 35.5 us -> 28.5 us  [exchange(): lax.ppermute(head, axis, [(i + 1, i) for i in range(count - 1)])]
    concatenate x6 -> x5, other arithmetic: 18.8 us -> 11.9 us  [exchange(): jnp.concatenate([lax.ppermute(tail, axis, [(i, i + 1) for i in range(coun...]
    psum x3, blocking collectives: 20.3 us -> 14.3 us  [shards(): summed = lax.psum(summed, 'gy', axis_index_groups=groups)]
    ppermute x9, starting transfers between devices: 35.6 us -> 39.9 us  [exchange(): lax.ppermute(tail, axis, [(i, i + 1) for i in range(count - 1)])]
    slice x6 -> x4, local copies, waits for them, and re-layouts: 8.85 us -> 4.83 us  [exchange(): lax.slice_in_dim(stack, stack.shape[dim] - width, stack.shape[dim], axis=...]
    slice x3 -> x2, local copies, waits for them, and re-layouts: 4.78 us -> 2.16 us  [exchange(): head = lax.slice_in_dim(stack, 0, width, axis=dim)]
    ppermute x3 -> x2, local copies, waits for them, and re-layouts: 4.96 us -> 4.07 us  [exchange(): lax.ppermute(head, axis, [(i + 1, i) for i in range(count - 1)])]
  transfers between devices with their start and end apart: 18 -> 18, of which waited for: 12 -> 12; matrix products, arithmetic and copies ran while one was open for 10% -> 7% of each run, Pallas kernels for 0% -> 0%
where the time goes in v2:
time: 245 us; the launch traced here: 242 us
  waiting for transfers between devices  72.4 us (30%)
  other arithmetic  64.3 us (26%)
  starting transfers between devices  53.8 us (22%)
  blocking collectives  25.8 us (11%)
  local copies, waits for them, and re-layouts  16.8 us (7%)
  matrix products  6.93 us (3%)
    ppermute x9, waiting for transfers between devices, exchange(): lax.ppermute(tail, axis, [(i, i + 1) for i in range(count - 1)])  43.9 us
    ppermute x9, starting transfers between devices, exchange(): lax.ppermute(tail, axis, [(i, i + 1) for i in range(count - 1)])  39.9 us
    select_n x10, other arithmetic, smooth_wide(): current = jnp.where(crop(mask, step), current, 0.0)  29.9 us
    ppermute x9, waiting for transfers between devices, exchange(): lax.ppermute(head, axis, [(i + 1, i) for i in range(count - 1)])  28.5 us
    psum x3, blocking collectives, shards(): summed = lax.psum(summed, 'gy', axis_index_groups=groups)  14.3 us
    ppermute x9, starting transfers between devices, exchange(): lax.ppermute(head, axis, [(i + 1, i) for i in range(count - 1)])  13.9 us
    concatenate x5, other arithmetic, exchange(): jnp.concatenate([lax.ppermute(tail, axis, [(i, i + 1) for i in range(coun...  11.9 us
    psum x1, blocking collectives, shards(): summed = lax.psum(summed, 'gx')  6.2 us
  transfers between devices with their start and end apart: 18, of which 12 were waited for; matrix products, arithmetic and copies ran while one was open for 7% of the time, Pallas kernels for 0%

profile of v2, /device:TPU:1, one launch (start us, length us, event | category | flops | bytes accessed | tf_op | source)
XLA Modules:
  0.0 241.6 jit_solution(5976206577523022680)
XLA Ops:
  6.7 6.3 %collective-permute-start = (f32[3,16,64,5]{2,1,3,0:T(8,128)S(1)}, f32[3,16,64,5]{2,1,3,0:T(8,128)}, u32[]{:S(2)}, u32[]{:S(2)}) collective-permute-start(f32[3,16,64,5]{2,1,3,0:T(8,128)S(1)} %copy.45), channel_id=1, source_target_pairs={{0,1},{2,3},{4,5},{6,7},{8,9},{10,11},{12,13},{14,15},{16,17},{18,... | collective-permute-start | bytes 184328 | tf_op jit(solution)/shard_map/ppermute | solution.py:74
  31.3 3.6 %collective-permute-start.2 = (f32[3,5,64,266]{3,2,1,0:T(8,128)S(1)}, f32[3,5,64,266]{3,2,1,0:T(8,128)S(1)}, u32[]{:S(2)}, u32[]{:S(2)}) collective-permute-start(f32[3,5,64,266]{3,2,1,0:T(8,128)S(1)} %get-tuple-element.23), channel_id=1, source_target_pairs={{0,32},{32,64},{64,96},{1,33},{33,65},{65,97},{2,34},{34,66},{66,9... | collective-permute-start | bytes 3064328 | tf_op jit(solution)/shard_map/ppermute | solution.py:74
  39.0 26.5 %collective-permute-done.2 = f32[3,5,64,266]{3,2,1,0:T(8,128)S(1)} collective-permute-done((f32[3,5,64,266]{3,2,1,0:T(8,128)S(1)}, f32[3,5,64,266]{3,2,1,0:T(8,128)S(1)}, u32[]{:S(2)}, u32[]{:S(2)}) %collective-permute-start.2) | collective-permute-done | bytes 1021472 | tf_op jit(solution)/shard_map/ppermute | solution.py:74
  65.5 4.1 %collective-permute-done.3 = f32[3,5,64,266]{3,2,1,0:T(8,128)S(1)} collective-permute-done((f32[3,5,64,266]{3,2,1,0:T(8,128)S(1)}, f32[3,5,64,266]{3,2,1,0:T(8,128)S(1)}, u32[]{:S(2)}, u32[]{:S(2)}) %collective-permute-start.3) | collective-permute-done | bytes 1021472 | tf_op jit(solution)/shard_map/ppermute | solution.py:76
  71.7 4.2 %collective-permute-start.4 = (f32[3,26,5,266]{3,1,2,0:T(8,128)}, f32[3,26,5,266]{3,1,2,0:T(8,128)}, u32[]{:S(2)}, u32[]{:S(2)}) collective-permute-start(f32[3,26,5,266]{3,1,2,0:T(8,128)} %copy.49), channel_id=1, source_target_pairs={{0,2},{2,4},{4,6},{6,8},{8,10},{10,12},{12,14},{14,16},{16,18},{18... | collective-permute-start | bytes 1244888 | tf_op jit(solution)/shard_map/ppermute | solution.py:74
  79.7 12.8 %collective-permute-done.4 = f32[3,26,5,266]{3,1,2,0:T(8,128)} collective-permute-done((f32[3,26,5,266]{3,1,2,0:T(8,128)}, f32[3,26,5,266]{3,1,2,0:T(8,128)}, u32[]{:S(2)}, u32[]{:S(2)}) %collective-permute-start.4) | collective-permute-done | bytes 414992 | tf_op jit(solution)/shard_map/ppermute | solution.py:74
  95.5 11.1 %pad_maximum_fusion = f32[3,26,74,266]{3,2,1,0:T(8,128)} fusion(f32[3,26,5,266]{3,2,1,0:T(8,128)S(1)} %copy.52, f32[3,5,64,266]{3,2,1,0:T(8,128)} %copy-done.9, f32[3,16,64,5]{3,2,1,0:T(8,128)S(1)} %copy-done.6, f32[1,16,64,256]{3,2,1,0:T(8,128)S(1)} %bitcast.58, f32[1,16,64,256]{3,2,1,0:T(8,128)S(1)} %bitcast.62, f32[1,16,64,256]{3,2,1,0:T(8,128)S(1)} %bitcast.66, ...), kind=kLoop, calls=%fused_computation | loop fusion | flops 12282816 | bytes 12282816 | tf_op jit(solution)/shard_map/concatenate | solution.py:72
  106.6 4.5 %fusion = (f32[26,74,266]{2,1,0:T(8,128)S(1)}, f32[26,74,266]{2,1,0:T(8,128)S(1)}, f32[26,74,266]{2,1,0:T(8,128)S(1)}) fusion(f32[3,26,74,266]{3,2,1,0:T(8,128)} %pad_maximum_fusion), kind=kLoop, calls=%fused_computation.2 | loop fusion | flops 511784 | bytes 12282816 | tf_op jit(solution)/shard_map/add | solution.py:121
  111.1 7.2 %fusion.6 = f32[24,72,264]{2,1,0:T(8,128)S(1)} fusion(f32[26,74,266]{2,1,0:T(8,128)S(1)} %get-tuple-element.20, f32[26,74,266]{2,1,0:T(8,128)S(1)} %get-tuple-element.19, f32[26,74,266]{2,1,0:T(8,128)S(1)} %get-tuple-element.18, pred[26,74,266]{2,1,0:T(8,128)(4,1)S(1)} %broadcast_and_fusion), kind=kLoop, calls=%fused_computation.12 | loop fusion | flops 5474304 | bytes 18703872 | tf_op jit(solution)/shard_map/jit(_where)/select_n | solution.py:102
  118.3 6.5 %fusion.12 = f32[22,70,262]{2,1,0:T(8,128)S(1)} fusion(f32[24,72,264]{2,1,0:T(8,128)S(1)} %fusion.6, f32[26,74,266]{2,1,0:T(8,128)S(1)} %get-tuple-element.19, f32[26,74,266]{2,1,0:T(8,128)S(1)} %get-tuple-element.18, pred[26,74,266]{2,1,0:T(8,128)(4,1)S(1)} %broadcast_and_fusion), kind=kLoop, calls=%fused_computation.23 | loop fusion | flops 4841760 | bytes 16542680 | tf_op jit(solution)/shard_map/jit(_where)/select_n | solution.py:102
  124.9 6.2 %fusion.18 = f32[20,68,260]{2,1,0:T(8,128)S(1)} fusion(f32[22,70,262]{2,1,0:T(8,128)S(1)} %fusion.12, f32[26,74,266]{2,1,0:T(8,128)S(1)} %get-tuple-element.19, f32[26,74,266]{2,1,0:T(8,128)S(1)} %get-tuple-element.18, pred[26,74,266]{2,1,0:T(8,128)(4,1)S(1)} %broadcast_and_fusion), kind=kLoop, calls=%fused_computation.34 | loop fusion | flops 4243200 | bytes 14497600 | tf_op jit(solution)/shard_map/jit(_where)/select_n | solution.py:102
  131.1 5.4 %fusion.24 = f32[18,66,258]{2,1,0:T(8,128)S(1)} fusion(f32[20,68,260]{2,1,0:T(8,128)S(1)} %fusion.18, f32[26,74,266]{2,1,0:T(8,128)S(1)} %get-tuple-element.19, f32[26,74,266]{2,1,0:T(8,128)S(1)} %get-tuple-element.18, pred[26,74,266]{2,1,0:T(8,128)(4,1)S(1)} %broadcast_and_fusion), kind=kLoop, calls=%fused_computation.45 | loop fusion | flops 3678048 | bytes 12566664 | tf_op jit(solution)/shard_map/jit(_where)/select_n | solution.py:102
  140.4 6.7 %collective-permute-start.6 = (f32[2,8,32,4]{3,2,1,0:T(8,128)S(1)}, f32[2,8,32,4]{3,2,1,0:T(8,128)S(1)}, u32[]{:S(2)}, u32[]{:S(2)}) collective-permute-start(f32[2,8,32,4]{3,2,1,0:T(8,128)S(1)} %get-tuple-element.37), channel_id=1, source_target_pairs={{0,1},{2,3},{4,5},{6,7},{8,9},{10,11},{12,13},{14,15},{16,17},{18,... | collective-permute-start | bytes 24584 | tf_op jit(solution)/shard_map/ppermute | solution.py:74
  150.4 5.3 %collective-permute-done.7 = f32[2,8,32,4]{3,2,1,0:T(8,128)S(1)} collective-permute-done((f32[2,8,32,4]{3,2,1,0:T(8,128)S(1)}, f32[2,8,32,4]{3,2,1,0:T(8,128)S(1)}, u32[]{:S(2)}, u32[]{:S(2)}) %collective-permute-start.7) | collective-permute-done | bytes 8224 | tf_op jit(solution)/shard_map/ppermute | solution.py:76
  156.1 3.4 %collective-permute-start.8 = (f32[2,4,32,136]{3,2,1,0:T(8,128)S(1)}, f32[2,4,32,136]{3,2,1,0:T(8,128)S(1)}, u32[]{:S(2)}, u32[]{:S(2)}) collective-permute-start(f32[2,4,32,136]{3,2,1,0:T(8,128)S(1)} %get-tuple-element.31), channel_id=1, source_target_pairs={{0,32},{32,64},{64,96},{1,33},{33,65},{65,97},{2,34},{34,66},{66,9... | collective-permute-start | bytes 417800 | tf_op jit(solution)/shard_map/ppermute | solution.py:74
  162.7 3.8 %collective-permute-done.9 = f32[2,4,32,136]{3,2,1,0:T(8,128)S(1)} collective-permute-done((f32[2,4,32,136]{3,2,1,0:T(8,128)S(1)}, f32[2,4,32,136]{3,2,1,0:T(8,128)S(1)}, u32[]{:S(2)}, u32[]{:S(2)}) %collective-permute-start.9) | collective-permute-done | bytes 139296 | tf_op jit(solution)/shard_map/ppermute | solution.py:76
  166.7 6.6 %collective-permute-start.10 = (f32[2,16,4,136]{3,2,1,0:T(4,128)S(1)}, f32[2,16,4,136]{3,2,1,0:T(4,128)S(1)}, u32[]{:S(2)}, u32[]{:S(2)}) collective-permute-start(f32[2,16,4,136]{3,2,1,0:T(4,128)S(1)} %get-tuple-element.29), channel_id=1, source_target_pairs={{0,2},{2,4},{4,6},{6,8},{8,10},{10,12},{12,14},{14,16},{16,18},{18... | collective-permute-start | bytes 208904 | tf_op jit(solution)/shard_map/ppermute | solution.py:74
  189.3 5.1 %collective-permute-done.13 = f32[2,4,16,4]{3,2,1,0:T(8,128)S(1)} collective-permute-done((f32[2,4,16,4]{3,2,1,0:T(8,128)S(1)}, f32[2,4,16,4]{3,2,1,0:T(8,128)S(1)}, u32[]{:S(2)}, u32[]{:S(2)}) %collective-permute-start.13) | collective-permute-done | bytes 2080 | tf_op jit(solution)/shard_map/ppermute | solution.py:76
  199.1 3.7 %collective-permute-done.15 = f32[2,4,16,72]{3,2,1,0:T(8,128)S(1)} collective-permute-done((f32[2,4,16,72]{3,2,1,0:T(8,128)S(1)}, f32[2,4,16,72]{3,2,1,0:T(8,128)S(1)}, u32[]{:S(2)}, u32[]{:S(2)}) %collective-permute-start.15) | collective-permute-done | bytes 36896 | tf_op jit(solution)/shard_map/ppermute | solution.py:76
  202.9 4.0 %collective-permute-start.16 = (f32[2,12,4,72]{3,2,1,0:T(4,128)S(1)}, f32[2,12,4,72]{3,2,1,0:T(4,128)S(1)}, u32[]{:S(2)}, u32[]{:S(2)}) collective-permute-start(f32[2,12,4,72]{3,2,1,0:T(4,128)S(1)} %get-tuple-element.33), channel_id=1, source_target_pairs={{0,2},{2,4},{4,6},{6,8},{8,10},{10,12},{12,14},{14,16},{16,18},{18... | collective-permute-start | bytes 82952 | tf_op jit(solution)/shard_map/ppermute | solution.py:74
  214.9 5.3 %psum.35 = f32[1024]{0:T(1024)S(1)} all-reduce(f32[1024]{0:T(1024)S(1)} %reshape.365), channel_id=1, replica_groups=mesh['gx'=4,'gy'=16,'gz'=2] {'gz'}, use_global_device_ids=true, to_apply=%region_0.1 | all-reduce | flops 1024 | bytes 8192 | tf_op jit(solution)/shard_map/psum | solution.py:141
  220.2 6.2 %psum.36 = f32[1024]{0:T(1024)S(1)} all-reduce(f32[1024]{0:T(1024)S(1)} %psum.35), channel_id=1, replica_groups=mesh['gx'=4,'gy'=16,'gz'=2] {'gx'}, use_global_device_ids=true, to_apply=%region_1.2 | all-reduce | flops 1024 | bytes 8192 | tf_op jit(solution)/shard_map/psum | solution.py:142
  228.9 4.7 %psum.38 = f32[1024]{0:T(1024)S(1)} all-reduce(f32[1024]{0:T(1024)S(1)} %psum.37), channel_id=1, replica_groups={{0,4},{2,6},{8,12},{10,14},{16,20},{18,22},{24,28},{26,30},{1,5},{3,7},..., use_global_device_ids=true, to_apply=%region_3.4 | all-reduce | flops 1024 | bytes 8192 | tf_op jit(solution)/shard_map/psum | solution.py:150
  233.5 7.2 %psum.39 = f32[1024]{0:T(1024)S(1)} all-reduce(f32[1024]{0:T(1024)S(1)} %psum.38), channel_id=1, replica_groups={{0,8,16,24},{2,10,18,26},{4,12,20,28},{6,14,22,30},{1,9,17,25},{3,11,19..., use_global_device_ids=true, to_apply=%region_4.5 | all-reduce | flops 1024 | bytes 8192 | tf_op jit(solution)/shard_map/psum | solution.py:150
  (163 shorter events, 79.5 us)
Async XLA Ops:
  0.6 240.1 %copy-start = (f32[64,1024]{1,0:T(8,128)S(1)}, f32[64,1024]{1,0:T(8,128)}, u32[]{:S(2)}) copy-start(f32[64,1024]{1,0:T(8,128)} %param.9) | copy-start | bytes 786436
  6.7 16.5 %collective-permute-start = (f32[3,16,64,5]{2,1,3,0:T(8,128)S(1)}, f32[3,16,64,5]{2,1,3,0:T(8,128)}, u32[]{:S(2)}, u32[]{:S(2)}) collective-permute-start(f32[3,16,64,5]{2,1,3,0:T(8,128)S(1)} %copy.45), channel_id=1, source_target_pairs={{0,1},{2,3},{4,5},{6,7},{8,9},{10,11},{12,13},{14,15},{16,17},{18,... | collective-permute-start | bytes 184328 | tf_op jit(solution)/shard_map/ppermute | solution.py:74
  14.2 11.7 %collective-permute-start.1 = (f32[3,16,64,5]{2,1,3,0:T(8,128)}, f32[3,16,64,5]{2,1,3,0:T(8,128)}, u32[]{:S(2)}, u32[]{:S(2)}) collective-permute-start(f32[3,16,64,5]{2,1,3,0:T(8,128)} %copy.46), channel_id=1, source_target_pairs={{1,0},{3,2},{5,4},{7,6},{9,8},{11,10},{13,12},{15,14},{17,16},{19,... | collective-permute-start | bytes 184328 | tf_op jit(solution)/shard_map/ppermute | solution.py:76
  16.0 20.2 %copy-start.15 = (s32[256]{0:T(256)}, s32[256]{0:T(256)S(1)}, u32[]{:S(2)}) copy-start(s32[256]{0:T(256)S(1)} %get-tuple-element.49) | copy-start | bytes 3076
  28.5 41.1 %copy-start.3 = (f32[3,16,64,5]{3,2,1,0:T(8,128)S(1)}, f32[3,16,64,5]{3,2,1,0:T(8,128)}, u32[]{:S(2)}) copy-start(f32[3,16,64,5]{3,2,1,0:T(8,128)} %copy.47) | copy-start | bytes 184324
  28.6 41.1 %copy-start.5 = (f32[3,16,64,5]{3,2,1,0:T(8,128)S(1)}, f32[3,16,64,5]{3,2,1,0:T(8,128)}, u32[]{:S(2)}) copy-start(f32[3,16,64,5]{3,2,1,0:T(8,128)} %copy.48) | copy-start | bytes 184324
  31.3 34.2 %collective-permute-start.2 = (f32[3,5,64,266]{3,2,1,0:T(8,128)S(1)}, f32[3,5,64,266]{3,2,1,0:T(8,128)S(1)}, u32[]{:S(2)}, u32[]{:S(2)}) collective-permute-start(f32[3,5,64,266]{3,2,1,0:T(8,128)S(1)} %get-tuple-element.23), channel_id=1, source_target_pairs={{0,32},{32,64},{64,96},{1,33},{33,65},{65,97},{2,34},{34,66},{66,9... | collective-permute-start | bytes 3064328 | tf_op jit(solution)/shard_map/ppermute | solution.py:74
  34.9 34.7 %collective-permute-start.3 = (f32[3,5,64,266]{3,2,1,0:T(8,128)S(1)}, f32[3,5,64,266]{3,2,1,0:T(8,128)S(1)}, u32[]{:S(2)}, u32[]{:S(2)}) collective-permute-start(f32[3,5,64,266]{3,2,1,0:T(8,128)S(1)} %get-tuple-element.24), channel_id=1, source_target_pairs={{32,0},{64,32},{96,64},{33,1},{65,33},{97,65},{34,2},{66,34},{98,6... | collective-permute-start | bytes 3064328 | tf_op jit(solution)/shard_map/ppermute | solution.py:76
  36.2 33.9 %copy-start.25 = (pred[136]{0:T(512)(128)(4,1)}, pred[136]{0:T(512)(128)(4,1)S(1)}, u32[]{:S(2)}) copy-start(pred[136]{0:T(512)(128)(4,1)S(1)} %compare_and_fusion.5) | copy-start | bytes 412
  71.7 20.8 %collective-permute-start.4 = (f32[3,26,5,266]{3,1,2,0:T(8,128)}, f32[3,26,5,266]{3,1,2,0:T(8,128)}, u32[]{:S(2)}, u32[]{:S(2)}) collective-permute-start(f32[3,26,5,266]{3,1,2,0:T(8,128)} %copy.49), channel_id=1, source_target_pairs={{0,2},{2,4},{4,6},{6,8},{8,10},{10,12},{12,14},{14,16},{16,18},{18... | collective-permute-start | bytes 1244888 | tf_op jit(solution)/shard_map/ppermute | solution.py:74
  76.9 17.1 %collective-permute-start.5 = (f32[3,26,5,266]{3,1,2,0:T(8,128)}, f32[3,26,5,266]{3,1,2,0:T(8,128)}, u32[]{:S(2)}, u32[]{:S(2)}) collective-permute-start(f32[3,26,5,266]{3,1,2,0:T(8,128)} %copy.50), channel_id=1, source_target_pairs={{2,0},{4,2},{6,4},{8,6},{10,8},{12,10},{14,12},{16,14},{18,16},{20... | collective-permute-start | bytes 1244888 | tf_op jit(solution)/shard_map/ppermute | solution.py:76
  79.1 16.4 %copy-start.6 = (f32[3,16,64,5]{3,2,1,0:T(8,128)S(1)}, f32[3,16,64,5]{3,2,1,0:T(8,128)}, u32[]{:S(2)}) copy-start(f32[3,16,64,5]{3,2,1,0:T(8,128)} %copy.48) | copy-start | bytes 184324
  140.4 10.0 %collective-permute-start.6 = (f32[2,8,32,4]{3,2,1,0:T(8,128)S(1)}, f32[2,8,32,4]{3,2,1,0:T(8,128)S(1)}, u32[]{:S(2)}, u32[]{:S(2)}) collective-permute-start(f32[2,8,32,4]{3,2,1,0:T(8,128)S(1)} %get-tuple-element.37), channel_id=1, source_target_pairs={{0,1},{2,3},{4,5},{6,7},{8,9},{10,11},{12,13},{14,15},{16,17},{18,... | collective-permute-start | bytes 24584 | tf_op jit(solution)/shard_map/ppermute | solution.py:74
  147.1 8.6 %collective-permute-start.7 = (f32[2,8,32,4]{3,2,1,0:T(8,128)S(1)}, f32[2,8,32,4]{3,2,1,0:T(8,128)S(1)}, u32[]{:S(2)}, u32[]{:S(2)}) collective-permute-start(f32[2,8,32,4]{3,2,1,0:T(8,128)S(1)} %get-tuple-element.38), channel_id=1, source_target_pairs={{1,0},{3,2},{5,4},{7,6},{9,8},{11,10},{13,12},{15,14},{17,16},{19,... | collective-permute-start | bytes 24584 | tf_op jit(solution)/shard_map/ppermute | solution.py:76
  156.1 6.7 %collective-permute-start.8 = (f32[2,4,32,136]{3,2,1,0:T(8,128)S(1)}, f32[2,4,32,136]{3,2,1,0:T(8,128)S(1)}, u32[]{:S(2)}, u32[]{:S(2)}) collective-permute-start(f32[2,4,32,136]{3,2,1,0:T(8,128)S(1)} %get-tuple-element.31), channel_id=1, source_target_pairs={{0,32},{32,64},{64,96},{1,33},{33,65},{65,97},{2,34},{34,66},{66,9... | collective-permute-start | bytes 417800 | tf_op jit(solution)/shard_map/ppermute | solution.py:74
  159.5 7.1 %collective-permute-start.9 = (f32[2,4,32,136]{3,2,1,0:T(8,128)S(1)}, f32[2,4,32,136]{3,2,1,0:T(8,128)S(1)}, u32[]{:S(2)}, u32[]{:S(2)}) collective-permute-start(f32[2,4,32,136]{3,2,1,0:T(8,128)S(1)} %get-tuple-element.32), channel_id=1, source_target_pairs={{32,0},{64,32},{96,64},{33,1},{65,33},{97,65},{34,2},{66,34},{98,6... | collective-permute-start | bytes 417800 | tf_op jit(solution)/shard_map/ppermute | solution.py:76
  166.7 9.9 %collective-permute-start.10 = (f32[2,16,4,136]{3,2,1,0:T(4,128)S(1)}, f32[2,16,4,136]{3,2,1,0:T(4,128)S(1)}, u32[]{:S(2)}, u32[]{:S(2)}) collective-permute-start(f32[2,16,4,136]{3,2,1,0:T(4,128)S(1)} %get-tuple-element.29), channel_id=1, source_target_pairs={{0,2},{2,4},{4,6},{6,8},{8,10},{10,12},{12,14},{14,16},{16,18},{18... | collective-permute-start | bytes 208904 | tf_op jit(solution)/shard_map/ppermute | solution.py:74
  173.4 6.3 %collective-permute-start.11 = (f32[2,16,4,136]{3,2,1,0:T(4,128)S(1)}, f32[2,16,4,136]{3,2,1,0:T(4,128)S(1)}, u32[]{:S(2)}, u32[]{:S(2)}) collective-permute-start(f32[2,16,4,136]{3,2,1,0:T(4,128)S(1)} %get-tuple-element.30), channel_id=1, source_target_pairs={{2,0},{4,2},{6,4},{8,6},{10,8},{12,10},{14,12},{16,14},{18,16},{20... | collective-permute-start | bytes 208904 | tf_op jit(solution)/shard_map/ppermute | solution.py:76
  186.1 3.2 %collective-permute-start.12 = (f32[2,4,16,4]{3,2,1,0:T(8,128)S(1)}, f32[2,4,16,4]{3,2,1,0:T(8,128)S(1)}, u32[]{:S(2)}, u32[]{:S(2)}) collective-permute-start(f32[2,4,16,4]{3,2,1,0:T(8,128)S(1)} %get-tuple-element.39), channel_id=1, source_target_pairs={{0,1},{2,3},{4,5},{6,7},{8,9},{10,11},{12,13},{14,15},{16,17},{18,... | collective-permute-start | bytes 6152 | tf_op jit(solution)/shard_map/ppermute | solution.py:74
  187.9 6.5 %collective-permute-start.13 = (f32[2,4,16,4]{3,2,1,0:T(8,128)S(1)}, f32[2,4,16,4]{3,2,1,0:T(8,128)S(1)}, u32[]{:S(2)}, u32[]{:S(2)}) collective-permute-start(f32[2,4,16,4]{3,2,1,0:T(8,128)S(1)} %get-tuple-element.40), channel_id=1, source_target_pairs={{1,0},{3,2},{5,4},{7,6},{9,8},{11,10},{13,12},{15,14},{17,16},{19,... | collective-permute-start | bytes 6152 | tf_op jit(solution)/shard_map/ppermute | solution.py:76
  194.5 4.6 %collective-permute-start.14 = (f32[2,4,16,72]{3,2,1,0:T(8,128)S(1)}, f32[2,4,16,72]{3,2,1,0:T(8,128)S(1)}, u32[]{:S(2)}, u32[]{:S(2)}) collective-permute-start(f32[2,4,16,72]{3,2,1,0:T(8,128)S(1)} %pad_maximum_fusion.25), channel_id=1, source_target_pairs={{0,32},{32,64},{64,96},{1,33},{33,65},{65,97},{2,34},{34,66},{66,9... | collective-permute-start | bytes 110600 | tf_op jit(solution)/shard_map/ppermute | solution.py:74
  197.8 5.0 %collective-permute-start.15 = (f32[2,4,16,72]{3,2,1,0:T(8,128)S(1)}, f32[2,4,16,72]{3,2,1,0:T(8,128)S(1)}, u32[]{:S(2)}, u32[]{:S(2)}) collective-permute-start(f32[2,4,16,72]{3,2,1,0:T(8,128)S(1)} %pad_maximum_fusion.25), channel_id=1, source_target_pairs={{32,0},{64,32},{96,64},{33,1},{65,33},{97,65},{34,2},{66,34},{98,6... | collective-permute-start | bytes 110600 | tf_op jit(solution)/shard_map/ppermute | solution.py:76
  202.9 6.1 %collective-permute-start.16 = (f32[2,12,4,72]{3,2,1,0:T(4,128)S(1)}, f32[2,12,4,72]{3,2,1,0:T(4,128)S(1)}, u32[]{:S(2)}, u32[]{:S(2)}) collective-permute-start(f32[2,12,4,72]{3,2,1,0:T(4,128)S(1)} %get-tuple-element.33), channel_id=1, source_target_pairs={{0,2},{2,4},{4,6},{6,8},{8,10},{10,12},{12,14},{14,16},{16,18},{18... | collective-permute-start | bytes 82952 | tf_op jit(solution)/shard_map/ppermute | solution.py:74
  206.9 5.4 %collective-permute-start.17 = (f32[2,12,4,72]{3,2,1,0:T(4,128)S(1)}, f32[2,12,4,72]{3,2,1,0:T(4,128)S(1)}, u32[]{:S(2)}, u32[]{:S(2)}) collective-permute-start(f32[2,12,4,72]{3,2,1,0:T(4,128)S(1)} %get-tuple-element.34), channel_id=1, source_target_pairs={{2,0},{4,2},{6,4},{8,6},{10,8},{12,10},{14,12},{16,14},{18,16},{20... | collective-permute-start | bytes 82952 | tf_op jit(solution)/shard_map/ppermute | solution.py:76
  (27 other events, 191.4 us)

commit v3 on v1

--- a/solution.py
+++ b/solution.py
@@ -138,9 +138,8 @@
     partial_sums = lax.dot_general(
         high, low, (((0,), (0,)), ((), ())), precision=lax.Precision.HIGHEST
     ).reshape(NAGG)
-    summed = lax.psum(partial_sums, "gz")
-    summed = lax.psum(summed, "gx")
-    splits = ((1, 2), (2, 2), (4, 4)) if lax.axis_size("gy") == 16 else ((1, lax.axis_size("gy")),)
+    summed = lax.psum(partial_sums, ("gx", "gz"))
+    splits = ((1, 4), (4, 4)) if lax.axis_size("gy") == 16 else ((1, lax.axis_size("gy")),)
     for stride, span in splits:
         groups = [
             [base + stride * k for k in range(span)]

time: 240 us -> 243 us (1.012)
  blocking collectives: 31.6 us -> 35.4 us
    psum x2 -> x1, blocking collectives: 11.3 us -> 15.6 us  [shards(): summed = lax.psum(partial_sums, ('gx', 'gz'))]
    psum x3 -> x2, blocking collectives: 20.3 us -> 19.9 us  [shards(): summed = lax.psum(summed, 'gy', axis_index_groups=groups)]
where the time goes in v3:
time: 243 us; the launch traced here: 241 us
  other arithmetic  69.4 us (29%)
  waiting for transfers between devices  49.7 us (20%)
  starting transfers between devices  49.5 us (20%)
  blocking collectives  35.4 us (15%)
  local copies, waits for them, and re-layouts  26.1 us (11%)
  matrix products  8.96 us (4%)
    ppermute x9, starting transfers between devices, exchange(): lax.ppermute(tail, axis, [(i, i + 1) for i in range(count - 1)])  35.6 us
    ppermute x9, waiting for transfers between devices, exchange(): lax.ppermute(head, axis, [(i + 1, i) for i in range(count - 1)])  35.5 us
    select_n x10, other arithmetic, smooth_wide(): current = jnp.where(crop(mask, step), current, 0.0)  29.9 us
    psum x2, blocking collectives, shards(): summed = lax.psum(summed, 'gy', axis_index_groups=groups)  19.9 us
    concatenate x6, other arithmetic, exchange(): jnp.concatenate([lax.ppermute(tail, axis, [(i, i + 1) for i in range(coun...  18.8 us
    psum x1, blocking collectives, shards(): summed = lax.psum(partial_sums, ('gx', 'gz'))  15.6 us
    ppermute x9, waiting for transfers between devices, exchange(): lax.ppermute(tail, axis, [(i, i + 1) for i in range(count - 1)])  14.2 us
    ppermute x9, starting transfers between devices, exchange(): lax.ppermute(head, axis, [(i + 1, i) for i in range(count - 1)])  13.9 us
  transfers between devices with their start and end apart: 18, of which 12 were waited for; matrix products, arithmetic and copies ran while one was open for 10% of the time, Pallas kernels for 0%

profile of v3, /device:TPU:1, one launch (start us, length us, event | category | flops | bytes accessed | tf_op | source)
XLA Modules:
  0.0 240.6 jit_solution(7282188839746293745)
XLA Ops:
  3.8 5.5 %collective-permute-start = (f32[3,5,64,256]{3,2,1,0:T(8,128)}, f32[3,5,64,256]{3,2,1,0:T(8,128)}, u32[]{:S(2)}, u32[]{:S(2)}) collective-permute-start(f32[3,5,64,256]{3,2,1,0:T(8,128)} %get-tuple-element.25), channel_id=1, source_target_pairs={{0,32},{32,64},{64,96},{1,33},{33,65},{65,97},{2,34},{34,66},{66,9... | collective-permute-start | bytes 2949128 | tf_op jit(solution)/shard_map/ppermute | solution.py:74
  19.5 9.5 %collective-permute-done = f32[3,5,64,256]{3,2,1,0:T(8,128)} collective-permute-done((f32[3,5,64,256]{3,2,1,0:T(8,128)}, f32[3,5,64,256]{3,2,1,0:T(8,128)}, u32[]{:S(2)}, u32[]{:S(2)}) %collective-permute-start) | collective-permute-done | bytes 983072 | tf_op jit(solution)/shard_map/ppermute | solution.py:74
  29.0 4.8 %collective-permute-done.1 = f32[3,5,64,256]{3,2,1,0:T(8,128)} collective-permute-done((f32[3,5,64,256]{3,2,1,0:T(8,128)}, f32[3,5,64,256]{3,2,1,0:T(8,128)}, u32[]{:S(2)}, u32[]{:S(2)}) %collective-permute-start.1) | collective-permute-done | bytes 983072 | tf_op jit(solution)/shard_map/ppermute | solution.py:76
  36.0 4.9 %collective-permute-start.2 = (f32[3,26,5,256]{3,1,2,0:T(8,128)}, f32[3,26,5,256]{3,1,2,0:T(8,128)}, u32[]{:S(2)}, u32[]{:S(2)}) collective-permute-start(f32[3,26,5,256]{3,1,2,0:T(8,128)} %copy.63), channel_id=1, source_target_pairs={{0,2},{2,4},{4,6},{6,8},{8,10},{10,12},{12,14},{14,16},{16,18},{18... | collective-permute-start | bytes 1198088 | tf_op jit(solution)/shard_map/ppermute | solution.py:74
  48.5 3.8 %collective-permute-done.3 = f32[3,26,5,256]{3,1,2,0:T(8,128)} collective-permute-done((f32[3,26,5,256]{3,1,2,0:T(8,128)}, f32[3,26,5,256]{3,1,2,0:T(8,128)}, u32[]{:S(2)}, u32[]{:S(2)}) %collective-permute-start.3) | collective-permute-done | bytes 399392 | tf_op jit(solution)/shard_map/ppermute | solution.py:76
  56.7 3.7 %fusion.113 = (f32[3,26,74,5]{3,2,1,0:T(8,128)}, f32[3,26,74,5]{3,2,1,0:T(8,128)}) fusion(f32[3,26,74,256]{3,2,1,0:T(8,128)S(1)} %pad_maximum_fusion.1), kind=kLoop, calls=%fused_computation.266 | loop fusion | bytes 461760 | tf_op jit(solution)/shard_map/slice | solution.py:71
  60.4 3.6 %copy.67 = f32[3,26,74,5]{2,1,3,0:T(8,128)} copy(f32[3,26,74,5]{3,2,1,0:T(8,128)} %get-tuple-element.21) | data formatting | bytes 230880 | tf_op jit(solution)/shard_map/slice | solution.py:71
  64.0 5.2 %collective-permute-start.4 = (f32[3,26,74,5]{2,1,3,0:T(8,128)}, f32[3,26,74,5]{2,1,3,0:T(8,128)}, u32[]{:S(2)}, u32[]{:S(2)}) collective-permute-start(f32[3,26,74,5]{2,1,3,0:T(8,128)} %copy.67), channel_id=1, source_target_pairs={{0,1},{2,3},{4,5},{6,7},{8,9},{10,11},{12,13},{14,15},{16,17},{18,... | collective-permute-start | bytes 346328 | tf_op jit(solution)/shard_map/ppermute | solution.py:74
  84.9 15.3 %pad_maximum_fusion = f32[3,26,74,266]{3,2,1,0:T(8,128)} fusion(f32[3,26,74,5]{3,2,1,0:T(8,128)} %copy.70, f32[3,26,5,256]{3,2,1,0:T(8,128)} %copy-done.6, f32[3,5,64,256]{3,2,1,0:T(8,128)} %collective-permute-done.1, f32[1,16,64,256]{3,2,1,0:T(8,128)S(1)} %bitcast.58, f32[1,16,64,256]{3,2,1,0:T(8,128)S(1)} %bitcast.62, f32[1,16,64,256]{3,2,1,0:T(8,128)S(1)} %bitcast.66, ...), kind=kLoop, calls=%fused_computation | loop fusion | flops 12282816 | bytes 12282816 | tf_op jit(solution)/shard_map/concatenate | solution.py:72
  100.2 4.5 %fusion = (f32[26,74,266]{2,1,0:T(8,128)S(1)}, f32[26,74,266]{2,1,0:T(8,128)S(1)}, f32[26,74,266]{2,1,0:T(8,128)S(1)}) fusion(f32[3,26,74,266]{3,2,1,0:T(8,128)} %pad_maximum_fusion), kind=kLoop, calls=%fused_computation.3 | loop fusion | flops 511784 | bytes 12282816 | tf_op jit(solution)/shard_map/add | solution.py:121
  104.7 7.2 %fusion.6 = f32[24,72,264]{2,1,0:T(8,128)S(1)} fusion(f32[26,74,266]{2,1,0:T(8,128)S(1)} %get-tuple-element.20, f32[26,74,266]{2,1,0:T(8,128)S(1)} %get-tuple-element.19, f32[26,74,266]{2,1,0:T(8,128)S(1)} %get-tuple-element.18, pred[26,74,266]{2,1,0:T(8,128)(4,1)S(1)} %copy-done.4), kind=kLoop, calls=%fused_computation.12 | loop fusion | flops 5474304 | bytes 18703872 | tf_op jit(solution)/shard_map/jit(_where)/select_n | solution.py:102
  111.9 6.8 %fusion.12 = f32[22,70,262]{2,1,0:T(8,128)S(1)} fusion(f32[24,72,264]{2,1,0:T(8,128)S(1)} %fusion.6, f32[26,74,266]{2,1,0:T(8,128)S(1)} %get-tuple-element.19, f32[26,74,266]{2,1,0:T(8,128)S(1)} %get-tuple-element.18, pred[26,74,266]{2,1,0:T(8,128)(4,1)S(1)} %copy-done.4), kind=kLoop, calls=%fused_computation.23 | loop fusion | flops 4841760 | bytes 16542680 | tf_op jit(solution)/shard_map/jit(_where)/select_n | solution.py:102
  118.7 6.0 %fusion.18 = f32[20,68,260]{2,1,0:T(8,128)S(1)} fusion(f32[22,70,262]{2,1,0:T(8,128)S(1)} %fusion.12, f32[26,74,266]{2,1,0:T(8,128)S(1)} %get-tuple-element.19, f32[26,74,266]{2,1,0:T(8,128)S(1)} %get-tuple-element.18, pred[26,74,266]{2,1,0:T(8,128)(4,1)S(1)} %copy-done.4), kind=kLoop, calls=%fused_computation.34 | loop fusion | flops 4243200 | bytes 14497600 | tf_op jit(solution)/shard_map/jit(_where)/select_n | solution.py:102
  124.7 5.4 %fusion.24 = f32[18,66,258]{2,1,0:T(8,128)S(1)} fusion(f32[20,68,260]{2,1,0:T(8,128)S(1)} %fusion.18, f32[26,74,266]{2,1,0:T(8,128)S(1)} %get-tuple-element.19, f32[26,74,266]{2,1,0:T(8,128)S(1)} %get-tuple-element.18, pred[26,74,266]{2,1,0:T(8,128)(4,1)S(1)} %copy-done.4), kind=kLoop, calls=%fused_computation.45 | loop fusion | flops 3678048 | bytes 12566664 | tf_op jit(solution)/shard_map/jit(_where)/select_n | solution.py:102
  138.4 3.8 %collective-permute-done.7 = f32[2,4,32,128]{3,2,1,0:T(8,128)S(1)} collective-permute-done((f32[2,4,32,128]{3,2,1,0:T(8,128)S(1)}, f32[2,4,32,128]{3,2,1,0:T(8,128)S(1)}, u32[]{:S(2)}, u32[]{:S(2)}) %collective-permute-start.7) | collective-permute-done | bytes 131104 | tf_op jit(solution)/shard_map/ppermute | solution.py:76
  142.3 6.3 %collective-permute-start.8 = (f32[2,16,4,128]{3,2,1,0:T(4,128)S(1)}, f32[2,16,4,128]{3,2,1,0:T(4,128)S(1)}, u32[]{:S(2)}, u32[]{:S(2)}) collective-permute-start(f32[2,16,4,128]{3,2,1,0:T(4,128)S(1)} %get-tuple-element.31), channel_id=1, source_target_pairs={{0,2},{2,4},{4,6},{6,8},{8,10},{10,12},{12,14},{14,16},{16,18},{18... | collective-permute-start | bytes 196616 | tf_op jit(solution)/shard_map/ppermute | solution.py:74
  158.3 4.9 %collective-permute-done.11 = f32[2,16,40,4]{2,1,3,0:T(8,128)S(1)} collective-permute-done((f32[2,16,40,4]{2,1,3,0:T(8,128)S(1)}, f32[2,16,40,4]{2,1,3,0:T(8,128)S(1)}, u32[]{:S(2)}, u32[]{:S(2)}) %collective-permute-start.11) | collective-permute-done | bytes 20512 | tf_op jit(solution)/shard_map/ppermute | solution.py:76
  175.0 4.1 %collective-permute-done.13 = f32[2,4,16,64]{3,2,1,0:T(8,128)S(1)} collective-permute-done((f32[2,4,16,64]{3,2,1,0:T(8,128)S(1)}, f32[2,4,16,64]{3,2,1,0:T(8,128)S(1)}, u32[]{:S(2)}, u32[]{:S(2)}) %collective-permute-start.13) | collective-permute-done | bytes 32800 | tf_op jit(solution)/shard_map/ppermute | solution.py:76
  179.1 4.4 %collective-permute-start.14 = (f32[2,12,4,64]{3,2,1,0:T(4,128)S(1)}, f32[2,12,4,64]{3,2,1,0:T(4,128)S(1)}, u32[]{:S(2)}, u32[]{:S(2)}) collective-permute-start(f32[2,12,4,64]{3,2,1,0:T(4,128)S(1)} %get-tuple-element.39), channel_id=1, source_target_pairs={{0,2},{2,4},{4,6},{6,8},{8,10},{10,12},{12,14},{14,16},{16,18},{18... | collective-permute-start | bytes 73736 | tf_op jit(solution)/shard_map/ppermute | solution.py:74
  192.4 4.1 %collective-permute-done.16 = f32[2,12,24,4]{3,2,1,0:T(8,128)S(1)} collective-permute-done((f32[2,12,24,4]{3,2,1,0:T(8,128)S(1)}, f32[2,12,24,4]{3,2,1,0:T(8,128)S(1)}, u32[]{:S(2)}, u32[]{:S(2)}) %collective-permute-start.16) | collective-permute-done | bytes 9248 | tf_op jit(solution)/shard_map/ppermute | solution.py:74
  196.5 5.1 %collective-permute-done.17 = f32[2,12,24,4]{3,2,1,0:T(8,128)S(1)} collective-permute-done((f32[2,12,24,4]{3,2,1,0:T(8,128)S(1)}, f32[2,12,24,4]{3,2,1,0:T(8,128)S(1)}, u32[]{:S(2)}, u32[]{:S(2)}) %collective-permute-start.17) | collective-permute-done | bytes 9248 | tf_op jit(solution)/shard_map/ppermute | solution.py:76
  204.3 15.6 %psum.21 = f32[1024]{0:T(1024)S(1)} all-reduce(f32[1024]{0:T(1024)S(1)} %reshape.365), channel_id=1, replica_groups=mesh['gx'=4,'gy'=16,'gz'=2] {'gx','gz'}, use_global_device_ids=true, to_apply=%region_0.1 | all-reduce | flops 1024 | bytes 8192 | tf_op jit(solution)/shard_map/psum | solution.py:141
  219.9 8.2 %psum.22 = f32[1024]{0:T(1024)S(1)} all-reduce(f32[1024]{0:T(1024)S(1)} %psum.21), channel_id=1, replica_groups={{0,2,4,6},{8,10,12,14},{16,18,20,22},{24,26,28,30},{1,3,5,7},{9,11,13,1..., use_global_device_ids=true, to_apply=%region_1.2 | all-reduce | flops 1024 | bytes 8192 | tf_op jit(solution)/shard_map/psum | solution.py:149
  228.1 11.7 %psum.23 = f32[1024]{0:T(1024)S(1)} all-reduce(f32[1024]{0:T(1024)S(1)} %psum.22), channel_id=1, replica_groups={{0,8,16,24},{2,10,18,26},{4,12,20,28},{6,14,22,30},{1,9,17,25},{3,11,19..., use_global_device_ids=true, to_apply=%region_2.3 | all-reduce | flops 1024 | bytes 8192 | tf_op jit(solution)/shard_map/psum | solution.py:149
  (166 shorter events, 85.0 us)
Async XLA Ops:
  0.6 239.1 %copy-start = (f32[64,1024]{1,0:T(8,128)S(1)}, f32[64,1024]{1,0:T(8,128)}, u32[]{:S(2)}) copy-start(f32[64,1024]{1,0:T(8,128)} %param.9) | copy-start | bytes 786436
  3.8 30.1 %copy-start.2 = (f32[16,64,256]{2,1,0:T(8,128)S(1)}, f32[16,64,256]{2,1,0:T(8,128)}, u32[]{:S(2)}) copy-start(f32[16,64,256]{2,1,0:T(8,128)} %param.5) | copy-start | bytes 3145732
  3.8 30.1 %copy-start.3 = (f32[16,64,256]{2,1,0:T(8,128)S(1)}, f32[16,64,256]{2,1,0:T(8,128)}, u32[]{:S(2)}) copy-start(f32[16,64,256]{2,1,0:T(8,128)} %param.6) | copy-start | bytes 3145732
  3.8 25.2 %collective-permute-start = (f32[3,5,64,256]{3,2,1,0:T(8,128)}, f32[3,5,64,256]{3,2,1,0:T(8,128)}, u32[]{:S(2)}, u32[]{:S(2)}) collective-permute-start(f32[3,5,64,256]{3,2,1,0:T(8,128)} %get-tuple-element.25), channel_id=1, source_target_pairs={{0,32},{32,64},{64,96},{1,33},{33,65},{65,97},{2,34},{34,66},{66,9... | collective-permute-start | bytes 2949128 | tf_op jit(solution)/shard_map/ppermute | solution.py:74
  9.2 24.6 %collective-permute-start.1 = (f32[3,5,64,256]{3,2,1,0:T(8,128)}, f32[3,5,64,256]{3,2,1,0:T(8,128)}, u32[]{:S(2)}, u32[]{:S(2)}) collective-permute-start(f32[3,5,64,256]{3,2,1,0:T(8,128)} %get-tuple-element.26), channel_id=1, source_target_pairs={{32,0},{64,32},{96,64},{33,1},{65,33},{97,65},{34,2},{66,34},{98,6... | collective-permute-start | bytes 2949128 | tf_op jit(solution)/shard_map/ppermute | solution.py:76
  10.6 24.4 %copy-start.17 = (s32[256]{0:T(256)}, s32[256]{0:T(256)S(1)}, u32[]{:S(2)}) copy-start(s32[256]{0:T(256)S(1)} %get-tuple-element.49) | copy-start | bytes 3076
  10.6 24.4 %copy-start.19 = (s32[256]{0:T(256)}, s32[256]{0:T(256)S(1)}, u32[]{:S(2)}) copy-start(s32[256]{0:T(256)S(1)} %get-tuple-element.50) | copy-start | bytes 3076
  19.5 24.2 %copy-start.32 = (pred[26]{0:T(512)(128)(4,1)S(1)}, pred[26]{0:T(512)(128)(4,1)}, u32[]{:S(2)}) copy-start(pred[26]{0:T(512)(128)(4,1)} %compare_and_fusion.9) | copy-start | bytes 82
  36.0 11.2 %collective-permute-start.2 = (f32[3,26,5,256]{3,1,2,0:T(8,128)}, f32[3,26,5,256]{3,1,2,0:T(8,128)}, u32[]{:S(2)}, u32[]{:S(2)}) collective-permute-start(f32[3,26,5,256]{3,1,2,0:T(8,128)} %copy.63), channel_id=1, source_target_pairs={{0,2},{2,4},{4,6},{6,8},{8,10},{10,12},{12,14},{14,16},{16,18},{18... | collective-permute-start | bytes 1198088 | tf_op jit(solution)/shard_map/ppermute | solution.py:74
  41.8 10.5 %collective-permute-start.3 = (f32[3,26,5,256]{3,1,2,0:T(8,128)}, f32[3,26,5,256]{3,1,2,0:T(8,128)}, u32[]{:S(2)}, u32[]{:S(2)}) collective-permute-start(f32[3,26,5,256]{3,1,2,0:T(8,128)} %copy.64), channel_id=1, source_target_pairs={{2,0},{4,2},{6,4},{8,6},{10,8},{12,10},{14,12},{16,14},{18,16},{20... | collective-permute-start | bytes 1198088 | tf_op jit(solution)/shard_map/ppermute | solution.py:76
  64.0 11.9 %collective-permute-start.4 = (f32[3,26,74,5]{2,1,3,0:T(8,128)}, f32[3,26,74,5]{2,1,3,0:T(8,128)}, u32[]{:S(2)}, u32[]{:S(2)}) collective-permute-start(f32[3,26,74,5]{2,1,3,0:T(8,128)} %copy.67), channel_id=1, source_target_pairs={{0,1},{2,3},{4,5},{6,7},{8,9},{10,11},{12,13},{14,15},{16,17},{18,... | collective-permute-start | bytes 346328 | tf_op jit(solution)/shard_map/ppermute | solution.py:74
  72.8 8.8 %collective-permute-start.5 = (f32[3,26,74,5]{2,1,3,0:T(8,128)}, f32[3,26,74,5]{2,1,3,0:T(8,128)}, u32[]{:S(2)}, u32[]{:S(2)}) collective-permute-start(f32[3,26,74,5]{2,1,3,0:T(8,128)} %copy.68), channel_id=1, source_target_pairs={{1,0},{3,2},{5,4},{7,6},{9,8},{11,10},{13,12},{15,14},{17,16},{19,... | collective-permute-start | bytes 346328 | tf_op jit(solution)/shard_map/ppermute | solution.py:76
  134.0 4.5 %collective-permute-start.6 = (f32[2,4,32,128]{3,2,1,0:T(8,128)S(1)}, f32[2,4,32,128]{3,2,1,0:T(8,128)S(1)}, u32[]{:S(2)}, u32[]{:S(2)}) collective-permute-start(f32[2,4,32,128]{3,2,1,0:T(8,128)S(1)} %get-tuple-element.37), channel_id=1, source_target_pairs={{0,32},{32,64},{64,96},{1,33},{33,65},{65,97},{2,34},{34,66},{66,9... | collective-permute-start | bytes 393224 | tf_op jit(solution)/shard_map/ppermute | solution.py:74
  136.5 5.7 %collective-permute-start.7 = (f32[2,4,32,128]{3,2,1,0:T(8,128)S(1)}, f32[2,4,32,128]{3,2,1,0:T(8,128)S(1)}, u32[]{:S(2)}, u32[]{:S(2)}) collective-permute-start(f32[2,4,32,128]{3,2,1,0:T(8,128)S(1)} %get-tuple-element.38), channel_id=1, source_target_pairs={{32,0},{64,32},{96,64},{33,1},{65,33},{97,65},{34,2},{66,34},{98,6... | collective-permute-start | bytes 393224 | tf_op jit(solution)/shard_map/ppermute | solution.py:76
  142.3 8.5 %collective-permute-start.8 = (f32[2,16,4,128]{3,2,1,0:T(4,128)S(1)}, f32[2,16,4,128]{3,2,1,0:T(4,128)S(1)}, u32[]{:S(2)}, u32[]{:S(2)}) collective-permute-start(f32[2,16,4,128]{3,2,1,0:T(4,128)S(1)} %get-tuple-element.31), channel_id=1, source_target_pairs={{0,2},{2,4},{4,6},{6,8},{8,10},{10,12},{12,14},{14,16},{16,18},{18... | collective-permute-start | bytes 196616 | tf_op jit(solution)/shard_map/ppermute | solution.py:74
  148.5 5.6 %collective-permute-start.9 = (f32[2,16,4,128]{3,2,1,0:T(4,128)S(1)}, f32[2,16,4,128]{3,2,1,0:T(4,128)S(1)}, u32[]{:S(2)}, u32[]{:S(2)}) collective-permute-start(f32[2,16,4,128]{3,2,1,0:T(4,128)S(1)} %get-tuple-element.32), channel_id=1, source_target_pairs={{2,0},{4,2},{6,4},{8,6},{10,8},{12,10},{14,12},{16,14},{18,16},{20... | collective-permute-start | bytes 196616 | tf_op jit(solution)/shard_map/ppermute | solution.py:76
  154.7 3.3 %collective-permute-start.10 = (f32[2,16,40,4]{2,1,3,0:T(8,128)S(1)}, f32[2,16,40,4]{2,1,3,0:T(8,128)S(1)}, u32[]{:S(2)}, u32[]{:S(2)}) collective-permute-start(f32[2,16,40,4]{2,1,3,0:T(8,128)S(1)} %copy.71), channel_id=1, source_target_pairs={{0,1},{2,3},{4,5},{6,7},{8,9},{10,11},{12,13},{14,15},{16,17},{18,... | collective-permute-start | bytes 61448 | tf_op jit(solution)/shard_map/ppermute | solution.py:74
  156.7 6.5 %collective-permute-start.11 = (f32[2,16,40,4]{2,1,3,0:T(8,128)S(1)}, f32[2,16,40,4]{2,1,3,0:T(8,128)S(1)}, u32[]{:S(2)}, u32[]{:S(2)}) collective-permute-start(f32[2,16,40,4]{2,1,3,0:T(8,128)S(1)} %copy.72), channel_id=1, source_target_pairs={{1,0},{3,2},{5,4},{7,6},{9,8},{11,10},{13,12},{15,14},{17,16},{19,... | collective-permute-start | bytes 61448 | tf_op jit(solution)/shard_map/ppermute | solution.py:76
  170.3 4.6 %collective-permute-start.12 = (f32[2,4,16,64]{3,2,1,0:T(8,128)S(1)}, f32[2,4,16,64]{3,2,1,0:T(8,128)S(1)}, u32[]{:S(2)}, u32[]{:S(2)}) collective-permute-start(f32[2,4,16,64]{3,2,1,0:T(8,128)S(1)} %pad_maximum_fusion.19), channel_id=1, source_target_pairs={{0,32},{32,64},{64,96},{1,33},{33,65},{65,97},{2,34},{34,66},{66,9... | collective-permute-start | bytes 98312 | tf_op jit(solution)/shard_map/ppermute | solution.py:74
  173.6 5.5 %collective-permute-start.13 = (f32[2,4,16,64]{3,2,1,0:T(8,128)S(1)}, f32[2,4,16,64]{3,2,1,0:T(8,128)S(1)}, u32[]{:S(2)}, u32[]{:S(2)}) collective-permute-start(f32[2,4,16,64]{3,2,1,0:T(8,128)S(1)} %pad_maximum_fusion.19), channel_id=1, source_target_pairs={{32,0},{64,32},{96,64},{33,1},{65,33},{97,65},{34,2},{66,34},{98,6... | collective-permute-start | bytes 98312 | tf_op jit(solution)/shard_map/ppermute | solution.py:76
  179.1 6.3 %collective-permute-start.14 = (f32[2,12,4,64]{3,2,1,0:T(4,128)S(1)}, f32[2,12,4,64]{3,2,1,0:T(4,128)S(1)}, u32[]{:S(2)}, u32[]{:S(2)}) collective-permute-start(f32[2,12,4,64]{3,2,1,0:T(4,128)S(1)} %get-tuple-element.39), channel_id=1, source_target_pairs={{0,2},{2,4},{4,6},{6,8},{8,10},{10,12},{12,14},{14,16},{16,18},{18... | collective-permute-start | bytes 73736 | tf_op jit(solution)/shard_map/ppermute | solution.py:74
  183.5 5.4 %collective-permute-start.15 = (f32[2,12,4,64]{3,2,1,0:T(4,128)S(1)}, f32[2,12,4,64]{3,2,1,0:T(4,128)S(1)}, u32[]{:S(2)}, u32[]{:S(2)}) collective-permute-start(f32[2,12,4,64]{3,2,1,0:T(4,128)S(1)} %get-tuple-element.40), channel_id=1, source_target_pairs={{2,0},{4,2},{6,4},{8,6},{10,8},{12,10},{14,12},{16,14},{18,16},{20... | collective-permute-start | bytes 73736 | tf_op jit(solution)/shard_map/ppermute | solution.py:76
  189.1 7.4 %collective-permute-start.16 = (f32[2,12,24,4]{3,2,1,0:T(8,128)S(1)}, f32[2,12,24,4]{3,2,1,0:T(8,128)S(1)}, u32[]{:S(2)}, u32[]{:S(2)}) collective-permute-start(f32[2,12,24,4]{3,2,1,0:T(8,128)S(1)} %get-tuple-element.35), channel_id=1, source_target_pairs={{0,1},{2,3},{4,5},{6,7},{8,9},{10,11},{12,13},{14,15},{16,17},{18,... | collective-permute-start | bytes 27656 | tf_op jit(solution)/shard_map/ppermute | solution.py:74
  191.0 10.6 %collective-permute-start.17 = (f32[2,12,24,4]{3,2,1,0:T(8,128)S(1)}, f32[2,12,24,4]{3,2,1,0:T(8,128)S(1)}, u32[]{:S(2)}, u32[]{:S(2)}) collective-permute-start(f32[2,12,24,4]{3,2,1,0:T(8,128)S(1)} %get-tuple-element.36), channel_id=1, source_target_pairs={{1,0},{3,2},{5,4},{7,6},{9,8},{11,10},{13,12},{15,14},{17,16},{19,... | collective-permute-start | bytes 27656 | tf_op jit(solution)/shard_map/ppermute | solution.py:76
  (27 other events, 179.2 us)

commit v4 on v1

--- a/solution.py
+++ b/solution.py
@@ -140,7 +140,7 @@
     ).reshape(NAGG)
     summed = lax.psum(partial_sums, "gz")
     summed = lax.psum(summed, "gx")
-    splits = ((1, 2), (2, 2), (4, 4)) if lax.axis_size("gy") == 16 else ((1, lax.axis_size("gy")),)
+    splits = ((1, 4), (4, 4)) if lax.axis_size("gy") == 16 else ((1, lax.axis_size("gy")),)
     for stride, span in splits:
         groups = [
             [base + stride * k for k in range(span)]

time: 240 us -> 238 us (level)
    psum x3 -> x2, blocking collectives: 20.3 us -> 19.5 us  [shards(): summed = lax.psum(summed, 'gy', axis_index_groups=groups)]
where the time goes in v4:
time: 238 us; the launch traced here: 236 us
  other arithmetic  69.2 us (29%)
  waiting for transfers between devices  50 us (21%)
  starting transfers between devices  49.5 us (21%)
  blocking collectives  30.8 us (13%)
  local copies, waits for them, and re-layouts  26.1 us (11%)
  matrix products  8.85 us (4%)
    ppermute x9, starting transfers between devices, exchange(): lax.ppermute(tail, axis, [(i, i + 1) for i in range(count - 1)])  35.6 us
    ppermute x9, waiting for transfers between devices, exchange(): lax.ppermute(head, axis, [(i + 1, i) for i in range(count - 1)])  35.5 us
    select_n x10, other arithmetic, smooth_wide(): current = jnp.where(crop(mask, step), current, 0.0)  29.9 us
    psum x2, blocking collectives, shards(): summed = lax.psum(summed, 'gy', axis_index_groups=groups)  19.5 us
    concatenate x6, other arithmetic, exchange(): jnp.concatenate([lax.ppermute(tail, axis, [(i, i + 1) for i in range(coun...  18.8 us
    ppermute x9, waiting for transfers between devices, exchange(): lax.ppermute(tail, axis, [(i, i + 1) for i in range(count - 1)])  14.5 us
    ppermute x9, starting transfers between devices, exchange(): lax.ppermute(head, axis, [(i + 1, i) for i in range(count - 1)])  13.9 us
    slice x6, local copies, waits for them, and re-layouts, exchange(): lax.slice_in_dim(stack, stack.shape[dim] - width, stack.shape[dim], axis=...  8.82 us
  transfers between devices with their start and end apart: 18, of which 12 were waited for; matrix products, arithmetic and copies ran while one was open for 10% of the time, Pallas kernels for 0%

profile of v4, /device:TPU:1, one launch (start us, length us, event | category | flops | bytes accessed | tf_op | source)
XLA Modules:
  0.0 235.9 jit_solution(9083080457851918771)
XLA Ops:
  3.7 5.5 %collective-permute-start = (f32[3,5,64,256]{3,2,1,0:T(8,128)}, f32[3,5,64,256]{3,2,1,0:T(8,128)}, u32[]{:S(2)}, u32[]{:S(2)}) collective-permute-start(f32[3,5,64,256]{3,2,1,0:T(8,128)} %get-tuple-element.25), channel_id=1, source_target_pairs={{0,32},{32,64},{64,96},{1,33},{33,65},{65,97},{2,34},{34,66},{66,9... | collective-permute-start | bytes 2949128 | tf_op jit(solution)/shard_map/ppermute | solution.py:74
  19.1 9.8 %collective-permute-done = f32[3,5,64,256]{3,2,1,0:T(8,128)} collective-permute-done((f32[3,5,64,256]{3,2,1,0:T(8,128)}, f32[3,5,64,256]{3,2,1,0:T(8,128)}, u32[]{:S(2)}, u32[]{:S(2)}) %collective-permute-start) | collective-permute-done | bytes 983072 | tf_op jit(solution)/shard_map/ppermute | solution.py:74
  29.0 4.8 %collective-permute-done.1 = f32[3,5,64,256]{3,2,1,0:T(8,128)} collective-permute-done((f32[3,5,64,256]{3,2,1,0:T(8,128)}, f32[3,5,64,256]{3,2,1,0:T(8,128)}, u32[]{:S(2)}, u32[]{:S(2)}) %collective-permute-start.1) | collective-permute-done | bytes 983072 | tf_op jit(solution)/shard_map/ppermute | solution.py:76
  36.0 4.9 %collective-permute-start.2 = (f32[3,26,5,256]{3,1,2,0:T(8,128)}, f32[3,26,5,256]{3,1,2,0:T(8,128)}, u32[]{:S(2)}, u32[]{:S(2)}) collective-permute-start(f32[3,26,5,256]{3,1,2,0:T(8,128)} %copy.63), channel_id=1, source_target_pairs={{0,2},{2,4},{4,6},{6,8},{8,10},{10,12},{12,14},{14,16},{16,18},{18... | collective-permute-start | bytes 1198088 | tf_op jit(solution)/shard_map/ppermute | solution.py:74
  48.5 3.8 %collective-permute-done.3 = f32[3,26,5,256]{3,1,2,0:T(8,128)} collective-permute-done((f32[3,26,5,256]{3,1,2,0:T(8,128)}, f32[3,26,5,256]{3,1,2,0:T(8,128)}, u32[]{:S(2)}, u32[]{:S(2)}) %collective-permute-start.3) | collective-permute-done | bytes 399392 | tf_op jit(solution)/shard_map/ppermute | solution.py:76
  56.7 3.6 %fusion.113 = (f32[3,26,74,5]{3,2,1,0:T(8,128)}, f32[3,26,74,5]{3,2,1,0:T(8,128)}) fusion(f32[3,26,74,256]{3,2,1,0:T(8,128)S(1)} %pad_maximum_fusion.1), kind=kLoop, calls=%fused_computation.266 | loop fusion | bytes 461760 | tf_op jit(solution)/shard_map/slice | solution.py:71
  64.0 5.2 %collective-permute-start.4 = (f32[3,26,74,5]{2,1,3,0:T(8,128)}, f32[3,26,74,5]{2,1,3,0:T(8,128)}, u32[]{:S(2)}, u32[]{:S(2)}) collective-permute-start(f32[3,26,74,5]{2,1,3,0:T(8,128)} %copy.67), channel_id=1, source_target_pairs={{0,1},{2,3},{4,5},{6,7},{8,9},{10,11},{12,13},{14,15},{16,17},{18,... | collective-permute-start | bytes 346328 | tf_op jit(solution)/shard_map/ppermute | solution.py:74
  84.9 15.3 %pad_maximum_fusion = f32[3,26,74,266]{3,2,1,0:T(8,128)} fusion(f32[3,26,74,5]{3,2,1,0:T(8,128)} %copy.70, f32[3,26,5,256]{3,2,1,0:T(8,128)} %copy-done.6, f32[3,5,64,256]{3,2,1,0:T(8,128)} %collective-permute-done.1, f32[1,16,64,256]{3,2,1,0:T(8,128)S(1)} %bitcast.58, f32[1,16,64,256]{3,2,1,0:T(8,128)S(1)} %bitcast.62, f32[1,16,64,256]{3,2,1,0:T(8,128)S(1)} %bitcast.66, ...), kind=kLoop, calls=%fused_computation | loop fusion | flops 12282816 | bytes 12282816 | tf_op jit(solution)/shard_map/concatenate | solution.py:72
  100.2 4.5 %fusion = (f32[26,74,266]{2,1,0:T(8,128)S(1)}, f32[26,74,266]{2,1,0:T(8,128)S(1)}, f32[26,74,266]{2,1,0:T(8,128)S(1)}) fusion(f32[3,26,74,266]{3,2,1,0:T(8,128)} %pad_maximum_fusion), kind=kLoop, calls=%fused_computation.3 | loop fusion | flops 511784 | bytes 12282816 | tf_op jit(solution)/shard_map/add | solution.py:121
  104.7 7.2 %fusion.6 = f32[24,72,264]{2,1,0:T(8,128)S(1)} fusion(f32[26,74,266]{2,1,0:T(8,128)S(1)} %get-tuple-element.20, f32[26,74,266]{2,1,0:T(8,128)S(1)} %get-tuple-element.19, f32[26,74,266]{2,1,0:T(8,128)S(1)} %get-tuple-element.18, pred[26,74,266]{2,1,0:T(8,128)(4,1)S(1)} %copy-done.4), kind=kLoop, calls=%fused_computation.12 | loop fusion | flops 5474304 | bytes 18703872 | tf_op jit(solution)/shard_map/jit(_where)/select_n | solution.py:102
  111.9 6.8 %fusion.12 = f32[22,70,262]{2,1,0:T(8,128)S(1)} fusion(f32[24,72,264]{2,1,0:T(8,128)S(1)} %fusion.6, f32[26,74,266]{2,1,0:T(8,128)S(1)} %get-tuple-element.19, f32[26,74,266]{2,1,0:T(8,128)S(1)} %get-tuple-element.18, pred[26,74,266]{2,1,0:T(8,128)(4,1)S(1)} %copy-done.4), kind=kLoop, calls=%fused_computation.23 | loop fusion | flops 4841760 | bytes 16542680 | tf_op jit(solution)/shard_map/jit(_where)/select_n | solution.py:102
  118.7 6.0 %fusion.18 = f32[20,68,260]{2,1,0:T(8,128)S(1)} fusion(f32[22,70,262]{2,1,0:T(8,128)S(1)} %fusion.12, f32[26,74,266]{2,1,0:T(8,128)S(1)} %get-tuple-element.19, f32[26,74,266]{2,1,0:T(8,128)S(1)} %get-tuple-element.18, pred[26,74,266]{2,1,0:T(8,128)(4,1)S(1)} %copy-done.4), kind=kLoop, calls=%fused_computation.34 | loop fusion | flops 4243200 | bytes 14497600 | tf_op jit(solution)/shard_map/jit(_where)/select_n | solution.py:102
  124.7 5.4 %fusion.24 = f32[18,66,258]{2,1,0:T(8,128)S(1)} fusion(f32[20,68,260]{2,1,0:T(8,128)S(1)} %fusion.18, f32[26,74,266]{2,1,0:T(8,128)S(1)} %get-tuple-element.19, f32[26,74,266]{2,1,0:T(8,128)S(1)} %get-tuple-element.18, pred[26,74,266]{2,1,0:T(8,128)(4,1)S(1)} %copy-done.4), kind=kLoop, calls=%fused_computation.45 | loop fusion | flops 3678048 | bytes 12566664 | tf_op jit(solution)/shard_map/jit(_where)/select_n | solution.py:102
  138.4 3.8 %collective-permute-done.7 = f32[2,4,32,128]{3,2,1,0:T(8,128)S(1)} collective-permute-done((f32[2,4,32,128]{3,2,1,0:T(8,128)S(1)}, f32[2,4,32,128]{3,2,1,0:T(8,128)S(1)}, u32[]{:S(2)}, u32[]{:S(2)}) %collective-permute-start.7) | collective-permute-done | bytes 131104 | tf_op jit(solution)/shard_map/ppermute | solution.py:76
  142.3 6.3 %collective-permute-start.8 = (f32[2,16,4,128]{3,2,1,0:T(4,128)S(1)}, f32[2,16,4,128]{3,2,1,0:T(4,128)S(1)}, u32[]{:S(2)}, u32[]{:S(2)}) collective-permute-start(f32[2,16,4,128]{3,2,1,0:T(4,128)S(1)} %get-tuple-element.31), channel_id=1, source_target_pairs={{0,2},{2,4},{4,6},{6,8},{8,10},{10,12},{12,14},{14,16},{16,18},{18... | collective-permute-start | bytes 196616 | tf_op jit(solution)/shard_map/ppermute | solution.py:74
  158.3 4.9 %collective-permute-done.11 = f32[2,16,40,4]{2,1,3,0:T(8,128)S(1)} collective-permute-done((f32[2,16,40,4]{2,1,3,0:T(8,128)S(1)}, f32[2,16,40,4]{2,1,3,0:T(8,128)S(1)}, u32[]{:S(2)}, u32[]{:S(2)}) %collective-permute-start.11) | collective-permute-done | bytes 20512 | tf_op jit(solution)/shard_map/ppermute | solution.py:76
  174.9 4.1 %collective-permute-done.13 = f32[2,4,16,64]{3,2,1,0:T(8,128)S(1)} collective-permute-done((f32[2,4,16,64]{3,2,1,0:T(8,128)S(1)}, f32[2,4,16,64]{3,2,1,0:T(8,128)S(1)}, u32[]{:S(2)}, u32[]{:S(2)}) %collective-permute-start.13) | collective-permute-done | bytes 32800 | tf_op jit(solution)/shard_map/ppermute | solution.py:76
  179.1 4.4 %collective-permute-start.14 = (f32[2,12,4,64]{3,2,1,0:T(4,128)S(1)}, f32[2,12,4,64]{3,2,1,0:T(4,128)S(1)}, u32[]{:S(2)}, u32[]{:S(2)}) collective-permute-start(f32[2,12,4,64]{3,2,1,0:T(4,128)S(1)} %get-tuple-element.39), channel_id=1, source_target_pairs={{0,2},{2,4},{4,6},{6,8},{8,10},{10,12},{12,14},{14,16},{16,18},{18... | collective-permute-start | bytes 73736 | tf_op jit(solution)/shard_map/ppermute | solution.py:74
  192.4 4.1 %collective-permute-done.16 = f32[2,12,24,4]{3,2,1,0:T(8,128)S(1)} collective-permute-done((f32[2,12,24,4]{3,2,1,0:T(8,128)S(1)}, f32[2,12,24,4]{3,2,1,0:T(8,128)S(1)}, u32[]{:S(2)}, u32[]{:S(2)}) %collective-permute-start.16) | collective-permute-done | bytes 9248 | tf_op jit(solution)/shard_map/ppermute | solution.py:74
  196.5 5.1 %collective-permute-done.17 = f32[2,12,24,4]{3,2,1,0:T(8,128)S(1)} collective-permute-done((f32[2,12,24,4]{3,2,1,0:T(8,128)S(1)}, f32[2,12,24,4]{3,2,1,0:T(8,128)S(1)}, u32[]{:S(2)}, u32[]{:S(2)}) %collective-permute-start.17) | collective-permute-done | bytes 9248 | tf_op jit(solution)/shard_map/ppermute | solution.py:76
  204.3 5.3 %psum.28 = f32[1024]{0:T(1024)S(1)} all-reduce(f32[1024]{0:T(1024)S(1)} %reshape.365), channel_id=1, replica_groups=mesh['gx'=4,'gy'=16,'gz'=2] {'gz'}, use_global_device_ids=true, to_apply=%region_0.1 | all-reduce | flops 1024 | bytes 8192 | tf_op jit(solution)/shard_map/psum | solution.py:141
  209.6 6.0 %psum.29 = f32[1024]{0:T(1024)S(1)} all-reduce(f32[1024]{0:T(1024)S(1)} %psum.28), channel_id=1, replica_groups=mesh['gx'=4,'gy'=16,'gz'=2] {'gx'}, use_global_device_ids=true, to_apply=%region_1.2 | all-reduce | flops 1024 | bytes 8192 | tf_op jit(solution)/shard_map/psum | solution.py:142
  215.6 7.5 %psum.30 = f32[1024]{0:T(1024)S(1)} all-reduce(f32[1024]{0:T(1024)S(1)} %psum.29), channel_id=1, replica_groups={{0,2,4,6},{8,10,12,14},{16,18,20,22},{24,26,28,30},{1,3,5,7},{9,11,13,1..., use_global_device_ids=true, to_apply=%region_2.3 | all-reduce | flops 1024 | bytes 8192 | tf_op jit(solution)/shard_map/psum | solution.py:150
  223.1 12.0 %psum.31 = f32[1024]{0:T(1024)S(1)} all-reduce(f32[1024]{0:T(1024)S(1)} %psum.30), channel_id=1, replica_groups={{0,8,16,24},{2,10,18,26},{4,12,20,28},{6,14,22,30},{1,9,17,25},{3,11,19..., use_global_device_ids=true, to_apply=%region_3.4 | all-reduce | flops 1024 | bytes 8192 | tf_op jit(solution)/shard_map/psum | solution.py:150
  (167 shorter events, 88.2 us)
Async XLA Ops:
  0.6 234.5 %copy-start = (f32[64,1024]{1,0:T(8,128)S(1)}, f32[64,1024]{1,0:T(8,128)}, u32[]{:S(2)}) copy-start(f32[64,1024]{1,0:T(8,128)} %param.9) | copy-start | bytes 786436
  3.7 30.1 %copy-start.2 = (f32[16,64,256]{2,1,0:T(8,128)S(1)}, f32[16,64,256]{2,1,0:T(8,128)}, u32[]{:S(2)}) copy-start(f32[16,64,256]{2,1,0:T(8,128)} %param.5) | copy-start | bytes 3145732
  3.7 30.1 %copy-start.3 = (f32[16,64,256]{2,1,0:T(8,128)S(1)}, f32[16,64,256]{2,1,0:T(8,128)}, u32[]{:S(2)}) copy-start(f32[16,64,256]{2,1,0:T(8,128)} %param.6) | copy-start | bytes 3145732
  3.7 25.2 %collective-permute-start = (f32[3,5,64,256]{3,2,1,0:T(8,128)}, f32[3,5,64,256]{3,2,1,0:T(8,128)}, u32[]{:S(2)}, u32[]{:S(2)}) collective-permute-start(f32[3,5,64,256]{3,2,1,0:T(8,128)} %get-tuple-element.25), channel_id=1, source_target_pairs={{0,32},{32,64},{64,96},{1,33},{33,65},{65,97},{2,34},{34,66},{66,9... | collective-permute-start | bytes 2949128 | tf_op jit(solution)/shard_map/ppermute | solution.py:74
  9.2 24.6 %collective-permute-start.1 = (f32[3,5,64,256]{3,2,1,0:T(8,128)}, f32[3,5,64,256]{3,2,1,0:T(8,128)}, u32[]{:S(2)}, u32[]{:S(2)}) collective-permute-start(f32[3,5,64,256]{3,2,1,0:T(8,128)} %get-tuple-element.26), channel_id=1, source_target_pairs={{32,0},{64,32},{96,64},{33,1},{65,33},{97,65},{34,2},{66,34},{98,6... | collective-permute-start | bytes 2949128 | tf_op jit(solution)/shard_map/ppermute | solution.py:76
  10.6 24.4 %copy-start.17 = (s32[256]{0:T(256)}, s32[256]{0:T(256)S(1)}, u32[]{:S(2)}) copy-start(s32[256]{0:T(256)S(1)} %get-tuple-element.49) | copy-start | bytes 3076
  19.1 24.6 %copy-start.31 = (pred[74]{0:T(512)(128)(4,1)S(1)}, pred[74]{0:T(512)(128)(4,1)}, u32[]{:S(2)}) copy-start(pred[74]{0:T(512)(128)(4,1)} %compare_and_fusion.8) | copy-start | bytes 226
  19.1 24.6 %copy-start.32 = (pred[26]{0:T(512)(128)(4,1)S(1)}, pred[26]{0:T(512)(128)(4,1)}, u32[]{:S(2)}) copy-start(pred[26]{0:T(512)(128)(4,1)} %compare_and_fusion.9) | copy-start | bytes 82
  36.0 11.2 %collective-permute-start.2 = (f32[3,26,5,256]{3,1,2,0:T(8,128)}, f32[3,26,5,256]{3,1,2,0:T(8,128)}, u32[]{:S(2)}, u32[]{:S(2)}) collective-permute-start(f32[3,26,5,256]{3,1,2,0:T(8,128)} %copy.63), channel_id=1, source_target_pairs={{0,2},{2,4},{4,6},{6,8},{8,10},{10,12},{12,14},{14,16},{16,18},{18... | collective-permute-start | bytes 1198088 | tf_op jit(solution)/shard_map/ppermute | solution.py:74
  41.8 10.5 %collective-permute-start.3 = (f32[3,26,5,256]{3,1,2,0:T(8,128)}, f32[3,26,5,256]{3,1,2,0:T(8,128)}, u32[]{:S(2)}, u32[]{:S(2)}) collective-permute-start(f32[3,26,5,256]{3,1,2,0:T(8,128)} %copy.64), channel_id=1, source_target_pairs={{2,0},{4,2},{6,4},{8,6},{10,8},{12,10},{14,12},{16,14},{18,16},{20... | collective-permute-start | bytes 1198088 | tf_op jit(solution)/shard_map/ppermute | solution.py:76
  64.0 11.9 %collective-permute-start.4 = (f32[3,26,74,5]{2,1,3,0:T(8,128)}, f32[3,26,74,5]{2,1,3,0:T(8,128)}, u32[]{:S(2)}, u32[]{:S(2)}) collective-permute-start(f32[3,26,74,5]{2,1,3,0:T(8,128)} %copy.67), channel_id=1, source_target_pairs={{0,1},{2,3},{4,5},{6,7},{8,9},{10,11},{12,13},{14,15},{16,17},{18,... | collective-permute-start | bytes 346328 | tf_op jit(solution)/shard_map/ppermute | solution.py:74
  72.8 8.8 %collective-permute-start.5 = (f32[3,26,74,5]{2,1,3,0:T(8,128)}, f32[3,26,74,5]{2,1,3,0:T(8,128)}, u32[]{:S(2)}, u32[]{:S(2)}) collective-permute-start(f32[3,26,74,5]{2,1,3,0:T(8,128)} %copy.68), channel_id=1, source_target_pairs={{1,0},{3,2},{5,4},{7,6},{9,8},{11,10},{13,12},{15,14},{17,16},{19,... | collective-permute-start | bytes 346328 | tf_op jit(solution)/shard_map/ppermute | solution.py:76
  134.0 4.5 %collective-permute-start.6 = (f32[2,4,32,128]{3,2,1,0:T(8,128)S(1)}, f32[2,4,32,128]{3,2,1,0:T(8,128)S(1)}, u32[]{:S(2)}, u32[]{:S(2)}) collective-permute-start(f32[2,4,32,128]{3,2,1,0:T(8,128)S(1)} %get-tuple-element.37), channel_id=1, source_target_pairs={{0,32},{32,64},{64,96},{1,33},{33,65},{65,97},{2,34},{34,66},{66,9... | collective-permute-start | bytes 393224 | tf_op jit(solution)/shard_map/ppermute | solution.py:74
  136.5 5.7 %collective-permute-start.7 = (f32[2,4,32,128]{3,2,1,0:T(8,128)S(1)}, f32[2,4,32,128]{3,2,1,0:T(8,128)S(1)}, u32[]{:S(2)}, u32[]{:S(2)}) collective-permute-start(f32[2,4,32,128]{3,2,1,0:T(8,128)S(1)} %get-tuple-element.38), channel_id=1, source_target_pairs={{32,0},{64,32},{96,64},{33,1},{65,33},{97,65},{34,2},{66,34},{98,6... | collective-permute-start | bytes 393224 | tf_op jit(solution)/shard_map/ppermute | solution.py:76
  142.3 8.5 %collective-permute-start.8 = (f32[2,16,4,128]{3,2,1,0:T(4,128)S(1)}, f32[2,16,4,128]{3,2,1,0:T(4,128)S(1)}, u32[]{:S(2)}, u32[]{:S(2)}) collective-permute-start(f32[2,16,4,128]{3,2,1,0:T(4,128)S(1)} %get-tuple-element.31), channel_id=1, source_target_pairs={{0,2},{2,4},{4,6},{6,8},{8,10},{10,12},{12,14},{14,16},{16,18},{18... | collective-permute-start | bytes 196616 | tf_op jit(solution)/shard_map/ppermute | solution.py:74
  148.5 5.6 %collective-permute-start.9 = (f32[2,16,4,128]{3,2,1,0:T(4,128)S(1)}, f32[2,16,4,128]{3,2,1,0:T(4,128)S(1)}, u32[]{:S(2)}, u32[]{:S(2)}) collective-permute-start(f32[2,16,4,128]{3,2,1,0:T(4,128)S(1)} %get-tuple-element.32), channel_id=1, source_target_pairs={{2,0},{4,2},{6,4},{8,6},{10,8},{12,10},{14,12},{16,14},{18,16},{20... | collective-permute-start | bytes 196616 | tf_op jit(solution)/shard_map/ppermute | solution.py:76
  154.7 3.2 %collective-permute-start.10 = (f32[2,16,40,4]{2,1,3,0:T(8,128)S(1)}, f32[2,16,40,4]{2,1,3,0:T(8,128)S(1)}, u32[]{:S(2)}, u32[]{:S(2)}) collective-permute-start(f32[2,16,40,4]{2,1,3,0:T(8,128)S(1)} %copy.71), channel_id=1, source_target_pairs={{0,1},{2,3},{4,5},{6,7},{8,9},{10,11},{12,13},{14,15},{16,17},{18,... | collective-permute-start | bytes 61448 | tf_op jit(solution)/shard_map/ppermute | solution.py:74
  156.6 6.5 %collective-permute-start.11 = (f32[2,16,40,4]{2,1,3,0:T(8,128)S(1)}, f32[2,16,40,4]{2,1,3,0:T(8,128)S(1)}, u32[]{:S(2)}, u32[]{:S(2)}) collective-permute-start(f32[2,16,40,4]{2,1,3,0:T(8,128)S(1)} %copy.72), channel_id=1, source_target_pairs={{1,0},{3,2},{5,4},{7,6},{9,8},{11,10},{13,12},{15,14},{17,16},{19,... | collective-permute-start | bytes 61448 | tf_op jit(solution)/shard_map/ppermute | solution.py:76
  170.3 4.6 %collective-permute-start.12 = (f32[2,4,16,64]{3,2,1,0:T(8,128)S(1)}, f32[2,4,16,64]{3,2,1,0:T(8,128)S(1)}, u32[]{:S(2)}, u32[]{:S(2)}) collective-permute-start(f32[2,4,16,64]{3,2,1,0:T(8,128)S(1)} %pad_maximum_fusion.19), channel_id=1, source_target_pairs={{0,32},{32,64},{64,96},{1,33},{33,65},{65,97},{2,34},{34,66},{66,9... | collective-permute-start | bytes 98312 | tf_op jit(solution)/shard_map/ppermute | solution.py:74
  173.5 5.5 %collective-permute-start.13 = (f32[2,4,16,64]{3,2,1,0:T(8,128)S(1)}, f32[2,4,16,64]{3,2,1,0:T(8,128)S(1)}, u32[]{:S(2)}, u32[]{:S(2)}) collective-permute-start(f32[2,4,16,64]{3,2,1,0:T(8,128)S(1)} %pad_maximum_fusion.19), channel_id=1, source_target_pairs={{32,0},{64,32},{96,64},{33,1},{65,33},{97,65},{34,2},{66,34},{98,6... | collective-permute-start | bytes 98312 | tf_op jit(solution)/shard_map/ppermute | solution.py:76
  179.1 6.3 %collective-permute-start.14 = (f32[2,12,4,64]{3,2,1,0:T(4,128)S(1)}, f32[2,12,4,64]{3,2,1,0:T(4,128)S(1)}, u32[]{:S(2)}, u32[]{:S(2)}) collective-permute-start(f32[2,12,4,64]{3,2,1,0:T(4,128)S(1)} %get-tuple-element.39), channel_id=1, source_target_pairs={{0,2},{2,4},{4,6},{6,8},{8,10},{10,12},{12,14},{14,16},{16,18},{18... | collective-permute-start | bytes 73736 | tf_op jit(solution)/shard_map/ppermute | solution.py:74
  183.5 5.4 %collective-permute-start.15 = (f32[2,12,4,64]{3,2,1,0:T(4,128)S(1)}, f32[2,12,4,64]{3,2,1,0:T(4,128)S(1)}, u32[]{:S(2)}, u32[]{:S(2)}) collective-permute-start(f32[2,12,4,64]{3,2,1,0:T(4,128)S(1)} %get-tuple-element.40), channel_id=1, source_target_pairs={{2,0},{4,2},{6,4},{8,6},{10,8},{12,10},{14,12},{16,14},{18,16},{20... | collective-permute-start | bytes 73736 | tf_op jit(solution)/shard_map/ppermute | solution.py:76
  189.1 7.4 %collective-permute-start.16 = (f32[2,12,24,4]{3,2,1,0:T(8,128)S(1)}, f32[2,12,24,4]{3,2,1,0:T(8,128)S(1)}, u32[]{:S(2)}, u32[]{:S(2)}) collective-permute-start(f32[2,12,24,4]{3,2,1,0:T(8,128)S(1)} %get-tuple-element.35), channel_id=1, source_target_pairs={{0,1},{2,3},{4,5},{6,7},{8,9},{10,11},{12,13},{14,15},{16,17},{18,... | collective-permute-start | bytes 27656 | tf_op jit(solution)/shard_map/ppermute | solution.py:74
  191.0 10.6 %collective-permute-start.17 = (f32[2,12,24,4]{3,2,1,0:T(8,128)S(1)}, f32[2,12,24,4]{3,2,1,0:T(8,128)S(1)}, u32[]{:S(2)}, u32[]{:S(2)}) collective-permute-start(f32[2,12,24,4]{3,2,1,0:T(8,128)S(1)} %get-tuple-element.36), channel_id=1, source_target_pairs={{1,0},{3,2},{5,4},{7,6},{9,8},{11,10},{13,12},{15,14},{17,16},{19,... | collective-permute-start | bytes 27656 | tf_op jit(solution)/shard_map/ppermute | solution.py:76
  (27 other events, 179.1 us)

commit v5 on v4

--- a/solution.py
+++ b/solution.py
@@ -65,7 +65,7 @@
 
 
 def exchange(stack, width):
-    for axis, dim in (("gx", 1), ("gy", 2), ("gz", 3)):
+    for axis, dim in (("gx", 1), ("gz", 3), ("gy", 2)):
         count = lax.axis_size(axis)
         head = lax.slice_in_dim(stack, 0, width, axis=dim)
         tail = lax.slice_in_dim(stack, stack.shape[dim] - width, stack.shape[dim], axis=dim)

time: 238 us -> 242 us (1.017)
  waiting for transfers between devices: 50 us -> 62.9 us
  blocking collectives: 30.8 us -> 27.3 us
  other arithmetic: 69.2 us -> 66.4 us
  local copies, waits for them, and re-layouts: 26.1 us -> 23.6 us
    ppermute x9, waiting for transfers between devices: 14.5 us -> 27.5 us  [exchange(): lax.ppermute(tail, axis, [(i, i + 1) for i in range(count - 1)])]
    psum x2, blocking collectives: 19.5 us -> 15.7 us  [shards(): summed = lax.psum(summed, 'gy', axis_index_groups=groups)]
    concatenate x6, other arithmetic: 18.8 us -> 15.7 us  [exchange(): jnp.concatenate([lax.ppermute(tail, axis, [(i, i + 1) for i in range(coun...]
    slice x6 -> x5, local copies, waits for them, and re-layouts: 8.82 us -> 7.96 us  [exchange(): lax.slice_in_dim(stack, stack.shape[dim] - width, stack.shape[dim], axis=...]
    ppermute x3 -> x2, local copies, waits for them, and re-layouts: 4.96 us -> 4.74 us  [exchange(): lax.ppermute(tail, axis, [(i, i + 1) for i in range(count - 1)])]
    ppermute x3 -> x2, local copies, waits for them, and re-layouts: 4.96 us -> 4.75 us  [exchange(): lax.ppermute(head, axis, [(i + 1, i) for i in range(count - 1)])]
  transfers between devices with their start and end apart: 18 -> 18, of which waited for: 12 -> 13; matrix products, arithmetic and copies ran while one was open for 10% -> 9% of each run, Pallas kernels for 0% -> 0%
where the time goes in v5:
time: 242 us; the launch traced here: 239 us
  other arithmetic  66.4 us (27%)
  waiting for transfers between devices  62.9 us (26%)
  starting transfers between devices  49.5 us (20%)
  blocking collectives  27.3 us (11%)
  local copies, waits for them, and re-layouts  23.6 us (10%)
  matrix products  8.17 us (3%)
    ppermute x9, starting transfers between devices, exchange(): lax.ppermute(tail, axis, [(i, i + 1) for i in range(count - 1)])  35.6 us
    ppermute x9, waiting for transfers between devices, exchange(): lax.ppermute(head, axis, [(i + 1, i) for i in range(count - 1)])  35.4 us
    select_n x10, other arithmetic, smooth_wide(): current = jnp.where(crop(mask, step), current, 0.0)  29.9 us
    ppermute x9, waiting for transfers between devices, exchange(): lax.ppermute(tail, axis, [(i, i + 1) for i in range(count - 1)])  27.5 us
    psum x2, blocking collectives, shards(): summed = lax.psum(summed, 'gy', axis_index_groups=groups)  15.7 us
    concatenate x6, other arithmetic, exchange(): jnp.concatenate([lax.ppermute(tail, axis, [(i, i + 1) for i in range(coun...  15.7 us
    ppermute x9, starting transfers between devices, exchange(): lax.ppermute(head, axis, [(i + 1, i) for i in range(count - 1)])  13.9 us
    slice x5, local copies, waits for them, and re-layouts, exchange(): lax.slice_in_dim(stack, stack.shape[dim] - width, stack.shape[dim], axis=...  7.96 us
  transfers between devices with their start and end apart: 18, of which 13 were waited for; matrix products, arithmetic and copies ran while one was open for 9% of the time, Pallas kernels for 0%

profile of v5, /device:TPU:1, one launch (start us, length us, event | category | flops | bytes accessed | tf_op | source)
XLA Modules:
  0.0 239.3 jit_solution(7513064580427549841)
XLA Ops:
  3.7 5.5 %collective-permute-start = (f32[3,5,64,256]{3,2,1,0:T(8,128)}, f32[3,5,64,256]{3,2,1,0:T(8,128)}, u32[]{:S(2)}, u32[]{:S(2)}) collective-permute-start(f32[3,5,64,256]{3,2,1,0:T(8,128)} %get-tuple-element.25), channel_id=1, source_target_pairs={{0,32},{32,64},{64,96},{1,33},{33,65},{65,97},{2,34},{34,66},{66,9... | collective-permute-start | bytes 2949128 | tf_op jit(solution)/shard_map/ppermute | solution.py:74
  19.7 9.3 %collective-permute-done = f32[3,5,64,256]{3,2,1,0:T(8,128)} collective-permute-done((f32[3,5,64,256]{3,2,1,0:T(8,128)}, f32[3,5,64,256]{3,2,1,0:T(8,128)}, u32[]{:S(2)}, u32[]{:S(2)}) %collective-permute-start) | collective-permute-done | bytes 983072 | tf_op jit(solution)/shard_map/ppermute | solution.py:74
  29.0 4.8 %collective-permute-done.1 = f32[3,5,64,256]{3,2,1,0:T(8,128)} collective-permute-done((f32[3,5,64,256]{3,2,1,0:T(8,128)}, f32[3,5,64,256]{3,2,1,0:T(8,128)}, u32[]{:S(2)}, u32[]{:S(2)}) %collective-permute-start.1) | collective-permute-done | bytes 983072 | tf_op jit(solution)/shard_map/ppermute | solution.py:76
  42.2 5.5 %collective-permute-start.2 = (f32[3,26,64,5]{2,1,3,0:T(8,128)}, f32[3,26,64,5]{2,1,3,0:T(8,128)}, u32[]{:S(2)}, u32[]{:S(2)}) collective-permute-start(f32[3,26,64,5]{2,1,3,0:T(8,128)} %copy.45), channel_id=1, source_target_pairs={{0,1},{2,3},{4,5},{6,7},{8,9},{10,11},{12,13},{14,15},{16,17},{18,... | collective-permute-start | bytes 299528 | tf_op jit(solution)/shard_map/ppermute | solution.py:74
  55.7 4.5 %collective-permute-done.3 = f32[3,26,64,5]{2,1,3,0:T(8,128)} collective-permute-done((f32[3,26,64,5]{2,1,3,0:T(8,128)}, f32[3,26,64,5]{2,1,3,0:T(8,128)}, u32[]{:S(2)}, u32[]{:S(2)}) %collective-permute-start.3) | collective-permute-done | bytes 99872 | tf_op jit(solution)/shard_map/ppermute | solution.py:76
  66.7 5.1 %collective-permute-start.4 = (f32[3,26,5,266]{3,1,2,0:T(8,128)}, f32[3,26,5,266]{3,1,2,0:T(8,128)}, u32[]{:S(2)}, u32[]{:S(2)}) collective-permute-start(f32[3,26,5,266]{3,1,2,0:T(8,128)} %copy.49), channel_id=1, source_target_pairs={{0,2},{2,4},{4,6},{6,8},{8,10},{10,12},{12,14},{14,16},{16,18},{18... | collective-permute-start | bytes 1244888 | tf_op jit(solution)/shard_map/ppermute | solution.py:74
  77.8 10.6 %collective-permute-done.4 = f32[3,26,5,266]{3,1,2,0:T(8,128)} collective-permute-done((f32[3,26,5,266]{3,1,2,0:T(8,128)}, f32[3,26,5,266]{3,1,2,0:T(8,128)}, u32[]{:S(2)}, u32[]{:S(2)}) %collective-permute-start.4) | collective-permute-done | bytes 414992 | tf_op jit(solution)/shard_map/ppermute | solution.py:74
  91.4 13.1 %pad_maximum_fusion = f32[3,26,74,266]{3,2,1,0:T(8,128)} fusion(f32[3,26,5,266]{3,2,1,0:T(8,128)S(1)} %copy.52, f32[3,26,64,5]{3,2,1,0:T(8,128)} %copy.48, f32[3,5,64,256]{3,2,1,0:T(8,128)} %collective-permute-done.1, f32[1,16,64,256]{3,2,1,0:T(8,128)S(1)} %bitcast.58, f32[1,16,64,256]{3,2,1,0:T(8,128)S(1)} %bitcast.62, f32[1,16,64,256]{3,2,1,0:T(8,128)S(1)} %bitcast.66, ...), kind=kLoop, calls=%fused_computation | loop fusion | flops 12282816 | bytes 12282816 | tf_op jit(solution)/shard_map/concatenate | solution.py:72
  104.5 4.5 %fusion = (f32[26,74,266]{2,1,0:T(8,128)S(1)}, f32[26,74,266]{2,1,0:T(8,128)S(1)}, f32[26,74,266]{2,1,0:T(8,128)S(1)}) fusion(f32[3,26,74,266]{3,2,1,0:T(8,128)} %pad_maximum_fusion), kind=kLoop, calls=%fused_computation.3 | loop fusion | flops 511784 | bytes 12282816 | tf_op jit(solution)/shard_map/add | solution.py:121
  109.0 7.2 %fusion.6 = f32[24,72,264]{2,1,0:T(8,128)S(1)} fusion(f32[26,74,266]{2,1,0:T(8,128)S(1)} %get-tuple-element.22, f32[26,74,266]{2,1,0:T(8,128)S(1)} %get-tuple-element.21, f32[26,74,266]{2,1,0:T(8,128)S(1)} %get-tuple-element.20, pred[26,74,266]{2,1,0:T(8,128)(4,1)S(1)} %broadcast_and_fusion), kind=kLoop, calls=%fused_computation.12 | loop fusion | flops 5474304 | bytes 18703872 | tf_op jit(solution)/shard_map/jit(_where)/select_n | solution.py:102
  116.2 6.5 %fusion.12 = f32[22,70,262]{2,1,0:T(8,128)S(1)} fusion(f32[24,72,264]{2,1,0:T(8,128)S(1)} %fusion.6, f32[26,74,266]{2,1,0:T(8,128)S(1)} %get-tuple-element.21, f32[26,74,266]{2,1,0:T(8,128)S(1)} %get-tuple-element.20, pred[26,74,266]{2,1,0:T(8,128)(4,1)S(1)} %broadcast_and_fusion), kind=kLoop, calls=%fused_computation.23 | loop fusion | flops 4841760 | bytes 16542680 | tf_op jit(solution)/shard_map/jit(_where)/select_n | solution.py:102
  122.8 6.2 %fusion.18 = f32[20,68,260]{2,1,0:T(8,128)S(1)} fusion(f32[22,70,262]{2,1,0:T(8,128)S(1)} %fusion.12, f32[26,74,266]{2,1,0:T(8,128)S(1)} %get-tuple-element.21, f32[26,74,266]{2,1,0:T(8,128)S(1)} %get-tuple-element.20, pred[26,74,266]{2,1,0:T(8,128)(4,1)S(1)} %broadcast_and_fusion), kind=kLoop, calls=%fused_computation.34 | loop fusion | flops 4243200 | bytes 14497600 | tf_op jit(solution)/shard_map/jit(_where)/select_n | solution.py:102
  129.0 5.4 %fusion.24 = f32[18,66,258]{2,1,0:T(8,128)S(1)} fusion(f32[20,68,260]{2,1,0:T(8,128)S(1)} %fusion.18, f32[26,74,266]{2,1,0:T(8,128)S(1)} %get-tuple-element.21, f32[26,74,266]{2,1,0:T(8,128)S(1)} %get-tuple-element.20, pred[26,74,266]{2,1,0:T(8,128)(4,1)S(1)} %broadcast_and_fusion), kind=kLoop, calls=%fused_computation.45 | loop fusion | flops 3678048 | bytes 12566664 | tf_op jit(solution)/shard_map/jit(_where)/select_n | solution.py:102
  142.7 4.1 %collective-permute-done.7 = f32[2,4,32,128]{3,2,1,0:T(8,128)S(1)} collective-permute-done((f32[2,4,32,128]{3,2,1,0:T(8,128)S(1)}, f32[2,4,32,128]{3,2,1,0:T(8,128)S(1)}, u32[]{:S(2)}, u32[]{:S(2)}) %collective-permute-start.7) | collective-permute-done | bytes 131104 | tf_op jit(solution)/shard_map/ppermute | solution.py:76
  150.2 4.8 %collective-permute-done.8 = f32[2,16,32,4]{3,2,1,0:T(8,128)S(1)} collective-permute-done((f32[2,16,32,4]{3,2,1,0:T(8,128)S(1)}, f32[2,16,32,4]{3,2,1,0:T(8,128)S(1)}, u32[]{:S(2)}, u32[]{:S(2)}) %collective-permute-start.8) | collective-permute-done | bytes 16416 | tf_op jit(solution)/shard_map/ppermute | solution.py:74
  154.9 5.4 %collective-permute-done.9 = f32[2,16,32,4]{3,2,1,0:T(8,128)S(1)} collective-permute-done((f32[2,16,32,4]{3,2,1,0:T(8,128)S(1)}, f32[2,16,32,4]{3,2,1,0:T(8,128)S(1)}, u32[]{:S(2)}, u32[]{:S(2)}) %collective-permute-start.9) | collective-permute-done | bytes 16416 | tf_op jit(solution)/shard_map/ppermute | solution.py:76
  160.6 6.3 %collective-permute-start.10 = (f32[2,16,4,136]{3,2,1,0:T(4,128)S(1)}, f32[2,16,4,136]{3,2,1,0:T(4,128)S(1)}, u32[]{:S(2)}, u32[]{:S(2)}) collective-permute-start(f32[2,16,4,136]{3,2,1,0:T(4,128)S(1)} %get-tuple-element.27), channel_id=1, source_target_pairs={{0,2},{2,4},{4,6},{6,8},{8,10},{10,12},{12,14},{14,16},{16,18},{18... | collective-permute-start | bytes 208904 | tf_op jit(solution)/shard_map/ppermute | solution.py:74
  169.2 4.1 %collective-permute-done.11 = f32[2,16,4,136]{3,2,1,0:T(4,128)S(1)} collective-permute-done((f32[2,16,4,136]{3,2,1,0:T(4,128)S(1)}, f32[2,16,4,136]{3,2,1,0:T(4,128)S(1)}, u32[]{:S(2)}, u32[]{:S(2)}) %collective-permute-start.11) | collective-permute-done | bytes 69664 | tf_op jit(solution)/shard_map/ppermute | solution.py:76
  184.8 3.6 %collective-permute-done.13 = f32[2,4,16,64]{3,2,1,0:T(8,128)S(1)} collective-permute-done((f32[2,4,16,64]{3,2,1,0:T(8,128)S(1)}, f32[2,4,16,64]{3,2,1,0:T(8,128)S(1)}, u32[]{:S(2)}, u32[]{:S(2)}) %collective-permute-start.13) | collective-permute-done | bytes 32800 | tf_op jit(solution)/shard_map/ppermute | solution.py:76
  193.9 5.6 %collective-permute-done.15 = f32[2,12,16,4]{3,2,1,0:T(8,128)S(1)} collective-permute-done((f32[2,12,16,4]{3,2,1,0:T(8,128)S(1)}, f32[2,12,16,4]{3,2,1,0:T(8,128)S(1)}, u32[]{:S(2)}, u32[]{:S(2)}) %collective-permute-start.15) | collective-permute-done | bytes 6176 | tf_op jit(solution)/shard_map/ppermute | solution.py:76
  211.2 5.3 %psum.28 = f32[1024]{0:T(1024)S(1)} all-reduce(f32[1024]{0:T(1024)S(1)} %reshape.365), channel_id=1, replica_groups=mesh['gx'=4,'gy'=16,'gz'=2] {'gz'}, use_global_device_ids=true, to_apply=%region_0.1 | all-reduce | flops 1024 | bytes 8192 | tf_op jit(solution)/shard_map/psum | solution.py:141
  216.5 6.3 %psum.29 = f32[1024]{0:T(1024)S(1)} all-reduce(f32[1024]{0:T(1024)S(1)} %psum.28), channel_id=1, replica_groups=mesh['gx'=4,'gy'=16,'gz'=2] {'gx'}, use_global_device_ids=true, to_apply=%region_1.2 | all-reduce | flops 1024 | bytes 8192 | tf_op jit(solution)/shard_map/psum | solution.py:142
  222.7 6.9 %psum.30 = f32[1024]{0:T(1024)S(1)} all-reduce(f32[1024]{0:T(1024)S(1)} %psum.29), channel_id=1, replica_groups={{0,2,4,6},{8,10,12,14},{16,18,20,22},{24,26,28,30},{1,3,5,7},{9,11,13,1..., use_global_device_ids=true, to_apply=%region_2.3 | all-reduce | flops 1024 | bytes 8192 | tf_op jit(solution)/shard_map/psum | solution.py:150
  229.7 8.8 %psum.31 = f32[1024]{0:T(1024)S(1)} all-reduce(f32[1024]{0:T(1024)S(1)} %psum.30), channel_id=1, replica_groups={{0,8,16,24},{2,10,18,26},{4,12,20,28},{6,14,22,30},{1,9,17,25},{3,11,19..., use_global_device_ids=true, to_apply=%region_3.4 | all-reduce | flops 1024 | bytes 8192 | tf_op jit(solution)/shard_map/psum | solution.py:150
  (157 shorter events, 88.4 us)
Async XLA Ops:
  0.6 237.9 %copy-start = (f32[64,1024]{1,0:T(8,128)S(1)}, f32[64,1024]{1,0:T(8,128)}, u32[]{:S(2)}) copy-start(f32[64,1024]{1,0:T(8,128)} %param.9) | copy-start | bytes 786436
  3.7 30.0 %copy-start.2 = (f32[16,64,256]{2,1,0:T(8,128)S(1)}, f32[16,64,256]{2,1,0:T(8,128)}, u32[]{:S(2)}) copy-start(f32[16,64,256]{2,1,0:T(8,128)} %param.5) | copy-start | bytes 3145732
  3.7 30.0 %copy-start.4 = (f32[16,64,256]{2,1,0:T(8,128)S(1)}, f32[16,64,256]{2,1,0:T(8,128)}, u32[]{:S(2)}) copy-start(f32[16,64,256]{2,1,0:T(8,128)} %param.6) | copy-start | bytes 3145732
  3.7 25.2 %collective-permute-start = (f32[3,5,64,256]{3,2,1,0:T(8,128)}, f32[3,5,64,256]{3,2,1,0:T(8,128)}, u32[]{:S(2)}, u32[]{:S(2)}) collective-permute-start(f32[3,5,64,256]{3,2,1,0:T(8,128)} %get-tuple-element.25), channel_id=1, source_target_pairs={{0,32},{32,64},{64,96},{1,33},{33,65},{65,97},{2,34},{34,66},{66,9... | collective-permute-start | bytes 2949128 | tf_op jit(solution)/shard_map/ppermute | solution.py:74
  9.2 24.6 %collective-permute-start.1 = (f32[3,5,64,256]{3,2,1,0:T(8,128)}, f32[3,5,64,256]{3,2,1,0:T(8,128)}, u32[]{:S(2)}, u32[]{:S(2)}) collective-permute-start(f32[3,5,64,256]{3,2,1,0:T(8,128)} %get-tuple-element.26), channel_id=1, source_target_pairs={{32,0},{64,32},{96,64},{33,1},{65,33},{97,65},{34,2},{66,34},{98,6... | collective-permute-start | bytes 2949128 | tf_op jit(solution)/shard_map/ppermute | solution.py:76
  10.6 24.9 %copy-start.15 = (s32[256]{0:T(256)}, s32[256]{0:T(256)S(1)}, u32[]{:S(2)}) copy-start(s32[256]{0:T(256)S(1)} %get-tuple-element.49) | copy-start | bytes 3076
  10.6 24.9 %copy-start.17 = (s32[256]{0:T(256)}, s32[256]{0:T(256)S(1)}, u32[]{:S(2)}) copy-start(s32[256]{0:T(256)S(1)} %get-tuple-element.50) | copy-start | bytes 3076
  11.2 24.3 %copy-start.21 = (s32[128]{0:T(128)}, s32[128]{0:T(128)S(1)}, u32[]{:S(2)}) copy-start(s32[128]{0:T(128)S(1)} %get-tuple-element.52) | copy-start | bytes 1540
  42.2 10.3 %collective-permute-start.2 = (f32[3,26,64,5]{2,1,3,0:T(8,128)}, f32[3,26,64,5]{2,1,3,0:T(8,128)}, u32[]{:S(2)}, u32[]{:S(2)}) collective-permute-start(f32[3,26,64,5]{2,1,3,0:T(8,128)} %copy.45), channel_id=1, source_target_pairs={{0,1},{2,3},{4,5},{6,7},{8,9},{10,11},{12,13},{14,15},{16,17},{18,... | collective-permute-start | bytes 299528 | tf_op jit(solution)/shard_map/ppermute | solution.py:74
  51.1 9.1 %collective-permute-start.3 = (f32[3,26,64,5]{2,1,3,0:T(8,128)}, f32[3,26,64,5]{2,1,3,0:T(8,128)}, u32[]{:S(2)}, u32[]{:S(2)}) collective-permute-start(f32[3,26,64,5]{2,1,3,0:T(8,128)} %copy.46), channel_id=1, source_target_pairs={{1,0},{3,2},{5,4},{7,6},{9,8},{11,10},{13,12},{15,14},{17,16},{19,... | collective-permute-start | bytes 299528 | tf_op jit(solution)/shard_map/ppermute | solution.py:76
  66.7 21.7 %collective-permute-start.4 = (f32[3,26,5,266]{3,1,2,0:T(8,128)}, f32[3,26,5,266]{3,1,2,0:T(8,128)}, u32[]{:S(2)}, u32[]{:S(2)}) collective-permute-start(f32[3,26,5,266]{3,1,2,0:T(8,128)} %copy.49), channel_id=1, source_target_pairs={{0,2},{2,4},{4,6},{6,8},{8,10},{10,12},{12,14},{14,16},{16,18},{18... | collective-permute-start | bytes 1244888 | tf_op jit(solution)/shard_map/ppermute | solution.py:74
  72.8 17.1 %collective-permute-start.5 = (f32[3,26,5,266]{3,1,2,0:T(8,128)}, f32[3,26,5,266]{3,1,2,0:T(8,128)}, u32[]{:S(2)}, u32[]{:S(2)}) collective-permute-start(f32[3,26,5,266]{3,1,2,0:T(8,128)} %copy.50), channel_id=1, source_target_pairs={{2,0},{4,2},{6,4},{8,6},{10,8},{12,10},{14,12},{16,14},{18,16},{20... | collective-permute-start | bytes 1244888 | tf_op jit(solution)/shard_map/ppermute | solution.py:76
  138.2 4.5 %collective-permute-start.6 = (f32[2,4,32,128]{3,2,1,0:T(8,128)S(1)}, f32[2,4,32,128]{3,2,1,0:T(8,128)S(1)}, u32[]{:S(2)}, u32[]{:S(2)}) collective-permute-start(f32[2,4,32,128]{3,2,1,0:T(8,128)S(1)} %get-tuple-element.37), channel_id=1, source_target_pairs={{0,32},{32,64},{64,96},{1,33},{33,65},{65,97},{2,34},{34,66},{66,9... | collective-permute-start | bytes 393224 | tf_op jit(solution)/shard_map/ppermute | solution.py:74
  140.8 6.0 %collective-permute-start.7 = (f32[2,4,32,128]{3,2,1,0:T(8,128)S(1)}, f32[2,4,32,128]{3,2,1,0:T(8,128)S(1)}, u32[]{:S(2)}, u32[]{:S(2)}) collective-permute-start(f32[2,4,32,128]{3,2,1,0:T(8,128)S(1)} %get-tuple-element.38), channel_id=1, source_target_pairs={{32,0},{64,32},{96,64},{33,1},{65,33},{97,65},{34,2},{66,34},{98,6... | collective-permute-start | bytes 393224 | tf_op jit(solution)/shard_map/ppermute | solution.py:76
  147.0 7.9 %collective-permute-start.8 = (f32[2,16,32,4]{3,2,1,0:T(8,128)S(1)}, f32[2,16,32,4]{3,2,1,0:T(8,128)S(1)}, u32[]{:S(2)}, u32[]{:S(2)}) collective-permute-start(f32[2,16,32,4]{3,2,1,0:T(8,128)S(1)} %get-tuple-element.33), channel_id=1, source_target_pairs={{0,1},{2,3},{4,5},{6,7},{8,9},{10,11},{12,13},{14,15},{16,17},{18,... | collective-permute-start | bytes 49160 | tf_op jit(solution)/shard_map/ppermute | solution.py:74
  148.9 11.4 %collective-permute-start.9 = (f32[2,16,32,4]{3,2,1,0:T(8,128)S(1)}, f32[2,16,32,4]{3,2,1,0:T(8,128)S(1)}, u32[]{:S(2)}, u32[]{:S(2)}) collective-permute-start(f32[2,16,32,4]{3,2,1,0:T(8,128)S(1)} %get-tuple-element.34), channel_id=1, source_target_pairs={{1,0},{3,2},{5,4},{7,6},{9,8},{11,10},{13,12},{15,14},{17,16},{19,... | collective-permute-start | bytes 49160 | tf_op jit(solution)/shard_map/ppermute | solution.py:76
  160.6 8.6 %collective-permute-start.10 = (f32[2,16,4,136]{3,2,1,0:T(4,128)S(1)}, f32[2,16,4,136]{3,2,1,0:T(4,128)S(1)}, u32[]{:S(2)}, u32[]{:S(2)}) collective-permute-start(f32[2,16,4,136]{3,2,1,0:T(4,128)S(1)} %get-tuple-element.27), channel_id=1, source_target_pairs={{0,2},{2,4},{4,6},{6,8},{8,10},{10,12},{12,14},{14,16},{16,18},{18... | collective-permute-start | bytes 208904 | tf_op jit(solution)/shard_map/ppermute | solution.py:74
  166.9 6.3 %collective-permute-start.11 = (f32[2,16,4,136]{3,2,1,0:T(4,128)S(1)}, f32[2,16,4,136]{3,2,1,0:T(4,128)S(1)}, u32[]{:S(2)}, u32[]{:S(2)}) collective-permute-start(f32[2,16,4,136]{3,2,1,0:T(4,128)S(1)} %get-tuple-element.28), channel_id=1, source_target_pairs={{2,0},{4,2},{6,4},{8,6},{10,8},{12,10},{14,12},{16,14},{18,16},{20... | collective-permute-start | bytes 208904 | tf_op jit(solution)/shard_map/ppermute | solution.py:76
  179.9 4.9 %collective-permute-start.12 = (f32[2,4,16,64]{3,2,1,0:T(8,128)S(1)}, f32[2,4,16,64]{3,2,1,0:T(8,128)S(1)}, u32[]{:S(2)}, u32[]{:S(2)}) collective-permute-start(f32[2,4,16,64]{3,2,1,0:T(8,128)S(1)} %pad_maximum_fusion.23), channel_id=1, source_target_pairs={{0,32},{32,64},{64,96},{1,33},{33,65},{65,97},{2,34},{34,66},{66,9... | collective-permute-start | bytes 98312 | tf_op jit(solution)/shard_map/ppermute | solution.py:74
  183.4 5.0 %collective-permute-start.13 = (f32[2,4,16,64]{3,2,1,0:T(8,128)S(1)}, f32[2,4,16,64]{3,2,1,0:T(8,128)S(1)}, u32[]{:S(2)}, u32[]{:S(2)}) collective-permute-start(f32[2,4,16,64]{3,2,1,0:T(8,128)S(1)} %pad_maximum_fusion.23), channel_id=1, source_target_pairs={{32,0},{64,32},{96,64},{33,1},{65,33},{97,65},{34,2},{66,34},{98,6... | collective-permute-start | bytes 98312 | tf_op jit(solution)/shard_map/ppermute | solution.py:76
  188.6 5.3 %collective-permute-start.14 = (f32[2,12,16,4]{3,2,1,0:T(8,128)S(1)}, f32[2,12,16,4]{3,2,1,0:T(8,128)S(1)}, u32[]{:S(2)}, u32[]{:S(2)}) collective-permute-start(f32[2,12,16,4]{3,2,1,0:T(8,128)S(1)} %get-tuple-element.39), channel_id=1, source_target_pairs={{0,1},{2,3},{4,5},{6,7},{8,9},{10,11},{12,13},{14,15},{16,17},{18,... | collective-permute-start | bytes 18440 | tf_op jit(solution)/shard_map/ppermute | solution.py:74
  190.3 9.2 %collective-permute-start.15 = (f32[2,12,16,4]{3,2,1,0:T(8,128)S(1)}, f32[2,12,16,4]{3,2,1,0:T(8,128)S(1)}, u32[]{:S(2)}, u32[]{:S(2)}) collective-permute-start(f32[2,12,16,4]{3,2,1,0:T(8,128)S(1)} %get-tuple-element.40), channel_id=1, source_target_pairs={{1,0},{3,2},{5,4},{7,6},{9,8},{11,10},{13,12},{15,14},{17,16},{19,... | collective-permute-start | bytes 18440 | tf_op jit(solution)/shard_map/ppermute | solution.py:76
  199.7 5.5 %collective-permute-start.16 = (f32[2,12,4,72]{3,2,1,0:T(4,128)S(1)}, f32[2,12,4,72]{3,2,1,0:T(4,128)S(1)}, u32[]{:S(2)}, u32[]{:S(2)}) collective-permute-start(f32[2,12,4,72]{3,2,1,0:T(4,128)S(1)} %get-tuple-element.31), channel_id=1, source_target_pairs={{0,2},{2,4},{4,6},{6,8},{8,10},{10,12},{12,14},{14,16},{16,18},{18... | collective-permute-start | bytes 82952 | tf_op jit(solution)/shard_map/ppermute | solution.py:74
  203.2 5.4 %collective-permute-start.17 = (f32[2,12,4,72]{3,2,1,0:T(4,128)S(1)}, f32[2,12,4,72]{3,2,1,0:T(4,128)S(1)}, u32[]{:S(2)}, u32[]{:S(2)}) collective-permute-start(f32[2,12,4,72]{3,2,1,0:T(4,128)S(1)} %get-tuple-element.32), channel_id=1, source_target_pairs={{2,0},{4,2},{6,4},{8,6},{10,8},{12,10},{14,12},{16,14},{18,16},{20... | collective-permute-start | bytes 82952 | tf_op jit(solution)/shard_map/ppermute | solution.py:76
  (24 other events, 144.0 us)

commit v6 on v3

--- a/solution.py
+++ b/solution.py
@@ -138,15 +138,15 @@
     partial_sums = lax.dot_general(
         high, low, (((0,), (0,)), ((), ())), precision=lax.Precision.HIGHEST
     ).reshape(NAGG)
-    summed = lax.psum(partial_sums, ("gx", "gz"))
-    splits = ((1, 4), (4, 4)) if lax.axis_size("gy") == 16 else ((1, lax.axis_size("gy")),)
-    for stride, span in splits:
-        groups = [
-            [base + stride * k for k in range(span)]
-            for base in range(lax.axis_size("gy"))
-            if base % (stride * span) < stride
-        ]
-        summed = lax.psum(summed, "gy", axis_index_groups=groups)
+    summed = lax.psum(partial_sums, "gx")
+    if lax.axis_size("gy") == 16:
+        depth = lax.axis_size("gz")
+        column = [[(base + j) * depth + z for j in range(4) for z in range(depth)] for base in range(0, 16, 4)]
+        summed = lax.psum(summed, ("gy", "gz"), axis_index_groups=column)
+        rows = [[base + 4 * k for k in range(4)] for base in range(4)]
+        summed = lax.psum(summed, "gy", axis_index_groups=rows)
+    else:
+        summed = lax.psum(summed, ("gy", "gz"))
     group_cells = (
         coarse_source.size * lax.axis_size("gx") * lax.axis_size("gy") * lax.axis_size("gz") // NAGG
     )

time: 243 us -> 241 us (level)
  no operation moved by 1% of the time
where the time goes in v6:
time: 241 us; the launch traced here: 239 us
  other arithmetic  69.4 us (29%)
  waiting for transfers between devices  49.7 us (21%)
  starting transfers between devices  49.5 us (21%)
  blocking collectives  33.5 us (14%)
  local copies, waits for them, and re-layouts  26.1 us (11%)
  matrix products  8.96 us (4%)
    ppermute x9, starting transfers between devices, exchange(): lax.ppermute(tail, axis, [(i, i + 1) for i in range(count - 1)])  35.6 us
    ppermute x9, waiting for transfers between devices, exchange(): lax.ppermute(head, axis, [(i + 1, i) for i in range(count - 1)])  35.5 us
    select_n x10, other arithmetic, smooth_wide(): current = jnp.where(crop(mask, step), current, 0.0)  29.9 us
    concatenate x6, other arithmetic, exchange(): jnp.concatenate([lax.ppermute(tail, axis, [(i, i + 1) for i in range(coun...  18.8 us
    psum x1, blocking collectives, shards(): summed = lax.psum(summed, ('gy', 'gz'), axis_index_groups=column)  16.6 us
    ppermute x9, waiting for transfers between devices, exchange(): lax.ppermute(tail, axis, [(i, i + 1) for i in range(count - 1)])  14.2 us
    ppermute x9, starting transfers between devices, exchange(): lax.ppermute(head, axis, [(i + 1, i) for i in range(count - 1)])  13.9 us
    psum x1, blocking collectives, shards(): summed = lax.psum(summed, 'gy', axis_index_groups=rows)  10.9 us
  transfers between devices with their start and end apart: 18, of which 12 were waited for; matrix products, arithmetic and copies ran while one was open for 10% of the time, Pallas kernels for 0%

profile of v6, /device:TPU:1, one launch (start us, length us, event | category | flops | bytes accessed | tf_op | source)
XLA Modules:
  0.0 238.6 jit_solution(4065428628872745547)
XLA Ops:
  3.8 5.5 %collective-permute-start = (f32[3,5,64,256]{3,2,1,0:T(8,128)}, f32[3,5,64,256]{3,2,1,0:T(8,128)}, u32[]{:S(2)}, u32[]{:S(2)}) collective-permute-start(f32[3,5,64,256]{3,2,1,0:T(8,128)} %get-tuple-element.25), channel_id=1, source_target_pairs={{0,32},{32,64},{64,96},{1,33},{33,65},{65,97},{2,34},{34,66},{66,9... | collective-permute-start | bytes 2949128 | tf_op jit(solution)/shard_map/ppermute | solution.py:74
  19.5 9.5 %collective-permute-done = f32[3,5,64,256]{3,2,1,0:T(8,128)} collective-permute-done((f32[3,5,64,256]{3,2,1,0:T(8,128)}, f32[3,5,64,256]{3,2,1,0:T(8,128)}, u32[]{:S(2)}, u32[]{:S(2)}) %collective-permute-start) | collective-permute-done | bytes 983072 | tf_op jit(solution)/shard_map/ppermute | solution.py:74
  29.0 4.8 %collective-permute-done.1 = f32[3,5,64,256]{3,2,1,0:T(8,128)} collective-permute-done((f32[3,5,64,256]{3,2,1,0:T(8,128)}, f32[3,5,64,256]{3,2,1,0:T(8,128)}, u32[]{:S(2)}, u32[]{:S(2)}) %collective-permute-start.1) | collective-permute-done | bytes 983072 | tf_op jit(solution)/shard_map/ppermute | solution.py:76
  36.0 4.9 %collective-permute-start.2 = (f32[3,26,5,256]{3,1,2,0:T(8,128)}, f32[3,26,5,256]{3,1,2,0:T(8,128)}, u32[]{:S(2)}, u32[]{:S(2)}) collective-permute-start(f32[3,26,5,256]{3,1,2,0:T(8,128)} %copy.63), channel_id=1, source_target_pairs={{0,2},{2,4},{4,6},{6,8},{8,10},{10,12},{12,14},{14,16},{16,18},{18... | collective-permute-start | bytes 1198088 | tf_op jit(solution)/shard_map/ppermute | solution.py:74
  48.5 3.8 %collective-permute-done.3 = f32[3,26,5,256]{3,1,2,0:T(8,128)} collective-permute-done((f32[3,26,5,256]{3,1,2,0:T(8,128)}, f32[3,26,5,256]{3,1,2,0:T(8,128)}, u32[]{:S(2)}, u32[]{:S(2)}) %collective-permute-start.3) | collective-permute-done | bytes 399392 | tf_op jit(solution)/shard_map/ppermute | solution.py:76
  56.7 3.7 %fusion.113 = (f32[3,26,74,5]{3,2,1,0:T(8,128)}, f32[3,26,74,5]{3,2,1,0:T(8,128)}) fusion(f32[3,26,74,256]{3,2,1,0:T(8,128)S(1)} %pad_maximum_fusion.1), kind=kLoop, calls=%fused_computation.266 | loop fusion | bytes 461760 | tf_op jit(solution)/shard_map/slice | solution.py:71
  60.4 3.6 %copy.67 = f32[3,26,74,5]{2,1,3,0:T(8,128)} copy(f32[3,26,74,5]{3,2,1,0:T(8,128)} %get-tuple-element.21) | data formatting | bytes 230880 | tf_op jit(solution)/shard_map/slice | solution.py:71
  64.0 5.2 %collective-permute-start.4 = (f32[3,26,74,5]{2,1,3,0:T(8,128)}, f32[3,26,74,5]{2,1,3,0:T(8,128)}, u32[]{:S(2)}, u32[]{:S(2)}) collective-permute-start(f32[3,26,74,5]{2,1,3,0:T(8,128)} %copy.67), channel_id=1, source_target_pairs={{0,1},{2,3},{4,5},{6,7},{8,9},{10,11},{12,13},{14,15},{16,17},{18,... | collective-permute-start | bytes 346328 | tf_op jit(solution)/shard_map/ppermute | solution.py:74
  84.9 15.3 %pad_maximum_fusion = f32[3,26,74,266]{3,2,1,0:T(8,128)} fusion(f32[3,26,74,5]{3,2,1,0:T(8,128)} %copy.70, f32[3,26,5,256]{3,2,1,0:T(8,128)} %copy-done.6, f32[3,5,64,256]{3,2,1,0:T(8,128)} %collective-permute-done.1, f32[1,16,64,256]{3,2,1,0:T(8,128)S(1)} %bitcast.58, f32[1,16,64,256]{3,2,1,0:T(8,128)S(1)} %bitcast.62, f32[1,16,64,256]{3,2,1,0:T(8,128)S(1)} %bitcast.66, ...), kind=kLoop, calls=%fused_computation | loop fusion | flops 12282816 | bytes 12282816 | tf_op jit(solution)/shard_map/concatenate | solution.py:72
  100.2 4.5 %fusion = (f32[26,74,266]{2,1,0:T(8,128)S(1)}, f32[26,74,266]{2,1,0:T(8,128)S(1)}, f32[26,74,266]{2,1,0:T(8,128)S(1)}) fusion(f32[3,26,74,266]{3,2,1,0:T(8,128)} %pad_maximum_fusion), kind=kLoop, calls=%fused_computation.3 | loop fusion | flops 511784 | bytes 12282816 | tf_op jit(solution)/shard_map/add | solution.py:121
  104.7 7.2 %fusion.6 = f32[24,72,264]{2,1,0:T(8,128)S(1)} fusion(f32[26,74,266]{2,1,0:T(8,128)S(1)} %get-tuple-element.20, f32[26,74,266]{2,1,0:T(8,128)S(1)} %get-tuple-element.19, f32[26,74,266]{2,1,0:T(8,128)S(1)} %get-tuple-element.18, pred[26,74,266]{2,1,0:T(8,128)(4,1)S(1)} %copy-done.4), kind=kLoop, calls=%fused_computation.12 | loop fusion | flops 5474304 | bytes 18703872 | tf_op jit(solution)/shard_map/jit(_where)/select_n | solution.py:102
  111.9 6.8 %fusion.12 = f32[22,70,262]{2,1,0:T(8,128)S(1)} fusion(f32[24,72,264]{2,1,0:T(8,128)S(1)} %fusion.6, f32[26,74,266]{2,1,0:T(8,128)S(1)} %get-tuple-element.19, f32[26,74,266]{2,1,0:T(8,128)S(1)} %get-tuple-element.18, pred[26,74,266]{2,1,0:T(8,128)(4,1)S(1)} %copy-done.4), kind=kLoop, calls=%fused_computation.23 | loop fusion | flops 4841760 | bytes 16542680 | tf_op jit(solution)/shard_map/jit(_where)/select_n | solution.py:102
  118.7 6.0 %fusion.18 = f32[20,68,260]{2,1,0:T(8,128)S(1)} fusion(f32[22,70,262]{2,1,0:T(8,128)S(1)} %fusion.12, f32[26,74,266]{2,1,0:T(8,128)S(1)} %get-tuple-element.19, f32[26,74,266]{2,1,0:T(8,128)S(1)} %get-tuple-element.18, pred[26,74,266]{2,1,0:T(8,128)(4,1)S(1)} %copy-done.4), kind=kLoop, calls=%fused_computation.34 | loop fusion | flops 4243200 | bytes 14497600 | tf_op jit(solution)/shard_map/jit(_where)/select_n | solution.py:102
  124.7 5.4 %fusion.24 = f32[18,66,258]{2,1,0:T(8,128)S(1)} fusion(f32[20,68,260]{2,1,0:T(8,128)S(1)} %fusion.18, f32[26,74,266]{2,1,0:T(8,128)S(1)} %get-tuple-element.19, f32[26,74,266]{2,1,0:T(8,128)S(1)} %get-tuple-element.18, pred[26,74,266]{2,1,0:T(8,128)(4,1)S(1)} %copy-done.4), kind=kLoop, calls=%fused_computation.45 | loop fusion | flops 3678048 | bytes 12566664 | tf_op jit(solution)/shard_map/jit(_where)/select_n | solution.py:102
  138.4 3.8 %collective-permute-done.7 = f32[2,4,32,128]{3,2,1,0:T(8,128)S(1)} collective-permute-done((f32[2,4,32,128]{3,2,1,0:T(8,128)S(1)}, f32[2,4,32,128]{3,2,1,0:T(8,128)S(1)}, u32[]{:S(2)}, u32[]{:S(2)}) %collective-permute-start.7) | collective-permute-done | bytes 131104 | tf_op jit(solution)/shard_map/ppermute | solution.py:76
  142.3 6.3 %collective-permute-start.8 = (f32[2,16,4,128]{3,2,1,0:T(4,128)S(1)}, f32[2,16,4,128]{3,2,1,0:T(4,128)S(1)}, u32[]{:S(2)}, u32[]{:S(2)}) collective-permute-start(f32[2,16,4,128]{3,2,1,0:T(4,128)S(1)} %get-tuple-element.31), channel_id=1, source_target_pairs={{0,2},{2,4},{4,6},{6,8},{8,10},{10,12},{12,14},{14,16},{16,18},{18... | collective-permute-start | bytes 196616 | tf_op jit(solution)/shard_map/ppermute | solution.py:74
  158.3 4.9 %collective-permute-done.11 = f32[2,16,40,4]{2,1,3,0:T(8,128)S(1)} collective-permute-done((f32[2,16,40,4]{2,1,3,0:T(8,128)S(1)}, f32[2,16,40,4]{2,1,3,0:T(8,128)S(1)}, u32[]{:S(2)}, u32[]{:S(2)}) %collective-permute-start.11) | collective-permute-done | bytes 20512 | tf_op jit(solution)/shard_map/ppermute | solution.py:76
  175.0 4.1 %collective-permute-done.13 = f32[2,4,16,64]{3,2,1,0:T(8,128)S(1)} collective-permute-done((f32[2,4,16,64]{3,2,1,0:T(8,128)S(1)}, f32[2,4,16,64]{3,2,1,0:T(8,128)S(1)}, u32[]{:S(2)}, u32[]{:S(2)}) %collective-permute-start.13) | collective-permute-done | bytes 32800 | tf_op jit(solution)/shard_map/ppermute | solution.py:76
  179.1 4.4 %collective-permute-start.14 = (f32[2,12,4,64]{3,2,1,0:T(4,128)S(1)}, f32[2,12,4,64]{3,2,1,0:T(4,128)S(1)}, u32[]{:S(2)}, u32[]{:S(2)}) collective-permute-start(f32[2,12,4,64]{3,2,1,0:T(4,128)S(1)} %get-tuple-element.39), channel_id=1, source_target_pairs={{0,2},{2,4},{4,6},{6,8},{8,10},{10,12},{12,14},{14,16},{16,18},{18... | collective-permute-start | bytes 73736 | tf_op jit(solution)/shard_map/ppermute | solution.py:74
  192.4 4.1 %collective-permute-done.16 = f32[2,12,24,4]{3,2,1,0:T(8,128)S(1)} collective-permute-done((f32[2,12,24,4]{3,2,1,0:T(8,128)S(1)}, f32[2,12,24,4]{3,2,1,0:T(8,128)S(1)}, u32[]{:S(2)}, u32[]{:S(2)}) %collective-permute-start.16) | collective-permute-done | bytes 9248 | tf_op jit(solution)/shard_map/ppermute | solution.py:74
  196.5 5.1 %collective-permute-done.17 = f32[2,12,24,4]{3,2,1,0:T(8,128)S(1)} collective-permute-done((f32[2,12,24,4]{3,2,1,0:T(8,128)S(1)}, f32[2,12,24,4]{3,2,1,0:T(8,128)S(1)}, u32[]{:S(2)}, u32[]{:S(2)}) %collective-permute-start.17) | collective-permute-done | bytes 9248 | tf_op jit(solution)/shard_map/ppermute | solution.py:76
  204.3 6.0 %psum.21 = f32[1024]{0:T(1024)S(1)} all-reduce(f32[1024]{0:T(1024)S(1)} %reshape.365), channel_id=1, replica_groups=mesh['gx'=4,'gy'=16,'gz'=2] {'gx'}, use_global_device_ids=true, to_apply=%region_0.1 | all-reduce | flops 1024 | bytes 8192 | tf_op jit(solution)/shard_map/psum | solution.py:141
  210.3 16.6 %psum.22 = f32[1024]{0:T(1024)S(1)} all-reduce(f32[1024]{0:T(1024)S(1)} %psum.21), channel_id=1, replica_groups={{0,1,2,3,4,5,6,7},{8,9,10,11,12,13,14,15},{16,17,18,19,20,21,22,23},{24..., use_global_device_ids=true, to_apply=%region_1.2 | all-reduce | flops 1024 | bytes 8192 | tf_op jit(solution)/shard_map/psum | solution.py:145
  226.9 10.9 %psum.23 = f32[1024]{0:T(1024)S(1)} all-reduce(f32[1024]{0:T(1024)S(1)} %psum.22), channel_id=1, replica_groups={{0,8,16,24},{2,10,18,26},{4,12,20,28},{6,14,22,30},{1,9,17,25},{3,11,19..., use_global_device_ids=true, to_apply=%region_2.3 | all-reduce | flops 1024 | bytes 8192 | tf_op jit(solution)/shard_map/psum | solution.py:147
  (166 shorter events, 85.0 us)
Async XLA Ops:
  0.6 237.2 %copy-start = (f32[64,1024]{1,0:T(8,128)S(1)}, f32[64,1024]{1,0:T(8,128)}, u32[]{:S(2)}) copy-start(f32[64,1024]{1,0:T(8,128)} %param.9) | copy-start | bytes 786436
  3.8 30.1 %copy-start.2 = (f32[16,64,256]{2,1,0:T(8,128)S(1)}, f32[16,64,256]{2,1,0:T(8,128)}, u32[]{:S(2)}) copy-start(f32[16,64,256]{2,1,0:T(8,128)} %param.5) | copy-start | bytes 3145732
  3.8 30.1 %copy-start.3 = (f32[16,64,256]{2,1,0:T(8,128)S(1)}, f32[16,64,256]{2,1,0:T(8,128)}, u32[]{:S(2)}) copy-start(f32[16,64,256]{2,1,0:T(8,128)} %param.6) | copy-start | bytes 3145732
  3.8 25.2 %collective-permute-start = (f32[3,5,64,256]{3,2,1,0:T(8,128)}, f32[3,5,64,256]{3,2,1,0:T(8,128)}, u32[]{:S(2)}, u32[]{:S(2)}) collective-permute-start(f32[3,5,64,256]{3,2,1,0:T(8,128)} %get-tuple-element.25), channel_id=1, source_target_pairs={{0,32},{32,64},{64,96},{1,33},{33,65},{65,97},{2,34},{34,66},{66,9... | collective-permute-start | bytes 2949128 | tf_op jit(solution)/shard_map/ppermute | solution.py:74
  9.2 24.6 %collective-permute-start.1 = (f32[3,5,64,256]{3,2,1,0:T(8,128)}, f32[3,5,64,256]{3,2,1,0:T(8,128)}, u32[]{:S(2)}, u32[]{:S(2)}) collective-permute-start(f32[3,5,64,256]{3,2,1,0:T(8,128)} %get-tuple-element.26), channel_id=1, source_target_pairs={{32,0},{64,32},{96,64},{33,1},{65,33},{97,65},{34,2},{66,34},{98,6... | collective-permute-start | bytes 2949128 | tf_op jit(solution)/shard_map/ppermute | solution.py:76
  10.6 24.4 %copy-start.17 = (s32[256]{0:T(256)}, s32[256]{0:T(256)S(1)}, u32[]{:S(2)}) copy-start(s32[256]{0:T(256)S(1)} %get-tuple-element.49) | copy-start | bytes 3076
  10.6 24.4 %copy-start.19 = (s32[256]{0:T(256)}, s32[256]{0:T(256)S(1)}, u32[]{:S(2)}) copy-start(s32[256]{0:T(256)S(1)} %get-tuple-element.50) | copy-start | bytes 3076
  19.5 24.2 %copy-start.32 = (pred[26]{0:T(512)(128)(4,1)S(1)}, pred[26]{0:T(512)(128)(4,1)}, u32[]{:S(2)}) copy-start(pred[26]{0:T(512)(128)(4,1)} %compare_and_fusion.9) | copy-start | bytes 82
  36.0 11.2 %collective-permute-start.2 = (f32[3,26,5,256]{3,1,2,0:T(8,128)}, f32[3,26,5,256]{3,1,2,0:T(8,128)}, u32[]{:S(2)}, u32[]{:S(2)}) collective-permute-start(f32[3,26,5,256]{3,1,2,0:T(8,128)} %copy.63), channel_id=1, source_target_pairs={{0,2},{2,4},{4,6},{6,8},{8,10},{10,12},{12,14},{14,16},{16,18},{18... | collective-permute-start | bytes 1198088 | tf_op jit(solution)/shard_map/ppermute | solution.py:74
  41.8 10.5 %collective-permute-start.3 = (f32[3,26,5,256]{3,1,2,0:T(8,128)}, f32[3,26,5,256]{3,1,2,0:T(8,128)}, u32[]{:S(2)}, u32[]{:S(2)}) collective-permute-start(f32[3,26,5,256]{3,1,2,0:T(8,128)} %copy.64), channel_id=1, source_target_pairs={{2,0},{4,2},{6,4},{8,6},{10,8},{12,10},{14,12},{16,14},{18,16},{20... | collective-permute-start | bytes 1198088 | tf_op jit(solution)/shard_map/ppermute | solution.py:76
  64.0 11.9 %collective-permute-start.4 = (f32[3,26,74,5]{2,1,3,0:T(8,128)}, f32[3,26,74,5]{2,1,3,0:T(8,128)}, u32[]{:S(2)}, u32[]{:S(2)}) collective-permute-start(f32[3,26,74,5]{2,1,3,0:T(8,128)} %copy.67), channel_id=1, source_target_pairs={{0,1},{2,3},{4,5},{6,7},{8,9},{10,11},{12,13},{14,15},{16,17},{18,... | collective-permute-start | bytes 346328 | tf_op jit(solution)/shard_map/ppermute | solution.py:74
  72.8 8.8 %collective-permute-start.5 = (f32[3,26,74,5]{2,1,3,0:T(8,128)}, f32[3,26,74,5]{2,1,3,0:T(8,128)}, u32[]{:S(2)}, u32[]{:S(2)}) collective-permute-start(f32[3,26,74,5]{2,1,3,0:T(8,128)} %copy.68), channel_id=1, source_target_pairs={{1,0},{3,2},{5,4},{7,6},{9,8},{11,10},{13,12},{15,14},{17,16},{19,... | collective-permute-start | bytes 346328 | tf_op jit(solution)/shard_map/ppermute | solution.py:76
  134.0 4.5 %collective-permute-start.6 = (f32[2,4,32,128]{3,2,1,0:T(8,128)S(1)}, f32[2,4,32,128]{3,2,1,0:T(8,128)S(1)}, u32[]{:S(2)}, u32[]{:S(2)}) collective-permute-start(f32[2,4,32,128]{3,2,1,0:T(8,128)S(1)} %get-tuple-element.37), channel_id=1, source_target_pairs={{0,32},{32,64},{64,96},{1,33},{33,65},{65,97},{2,34},{34,66},{66,9... | collective-permute-start | bytes 393224 | tf_op jit(solution)/shard_map/ppermute | solution.py:74
  136.5 5.7 %collective-permute-start.7 = (f32[2,4,32,128]{3,2,1,0:T(8,128)S(1)}, f32[2,4,32,128]{3,2,1,0:T(8,128)S(1)}, u32[]{:S(2)}, u32[]{:S(2)}) collective-permute-start(f32[2,4,32,128]{3,2,1,0:T(8,128)S(1)} %get-tuple-element.38), channel_id=1, source_target_pairs={{32,0},{64,32},{96,64},{33,1},{65,33},{97,65},{34,2},{66,34},{98,6... | collective-permute-start | bytes 393224 | tf_op jit(solution)/shard_map/ppermute | solution.py:76
  142.3 8.5 %collective-permute-start.8 = (f32[2,16,4,128]{3,2,1,0:T(4,128)S(1)}, f32[2,16,4,128]{3,2,1,0:T(4,128)S(1)}, u32[]{:S(2)}, u32[]{:S(2)}) collective-permute-start(f32[2,16,4,128]{3,2,1,0:T(4,128)S(1)} %get-tuple-element.31), channel_id=1, source_target_pairs={{0,2},{2,4},{4,6},{6,8},{8,10},{10,12},{12,14},{14,16},{16,18},{18... | collective-permute-start | bytes 196616 | tf_op jit(solution)/shard_map/ppermute | solution.py:74
  148.5 5.6 %collective-permute-start.9 = (f32[2,16,4,128]{3,2,1,0:T(4,128)S(1)}, f32[2,16,4,128]{3,2,1,0:T(4,128)S(1)}, u32[]{:S(2)}, u32[]{:S(2)}) collective-permute-start(f32[2,16,4,128]{3,2,1,0:T(4,128)S(1)} %get-tuple-element.32), channel_id=1, source_target_pairs={{2,0},{4,2},{6,4},{8,6},{10,8},{12,10},{14,12},{16,14},{18,16},{20... | collective-permute-start | bytes 196616 | tf_op jit(solution)/shard_map/ppermute | solution.py:76
  154.7 3.3 %collective-permute-start.10 = (f32[2,16,40,4]{2,1,3,0:T(8,128)S(1)}, f32[2,16,40,4]{2,1,3,0:T(8,128)S(1)}, u32[]{:S(2)}, u32[]{:S(2)}) collective-permute-start(f32[2,16,40,4]{2,1,3,0:T(8,128)S(1)} %copy.71), channel_id=1, source_target_pairs={{0,1},{2,3},{4,5},{6,7},{8,9},{10,11},{12,13},{14,15},{16,17},{18,... | collective-permute-start | bytes 61448 | tf_op jit(solution)/shard_map/ppermute | solution.py:74
  156.7 6.5 %collective-permute-start.11 = (f32[2,16,40,4]{2,1,3,0:T(8,128)S(1)}, f32[2,16,40,4]{2,1,3,0:T(8,128)S(1)}, u32[]{:S(2)}, u32[]{:S(2)}) collective-permute-start(f32[2,16,40,4]{2,1,3,0:T(8,128)S(1)} %copy.72), channel_id=1, source_target_pairs={{1,0},{3,2},{5,4},{7,6},{9,8},{11,10},{13,12},{15,14},{17,16},{19,... | collective-permute-start | bytes 61448 | tf_op jit(solution)/shard_map/ppermute | solution.py:76
  170.3 4.6 %collective-permute-start.12 = (f32[2,4,16,64]{3,2,1,0:T(8,128)S(1)}, f32[2,4,16,64]{3,2,1,0:T(8,128)S(1)}, u32[]{:S(2)}, u32[]{:S(2)}) collective-permute-start(f32[2,4,16,64]{3,2,1,0:T(8,128)S(1)} %pad_maximum_fusion.19), channel_id=1, source_target_pairs={{0,32},{32,64},{64,96},{1,33},{33,65},{65,97},{2,34},{34,66},{66,9... | collective-permute-start | bytes 98312 | tf_op jit(solution)/shard_map/ppermute | solution.py:74
  173.6 5.5 %collective-permute-start.13 = (f32[2,4,16,64]{3,2,1,0:T(8,128)S(1)}, f32[2,4,16,64]{3,2,1,0:T(8,128)S(1)}, u32[]{:S(2)}, u32[]{:S(2)}) collective-permute-start(f32[2,4,16,64]{3,2,1,0:T(8,128)S(1)} %pad_maximum_fusion.19), channel_id=1, source_target_pairs={{32,0},{64,32},{96,64},{33,1},{65,33},{97,65},{34,2},{66,34},{98,6... | collective-permute-start | bytes 98312 | tf_op jit(solution)/shard_map/ppermute | solution.py:76
  179.1 6.3 %collective-permute-start.14 = (f32[2,12,4,64]{3,2,1,0:T(4,128)S(1)}, f32[2,12,4,64]{3,2,1,0:T(4,128)S(1)}, u32[]{:S(2)}, u32[]{:S(2)}) collective-permute-start(f32[2,12,4,64]{3,2,1,0:T(4,128)S(1)} %get-tuple-element.39), channel_id=1, source_target_pairs={{0,2},{2,4},{4,6},{6,8},{8,10},{10,12},{12,14},{14,16},{16,18},{18... | collective-permute-start | bytes 73736 | tf_op jit(solution)/shard_map/ppermute | solution.py:74
  183.5 5.4 %collective-permute-start.15 = (f32[2,12,4,64]{3,2,1,0:T(4,128)S(1)}, f32[2,12,4,64]{3,2,1,0:T(4,128)S(1)}, u32[]{:S(2)}, u32[]{:S(2)}) collective-permute-start(f32[2,12,4,64]{3,2,1,0:T(4,128)S(1)} %get-tuple-element.40), channel_id=1, source_target_pairs={{2,0},{4,2},{6,4},{8,6},{10,8},{12,10},{14,12},{16,14},{18,16},{20... | collective-permute-start | bytes 73736 | tf_op jit(solution)/shard_map/ppermute | solution.py:76
  189.1 7.4 %collective-permute-start.16 = (f32[2,12,24,4]{3,2,1,0:T(8,128)S(1)}, f32[2,12,24,4]{3,2,1,0:T(8,128)S(1)}, u32[]{:S(2)}, u32[]{:S(2)}) collective-permute-start(f32[2,12,24,4]{3,2,1,0:T(8,128)S(1)} %get-tuple-element.35), channel_id=1, source_target_pairs={{0,1},{2,3},{4,5},{6,7},{8,9},{10,11},{12,13},{14,15},{16,17},{18,... | collective-permute-start | bytes 27656 | tf_op jit(solution)/shard_map/ppermute | solution.py:74
  191.0 10.6 %collective-permute-start.17 = (f32[2,12,24,4]{3,2,1,0:T(8,128)S(1)}, f32[2,12,24,4]{3,2,1,0:T(8,128)S(1)}, u32[]{:S(2)}, u32[]{:S(2)}) collective-permute-start(f32[2,12,24,4]{3,2,1,0:T(8,128)S(1)} %get-tuple-element.36), channel_id=1, source_target_pairs={{1,0},{3,2},{5,4},{7,6},{9,8},{11,10},{13,12},{15,14},{17,16},{19,... | collective-permute-start | bytes 27656 | tf_op jit(solution)/shard_map/ppermute | solution.py:76
  (27 other events, 179.2 us)

commit v7 on v5

--- a/solution.py
+++ b/solution.py
@@ -64,8 +64,8 @@
     return flat.reshape(extent_a // 2, extent_b // 2, extent_c // 2) * 0.125
 
 
-def exchange(stack, width):
-    for axis, dim in (("gx", 1), ("gz", 3), ("gy", 2)):
+def exchange(stack, width, order=(("gx", 1), ("gy", 2), ("gz", 3))):
+    for axis, dim in order:
         count = lax.axis_size(axis)
         head = lax.slice_in_dim(stack, 0, width, axis=dim)
         tail = lax.slice_in_dim(stack, stack.shape[dim] - width, stack.shape[dim], axis=dim)
@@ -103,9 +103,9 @@
     return current
 
 
-def coarser_level(source, damp):
+def coarser_level(source, damp, order):
     width = SWEEPS
-    wide = exchange(jnp.stack([source, damp]), width)
+    wide = exchange(jnp.stack([source, damp]), width, order)
     wide_source = wide[0]
     wide_diag = 6.0 + wide[1]
     mask = inside(source.shape, width)
@@ -125,10 +125,10 @@
     fine_defect = defect(current, right_side, 6.0 + damping)
     middle_damp = 4.0 * shrink(damping)
     middle_source = 4.0 * shrink(fine_defect)
-    middle, middle_defect = coarser_level(middle_source, middle_damp)
+    middle, middle_defect = coarser_level(middle_source, middle_damp, (("gx", 1), ("gy", 2), ("gz", 3)))
     coarse_damp = 4.0 * shrink(middle_damp)
     coarse_source = 4.0 * shrink(middle_defect)
-    coarse, coarse_defect = coarser_level(coarse_source, coarse_damp)
+    coarse, coarse_defect = coarser_level(coarse_source, coarse_damp, (("gz", 3), ("gy", 2), ("gx", 1)))
     cells = coarse_defect.size
     digits = DIGITS
     owner = group_map.reshape(cells, 1)

time: 242 us -> 234 us (0.967)
  waiting for transfers between devices: 62.9 us -> 45.6 us
  blocking collectives: 27.3 us -> 31.3 us
  other arithmetic: 66.4 us -> 69.2 us
    ppermute x9, waiting for transfers between devices: 27.5 us -> 10.7 us  [exchange(): lax.ppermute(tail, axis, [(i, i + 1) for i in range(count - 1)])]
    psum x2, blocking collectives: 15.7 us -> 19.7 us  [shards(): summed = lax.psum(summed, 'gy', axis_index_groups=groups)]
    concatenate x6, other arithmetic: 15.7 us -> 18.7 us  [exchange(): jnp.concatenate([lax.ppermute(tail, axis, [(i, i + 1) for i in range(coun...]
    ppermute x2 -> x3, local copies, waits for them, and re-layouts: 4.74 us -> 4.96 us  [exchange(): lax.ppermute(tail, axis, [(i, i + 1) for i in range(count - 1)])]
    ppermute x2 -> x3, local copies, waits for them, and re-layouts: 4.75 us -> 4.96 us  [exchange(): lax.ppermute(head, axis, [(i + 1, i) for i in range(count - 1)])]
  transfers between devices with their start and end apart: 18 -> 18, of which waited for: 13 -> 12; matrix products, arithmetic and copies ran while one was open for 9% -> 10% of each run, Pallas kernels for 0% -> 0%
where the time goes in v7:
time: 234 us; the launch traced here: 232 us
  other arithmetic  69.2 us (30%)
  starting transfers between devices  49.2 us (21%)
  waiting for transfers between devices  45.6 us (19%)
  blocking collectives  31.3 us (13%)
  local copies, waits for them, and re-layouts  25.9 us (11%)
  matrix products  8.85 us (4%)
    ppermute x9, starting transfers between devices, exchange(): lax.ppermute(tail, axis, [(i, i + 1) for i in range(count - 1)])  35.3 us
    ppermute x9, waiting for transfers between devices, exchange(): lax.ppermute(head, axis, [(i + 1, i) for i in range(count - 1)])  35 us
    select_n x10, other arithmetic, smooth_wide(): current = jnp.where(crop(mask, step), current, 0.0)  29.9 us
    psum x2, blocking collectives, shards(): summed = lax.psum(summed, 'gy', axis_index_groups=groups)  19.7 us
    concatenate x6, other arithmetic, exchange(): jnp.concatenate([lax.ppermute(tail, axis, [(i, i + 1) for i in range(coun...  18.7 us
    ppermute x9, starting transfers between devices, exchange(): lax.ppermute(head, axis, [(i + 1, i) for i in range(count - 1)])  13.9 us
    ppermute x9, waiting for transfers between devices, exchange(): lax.ppermute(tail, axis, [(i, i + 1) for i in range(count - 1)])  10.7 us
    slice x5, local copies, waits for them, and re-layouts, exchange(): lax.slice_in_dim(stack, stack.shape[dim] - width, stack.shape[dim], axis=...  8.68 us
  transfers between devices with their start and end apart: 18, of which 12 were waited for; matrix products, arithmetic and copies ran while one was open for 10% of the time, Pallas kernels for 0%

profile of v7, /device:TPU:1, one launch (start us, length us, event | category | flops | bytes accessed | tf_op | source)
XLA Modules:
  0.0 231.7 jit_solution(4634110252556434756)
XLA Ops:
  3.7 5.5 %collective-permute-start = (f32[3,5,64,256]{3,2,1,0:T(8,128)}, f32[3,5,64,256]{3,2,1,0:T(8,128)}, u32[]{:S(2)}, u32[]{:S(2)}) collective-permute-start(f32[3,5,64,256]{3,2,1,0:T(8,128)} %get-tuple-element.25), channel_id=1, source_target_pairs={{0,32},{32,64},{64,96},{1,33},{33,65},{65,97},{2,34},{34,66},{66,9... | collective-permute-start | bytes 2949128 | tf_op jit(solution)/shard_map/ppermute | solution.py:74
  19.1 9.8 %collective-permute-done = f32[3,5,64,256]{3,2,1,0:T(8,128)} collective-permute-done((f32[3,5,64,256]{3,2,1,0:T(8,128)}, f32[3,5,64,256]{3,2,1,0:T(8,128)}, u32[]{:S(2)}, u32[]{:S(2)}) %collective-permute-start) | collective-permute-done | bytes 983072 | tf_op jit(solution)/shard_map/ppermute | solution.py:74
  29.0 4.8 %collective-permute-done.1 = f32[3,5,64,256]{3,2,1,0:T(8,128)} collective-permute-done((f32[3,5,64,256]{3,2,1,0:T(8,128)}, f32[3,5,64,256]{3,2,1,0:T(8,128)}, u32[]{:S(2)}, u32[]{:S(2)}) %collective-permute-start.1) | collective-permute-done | bytes 983072 | tf_op jit(solution)/shard_map/ppermute | solution.py:76
  36.0 4.9 %collective-permute-start.2 = (f32[3,26,5,256]{3,1,2,0:T(8,128)}, f32[3,26,5,256]{3,1,2,0:T(8,128)}, u32[]{:S(2)}, u32[]{:S(2)}) collective-permute-start(f32[3,26,5,256]{3,1,2,0:T(8,128)} %copy.63), channel_id=1, source_target_pairs={{0,2},{2,4},{4,6},{6,8},{8,10},{10,12},{12,14},{14,16},{16,18},{18... | collective-permute-start | bytes 1198088 | tf_op jit(solution)/shard_map/ppermute | solution.py:74
  48.5 3.8 %collective-permute-done.3 = f32[3,26,5,256]{3,1,2,0:T(8,128)} collective-permute-done((f32[3,26,5,256]{3,1,2,0:T(8,128)}, f32[3,26,5,256]{3,1,2,0:T(8,128)}, u32[]{:S(2)}, u32[]{:S(2)}) %collective-permute-start.3) | collective-permute-done | bytes 399392 | tf_op jit(solution)/shard_map/ppermute | solution.py:76
  56.7 3.6 %fusion.113 = (f32[3,26,74,5]{3,2,1,0:T(8,128)}, f32[3,26,74,5]{3,2,1,0:T(8,128)}) fusion(f32[3,26,74,256]{3,2,1,0:T(8,128)S(1)} %pad_maximum_fusion.1), kind=kLoop, calls=%fused_computation.267 | loop fusion | bytes 461760 | tf_op jit(solution)/shard_map/slice | solution.py:71
  60.4 3.6 %copy.67 = f32[3,26,74,5]{2,1,3,0:T(8,128)} copy(f32[3,26,74,5]{3,2,1,0:T(8,128)} %get-tuple-element.21) | data formatting | bytes 230880 | tf_op jit(solution)/shard_map/slice | solution.py:71
  64.0 5.2 %collective-permute-start.4 = (f32[3,26,74,5]{2,1,3,0:T(8,128)}, f32[3,26,74,5]{2,1,3,0:T(8,128)}, u32[]{:S(2)}, u32[]{:S(2)}) collective-permute-start(f32[3,26,74,5]{2,1,3,0:T(8,128)} %copy.67), channel_id=1, source_target_pairs={{0,1},{2,3},{4,5},{6,7},{8,9},{10,11},{12,13},{14,15},{16,17},{18,... | collective-permute-start | bytes 346328 | tf_op jit(solution)/shard_map/ppermute | solution.py:74
  84.9 15.3 %pad_maximum_fusion = f32[3,26,74,266]{3,2,1,0:T(8,128)} fusion(f32[3,26,74,5]{3,2,1,0:T(8,128)} %copy.70, f32[3,26,5,256]{3,2,1,0:T(8,128)} %copy-done.6, f32[3,5,64,256]{3,2,1,0:T(8,128)} %collective-permute-done.1, f32[1,16,64,256]{3,2,1,0:T(8,128)S(1)} %bitcast.58, f32[1,16,64,256]{3,2,1,0:T(8,128)S(1)} %bitcast.62, f32[1,16,64,256]{3,2,1,0:T(8,128)S(1)} %bitcast.66, ...), kind=kLoop, calls=%fused_computation | loop fusion | flops 12282816 | bytes 12282816 | tf_op jit(solution)/shard_map/concatenate | solution.py:72
  100.2 4.5 %fusion = (f32[26,74,266]{2,1,0:T(8,128)S(1)}, f32[26,74,266]{2,1,0:T(8,128)S(1)}, f32[26,74,266]{2,1,0:T(8,128)S(1)}) fusion(f32[3,26,74,266]{3,2,1,0:T(8,128)} %pad_maximum_fusion), kind=kLoop, calls=%fused_computation.3 | loop fusion | flops 511784 | bytes 12282816 | tf_op jit(solution)/shard_map/add | solution.py:121
  104.7 7.2 %fusion.6 = f32[24,72,264]{2,1,0:T(8,128)S(1)} fusion(f32[26,74,266]{2,1,0:T(8,128)S(1)} %get-tuple-element.20, f32[26,74,266]{2,1,0:T(8,128)S(1)} %get-tuple-element.19, f32[26,74,266]{2,1,0:T(8,128)S(1)} %get-tuple-element.18, pred[26,74,266]{2,1,0:T(8,128)(4,1)S(1)} %copy-done.4), kind=kLoop, calls=%fused_computation.12 | loop fusion | flops 5474304 | bytes 18703872 | tf_op jit(solution)/shard_map/jit(_where)/select_n | solution.py:102
  111.9 6.8 %fusion.12 = f32[22,70,262]{2,1,0:T(8,128)S(1)} fusion(f32[24,72,264]{2,1,0:T(8,128)S(1)} %fusion.6, f32[26,74,266]{2,1,0:T(8,128)S(1)} %get-tuple-element.19, f32[26,74,266]{2,1,0:T(8,128)S(1)} %get-tuple-element.18, pred[26,74,266]{2,1,0:T(8,128)(4,1)S(1)} %copy-done.4), kind=kLoop, calls=%fused_computation.23 | loop fusion | flops 4841760 | bytes 16542680 | tf_op jit(solution)/shard_map/jit(_where)/select_n | solution.py:102
  118.7 6.0 %fusion.18 = f32[20,68,260]{2,1,0:T(8,128)S(1)} fusion(f32[22,70,262]{2,1,0:T(8,128)S(1)} %fusion.12, f32[26,74,266]{2,1,0:T(8,128)S(1)} %get-tuple-element.19, f32[26,74,266]{2,1,0:T(8,128)S(1)} %get-tuple-element.18, pred[26,74,266]{2,1,0:T(8,128)(4,1)S(1)} %copy-done.4), kind=kLoop, calls=%fused_computation.34 | loop fusion | flops 4243200 | bytes 14497600 | tf_op jit(solution)/shard_map/jit(_where)/select_n | solution.py:102
  124.7 5.4 %fusion.24 = f32[18,66,258]{2,1,0:T(8,128)S(1)} fusion(f32[20,68,260]{2,1,0:T(8,128)S(1)} %fusion.18, f32[26,74,266]{2,1,0:T(8,128)S(1)} %get-tuple-element.19, f32[26,74,266]{2,1,0:T(8,128)S(1)} %get-tuple-element.18, pred[26,74,266]{2,1,0:T(8,128)(4,1)S(1)} %copy-done.4), kind=kLoop, calls=%fused_computation.45 | loop fusion | flops 3678048 | bytes 12566664 | tf_op jit(solution)/shard_map/jit(_where)/select_n | solution.py:102
  138.4 3.8 %collective-permute-done.7 = f32[2,4,32,128]{3,2,1,0:T(8,128)S(1)} collective-permute-done((f32[2,4,32,128]{3,2,1,0:T(8,128)S(1)}, f32[2,4,32,128]{3,2,1,0:T(8,128)S(1)}, u32[]{:S(2)}, u32[]{:S(2)}) %collective-permute-start.7) | collective-permute-done | bytes 131104 | tf_op jit(solution)/shard_map/ppermute | solution.py:76
  142.3 6.3 %collective-permute-start.8 = (f32[2,16,4,128]{3,2,1,0:T(4,128)S(1)}, f32[2,16,4,128]{3,2,1,0:T(4,128)S(1)}, u32[]{:S(2)}, u32[]{:S(2)}) collective-permute-start(f32[2,16,4,128]{3,2,1,0:T(4,128)S(1)} %get-tuple-element.31), channel_id=1, source_target_pairs={{0,2},{2,4},{4,6},{6,8},{8,10},{10,12},{12,14},{14,16},{16,18},{18... | collective-permute-start | bytes 196616 | tf_op jit(solution)/shard_map/ppermute | solution.py:74
  158.3 4.9 %collective-permute-done.11 = f32[2,16,40,4]{2,1,3,0:T(8,128)S(1)} collective-permute-done((f32[2,16,40,4]{2,1,3,0:T(8,128)S(1)}, f32[2,16,40,4]{2,1,3,0:T(8,128)S(1)}, u32[]{:S(2)}, u32[]{:S(2)}) %collective-permute-start.11) | collective-permute-done | bytes 20512 | tf_op jit(solution)/shard_map/ppermute | solution.py:76
  173.3 5.3 %collective-permute-done.13 = f32[2,4,16,4]{3,2,1,0:T(8,128)S(1)} collective-permute-done((f32[2,4,16,4]{3,2,1,0:T(8,128)S(1)}, f32[2,4,16,4]{3,2,1,0:T(8,128)S(1)}, u32[]{:S(2)}, u32[]{:S(2)}) %collective-permute-start.13) | collective-permute-done | bytes 2080 | tf_op jit(solution)/shard_map/ppermute | solution.py:76
  178.7 4.4 %collective-permute-start.14 = (f32[2,4,4,72]{3,2,1,0:T(4,128)S(1)}, f32[2,4,4,72]{3,2,1,0:T(4,128)S(1)}, u32[]{:S(2)}, u32[]{:S(2)}) collective-permute-start(f32[2,4,4,72]{3,2,1,0:T(4,128)S(1)} %get-tuple-element.37), channel_id=1, source_target_pairs={{0,2},{2,4},{4,6},{6,8},{8,10},{10,12},{12,14},{14,16},{16,18},{18... | collective-permute-start | bytes 27656 | tf_op jit(solution)/shard_map/ppermute | solution.py:74
  193.2 3.7 %collective-permute-done.17 = f32[2,4,24,72]{3,2,1,0:T(8,128)S(1)} collective-permute-done((f32[2,4,24,72]{3,2,1,0:T(8,128)S(1)}, f32[2,4,24,72]{3,2,1,0:T(8,128)S(1)}, u32[]{:S(2)}, u32[]{:S(2)}) %collective-permute-start.17) | collective-permute-done | bytes 55328 | tf_op jit(solution)/shard_map/ppermute | solution.py:76
  199.5 5.5 %psum.28 = f32[1024]{0:T(1024)S(1)} all-reduce(f32[1024]{0:T(1024)S(1)} %reshape.365), channel_id=1, replica_groups=mesh['gx'=4,'gy'=16,'gz'=2] {'gz'}, use_global_device_ids=true, to_apply=%region_0.1 | all-reduce | flops 1024 | bytes 8192 | tf_op jit(solution)/shard_map/psum | solution.py:141
  205.0 6.1 %psum.29 = f32[1024]{0:T(1024)S(1)} all-reduce(f32[1024]{0:T(1024)S(1)} %psum.28), channel_id=1, replica_groups=mesh['gx'=4,'gy'=16,'gz'=2] {'gx'}, use_global_device_ids=true, to_apply=%region_1.2 | all-reduce | flops 1024 | bytes 8192 | tf_op jit(solution)/shard_map/psum | solution.py:142
  211.1 9.5 %psum.30 = f32[1024]{0:T(1024)S(1)} all-reduce(f32[1024]{0:T(1024)S(1)} %psum.29), channel_id=1, replica_groups={{0,2,4,6},{8,10,12,14},{16,18,20,22},{24,26,28,30},{1,3,5,7},{9,11,13,1..., use_global_device_ids=true, to_apply=%region_2.3 | all-reduce | flops 1024 | bytes 8192 | tf_op jit(solution)/shard_map/psum | solution.py:150
  220.6 10.2 %psum.31 = f32[1024]{0:T(1024)S(1)} all-reduce(f32[1024]{0:T(1024)S(1)} %psum.30), channel_id=1, replica_groups={{0,8,16,24},{2,10,18,26},{4,12,20,28},{6,14,22,30},{1,9,17,25},{3,11,19..., use_global_device_ids=true, to_apply=%region_3.4 | all-reduce | flops 1024 | bytes 8192 | tf_op jit(solution)/shard_map/psum | solution.py:150
  (166 shorter events, 84.1 us)
Async XLA Ops:
  0.6 230.2 %copy-start = (f32[64,1024]{1,0:T(8,128)S(1)}, f32[64,1024]{1,0:T(8,128)}, u32[]{:S(2)}) copy-start(f32[64,1024]{1,0:T(8,128)} %param.9) | copy-start | bytes 786436
  3.7 30.1 %copy-start.2 = (f32[16,64,256]{2,1,0:T(8,128)S(1)}, f32[16,64,256]{2,1,0:T(8,128)}, u32[]{:S(2)}) copy-start(f32[16,64,256]{2,1,0:T(8,128)} %param.5) | copy-start | bytes 3145732
  3.7 30.1 %copy-start.3 = (f32[16,64,256]{2,1,0:T(8,128)S(1)}, f32[16,64,256]{2,1,0:T(8,128)}, u32[]{:S(2)}) copy-start(f32[16,64,256]{2,1,0:T(8,128)} %param.6) | copy-start | bytes 3145732
  3.7 25.2 %collective-permute-start = (f32[3,5,64,256]{3,2,1,0:T(8,128)}, f32[3,5,64,256]{3,2,1,0:T(8,128)}, u32[]{:S(2)}, u32[]{:S(2)}) collective-permute-start(f32[3,5,64,256]{3,2,1,0:T(8,128)} %get-tuple-element.25), channel_id=1, source_target_pairs={{0,32},{32,64},{64,96},{1,33},{33,65},{65,97},{2,34},{34,66},{66,9... | collective-permute-start | bytes 2949128 | tf_op jit(solution)/shard_map/ppermute | solution.py:74
  9.2 24.6 %collective-permute-start.1 = (f32[3,5,64,256]{3,2,1,0:T(8,128)}, f32[3,5,64,256]{3,2,1,0:T(8,128)}, u32[]{:S(2)}, u32[]{:S(2)}) collective-permute-start(f32[3,5,64,256]{3,2,1,0:T(8,128)} %get-tuple-element.26), channel_id=1, source_target_pairs={{32,0},{64,32},{96,64},{33,1},{65,33},{97,65},{34,2},{66,34},{98,6... | collective-permute-start | bytes 2949128 | tf_op jit(solution)/shard_map/ppermute | solution.py:76
  10.6 24.4 %copy-start.17 = (s32[256]{0:T(256)}, s32[256]{0:T(256)S(1)}, u32[]{:S(2)}) copy-start(s32[256]{0:T(256)S(1)} %get-tuple-element.49) | copy-start | bytes 3076
  19.1 24.6 %copy-start.31 = (pred[74]{0:T(512)(128)(4,1)S(1)}, pred[74]{0:T(512)(128)(4,1)}, u32[]{:S(2)}) copy-start(pred[74]{0:T(512)(128)(4,1)} %compare_and_fusion.8) | copy-start | bytes 226
  19.1 24.6 %copy-start.32 = (pred[26]{0:T(512)(128)(4,1)S(1)}, pred[26]{0:T(512)(128)(4,1)}, u32[]{:S(2)}) copy-start(pred[26]{0:T(512)(128)(4,1)} %compare_and_fusion.9) | copy-start | bytes 82
  36.0 11.2 %collective-permute-start.2 = (f32[3,26,5,256]{3,1,2,0:T(8,128)}, f32[3,26,5,256]{3,1,2,0:T(8,128)}, u32[]{:S(2)}, u32[]{:S(2)}) collective-permute-start(f32[3,26,5,256]{3,1,2,0:T(8,128)} %copy.63), channel_id=1, source_target_pairs={{0,2},{2,4},{4,6},{6,8},{8,10},{10,12},{12,14},{14,16},{16,18},{18... | collective-permute-start | bytes 1198088 | tf_op jit(solution)/shard_map/ppermute | solution.py:74
  41.8 10.5 %collective-permute-start.3 = (f32[3,26,5,256]{3,1,2,0:T(8,128)}, f32[3,26,5,256]{3,1,2,0:T(8,128)}, u32[]{:S(2)}, u32[]{:S(2)}) collective-permute-start(f32[3,26,5,256]{3,1,2,0:T(8,128)} %copy.64), channel_id=1, source_target_pairs={{2,0},{4,2},{6,4},{8,6},{10,8},{12,10},{14,12},{16,14},{18,16},{20... | collective-permute-start | bytes 1198088 | tf_op jit(solution)/shard_map/ppermute | solution.py:76
  64.0 11.9 %collective-permute-start.4 = (f32[3,26,74,5]{2,1,3,0:T(8,128)}, f32[3,26,74,5]{2,1,3,0:T(8,128)}, u32[]{:S(2)}, u32[]{:S(2)}) collective-permute-start(f32[3,26,74,5]{2,1,3,0:T(8,128)} %copy.67), channel_id=1, source_target_pairs={{0,1},{2,3},{4,5},{6,7},{8,9},{10,11},{12,13},{14,15},{16,17},{18,... | collective-permute-start | bytes 346328 | tf_op jit(solution)/shard_map/ppermute | solution.py:74
  72.8 8.8 %collective-permute-start.5 = (f32[3,26,74,5]{2,1,3,0:T(8,128)}, f32[3,26,74,5]{2,1,3,0:T(8,128)}, u32[]{:S(2)}, u32[]{:S(2)}) collective-permute-start(f32[3,26,74,5]{2,1,3,0:T(8,128)} %copy.68), channel_id=1, source_target_pairs={{1,0},{3,2},{5,4},{7,6},{9,8},{11,10},{13,12},{15,14},{17,16},{19,... | collective-permute-start | bytes 346328 | tf_op jit(solution)/shard_map/ppermute | solution.py:76
  134.0 4.5 %collective-permute-start.6 = (f32[2,4,32,128]{3,2,1,0:T(8,128)S(1)}, f32[2,4,32,128]{3,2,1,0:T(8,128)S(1)}, u32[]{:S(2)}, u32[]{:S(2)}) collective-permute-start(f32[2,4,32,128]{3,2,1,0:T(8,128)S(1)} %get-tuple-element.35), channel_id=1, source_target_pairs={{0,32},{32,64},{64,96},{1,33},{33,65},{65,97},{2,34},{34,66},{66,9... | collective-permute-start | bytes 393224 | tf_op jit(solution)/shard_map/ppermute | solution.py:74
  136.5 5.7 %collective-permute-start.7 = (f32[2,4,32,128]{3,2,1,0:T(8,128)S(1)}, f32[2,4,32,128]{3,2,1,0:T(8,128)S(1)}, u32[]{:S(2)}, u32[]{:S(2)}) collective-permute-start(f32[2,4,32,128]{3,2,1,0:T(8,128)S(1)} %get-tuple-element.36), channel_id=1, source_target_pairs={{32,0},{64,32},{96,64},{33,1},{65,33},{97,65},{34,2},{66,34},{98,6... | collective-permute-start | bytes 393224 | tf_op jit(solution)/shard_map/ppermute | solution.py:76
  142.3 8.5 %collective-permute-start.8 = (f32[2,16,4,128]{3,2,1,0:T(4,128)S(1)}, f32[2,16,4,128]{3,2,1,0:T(4,128)S(1)}, u32[]{:S(2)}, u32[]{:S(2)}) collective-permute-start(f32[2,16,4,128]{3,2,1,0:T(4,128)S(1)} %get-tuple-element.31), channel_id=1, source_target_pairs={{0,2},{2,4},{4,6},{6,8},{8,10},{10,12},{12,14},{14,16},{16,18},{18... | collective-permute-start | bytes 196616 | tf_op jit(solution)/shard_map/ppermute | solution.py:74
  148.5 5.6 %collective-permute-start.9 = (f32[2,16,4,128]{3,2,1,0:T(4,128)S(1)}, f32[2,16,4,128]{3,2,1,0:T(4,128)S(1)}, u32[]{:S(2)}, u32[]{:S(2)}) collective-permute-start(f32[2,16,4,128]{3,2,1,0:T(4,128)S(1)} %get-tuple-element.32), channel_id=1, source_target_pairs={{2,0},{4,2},{6,4},{8,6},{10,8},{12,10},{14,12},{16,14},{18,16},{20... | collective-permute-start | bytes 196616 | tf_op jit(solution)/shard_map/ppermute | solution.py:76
  154.7 3.2 %collective-permute-start.10 = (f32[2,16,40,4]{2,1,3,0:T(8,128)S(1)}, f32[2,16,40,4]{2,1,3,0:T(8,128)S(1)}, u32[]{:S(2)}, u32[]{:S(2)}) collective-permute-start(f32[2,16,40,4]{2,1,3,0:T(8,128)S(1)} %copy.71), channel_id=1, source_target_pairs={{0,1},{2,3},{4,5},{6,7},{8,9},{10,11},{12,13},{14,15},{16,17},{18,... | collective-permute-start | bytes 61448 | tf_op jit(solution)/shard_map/ppermute | solution.py:74
  156.6 6.5 %collective-permute-start.11 = (f32[2,16,40,4]{2,1,3,0:T(8,128)S(1)}, f32[2,16,40,4]{2,1,3,0:T(8,128)S(1)}, u32[]{:S(2)}, u32[]{:S(2)}) collective-permute-start(f32[2,16,40,4]{2,1,3,0:T(8,128)S(1)} %copy.72), channel_id=1, source_target_pairs={{1,0},{3,2},{5,4},{7,6},{9,8},{11,10},{13,12},{15,14},{17,16},{19,... | collective-permute-start | bytes 61448 | tf_op jit(solution)/shard_map/ppermute | solution.py:76
  170.4 3.0 %collective-permute-start.12 = (f32[2,4,16,4]{3,2,1,0:T(8,128)S(1)}, f32[2,4,16,4]{3,2,1,0:T(8,128)S(1)}, u32[]{:S(2)}, u32[]{:S(2)}) collective-permute-start(f32[2,4,16,4]{3,2,1,0:T(8,128)S(1)} %get-tuple-element.39), channel_id=1, source_target_pairs={{0,1},{2,3},{4,5},{6,7},{8,9},{10,11},{12,13},{14,15},{16,17},{18,... | collective-permute-start | bytes 6152 | tf_op jit(solution)/shard_map/ppermute | solution.py:74
  172.0 6.7 %collective-permute-start.13 = (f32[2,4,16,4]{3,2,1,0:T(8,128)S(1)}, f32[2,4,16,4]{3,2,1,0:T(8,128)S(1)}, u32[]{:S(2)}, u32[]{:S(2)}) collective-permute-start(f32[2,4,16,4]{3,2,1,0:T(8,128)S(1)} %get-tuple-element.40), channel_id=1, source_target_pairs={{1,0},{3,2},{5,4},{7,6},{9,8},{11,10},{13,12},{15,14},{17,16},{19,... | collective-permute-start | bytes 6152 | tf_op jit(solution)/shard_map/ppermute | solution.py:76
  178.7 6.4 %collective-permute-start.14 = (f32[2,4,4,72]{3,2,1,0:T(4,128)S(1)}, f32[2,4,4,72]{3,2,1,0:T(4,128)S(1)}, u32[]{:S(2)}, u32[]{:S(2)}) collective-permute-start(f32[2,4,4,72]{3,2,1,0:T(4,128)S(1)} %get-tuple-element.37), channel_id=1, source_target_pairs={{0,2},{2,4},{4,6},{6,8},{8,10},{10,12},{12,14},{14,16},{16,18},{18... | collective-permute-start | bytes 27656 | tf_op jit(solution)/shard_map/ppermute | solution.py:74
  183.1 5.1 %collective-permute-start.15 = (f32[2,4,4,72]{3,2,1,0:T(4,128)S(1)}, f32[2,4,4,72]{3,2,1,0:T(4,128)S(1)}, u32[]{:S(2)}, u32[]{:S(2)}) collective-permute-start(f32[2,4,4,72]{3,2,1,0:T(4,128)S(1)} %get-tuple-element.38), channel_id=1, source_target_pairs={{2,0},{4,2},{6,4},{8,6},{10,8},{12,10},{14,12},{16,14},{18,16},{20... | collective-permute-start | bytes 27656 | tf_op jit(solution)/shard_map/ppermute | solution.py:76
  188.3 4.9 %collective-permute-start.16 = (f32[2,4,24,72]{3,2,1,0:T(8,128)S(1)}, f32[2,4,24,72]{3,2,1,0:T(8,128)S(1)}, u32[]{:S(2)}, u32[]{:S(2)}) collective-permute-start(f32[2,4,24,72]{3,2,1,0:T(8,128)S(1)} %pad_maximum_fusion.14), channel_id=1, source_target_pairs={{0,32},{32,64},{64,96},{1,33},{33,65},{65,97},{2,34},{34,66},{66,9... | collective-permute-start | bytes 165896 | tf_op jit(solution)/shard_map/ppermute | solution.py:74
  191.6 5.4 %collective-permute-start.17 = (f32[2,4,24,72]{3,2,1,0:T(8,128)S(1)}, f32[2,4,24,72]{3,2,1,0:T(8,128)S(1)}, u32[]{:S(2)}, u32[]{:S(2)}) collective-permute-start(f32[2,4,24,72]{3,2,1,0:T(8,128)S(1)} %pad_maximum_fusion.14), channel_id=1, source_target_pairs={{32,0},{64,32},{96,64},{33,1},{65,33},{97,65},{34,2},{66,34},{98,6... | collective-permute-start | bytes 165896 | tf_op jit(solution)/shard_map/ppermute | solution.py:76
  (27 other events, 178.4 us)

commit v8 on v7

--- a/solution.py
+++ b/solution.py
@@ -128,7 +128,7 @@
     middle, middle_defect = coarser_level(middle_source, middle_damp, (("gx", 1), ("gy", 2), ("gz", 3)))
     coarse_damp = 4.0 * shrink(middle_damp)
     coarse_source = 4.0 * shrink(middle_defect)
-    coarse, coarse_defect = coarser_level(coarse_source, coarse_damp, (("gz", 3), ("gy", 2), ("gx", 1)))
+    coarse, coarse_defect = coarser_level(coarse_source, coarse_damp, (("gz", 3), ("gx", 1), ("gy", 2)))
     cells = coarse_defect.size
     digits = DIGITS
     owner = group_map.reshape(cells, 1)

time: 234 us -> 234 us (level)
  transfers between devices with their start and end apart: 18 -> 18, of which waited for: 12 -> 11; matrix products, arithmetic and copies ran while one was open for 10% -> 10% of each run, Pallas kernels for 0% -> 0%
where the time goes in v8:
time: 234 us; the launch traced here: 232 us
  other arithmetic  69.2 us (30%)
  starting transfers between devices  51 us (22%)
  waiting for transfers between devices  45.6 us (19%)
  blocking collectives  29.4 us (13%)
  local copies, waits for them, and re-layouts  25.9 us (11%)
  matrix products  8.85 us (4%)
    ppermute x9, starting transfers between devices, exchange(): lax.ppermute(tail, axis, [(i, i + 1) for i in range(count - 1)])  37.1 us
    ppermute x9, waiting for transfers between devices, exchange(): lax.ppermute(head, axis, [(i + 1, i) for i in range(count - 1)])  35.2 us
    select_n x10, other arithmetic, smooth_wide(): current = jnp.where(crop(mask, step), current, 0.0)  29.9 us
    concatenate x6, other arithmetic, exchange(): jnp.concatenate([lax.ppermute(tail, axis, [(i, i + 1) for i in range(coun...  18.7 us
    psum x2, blocking collectives, shards(): summed = lax.psum(summed, 'gy', axis_index_groups=groups)  18.2 us
    ppermute x9, starting transfers between devices, exchange(): lax.ppermute(head, axis, [(i + 1, i) for i in range(count - 1)])  13.9 us
    ppermute x9, waiting for transfers between devices, exchange(): lax.ppermute(tail, axis, [(i, i + 1) for i in range(count - 1)])  10.4 us
    slice x5, local copies, waits for them, and re-layouts, exchange(): lax.slice_in_dim(stack, stack.shape[dim] - width, stack.shape[dim], axis=...  8.68 us
  transfers between devices with their start and end apart: 18, of which 11 were waited for; matrix products, arithmetic and copies ran while one was open for 10% of the time, Pallas kernels for 0%

profile of v8, /device:TPU:1, one launch (start us, length us, event | category | flops | bytes accessed | tf_op | source)
XLA Modules:
  0.0 231.6 jit_solution(519784658766234337)
XLA Ops:
  3.7 5.5 %collective-permute-start = (f32[3,5,64,256]{3,2,1,0:T(8,128)}, f32[3,5,64,256]{3,2,1,0:T(8,128)}, u32[]{:S(2)}, u32[]{:S(2)}) collective-permute-start(f32[3,5,64,256]{3,2,1,0:T(8,128)} %get-tuple-element.25), channel_id=1, source_target_pairs={{0,32},{32,64},{64,96},{1,33},{33,65},{65,97},{2,34},{34,66},{66,9... | collective-permute-start | bytes 2949128 | tf_op jit(solution)/shard_map/ppermute | solution.py:74
  19.1 9.8 %collective-permute-done = f32[3,5,64,256]{3,2,1,0:T(8,128)} collective-permute-done((f32[3,5,64,256]{3,2,1,0:T(8,128)}, f32[3,5,64,256]{3,2,1,0:T(8,128)}, u32[]{:S(2)}, u32[]{:S(2)}) %collective-permute-start) | collective-permute-done | bytes 983072 | tf_op jit(solution)/shard_map/ppermute | solution.py:74
  29.0 4.8 %collective-permute-done.1 = f32[3,5,64,256]{3,2,1,0:T(8,128)} collective-permute-done((f32[3,5,64,256]{3,2,1,0:T(8,128)}, f32[3,5,64,256]{3,2,1,0:T(8,128)}, u32[]{:S(2)}, u32[]{:S(2)}) %collective-permute-start.1) | collective-permute-done | bytes 983072 | tf_op jit(solution)/shard_map/ppermute | solution.py:76
  36.0 4.9 %collective-permute-start.2 = (f32[3,26,5,256]{3,1,2,0:T(8,128)}, f32[3,26,5,256]{3,1,2,0:T(8,128)}, u32[]{:S(2)}, u32[]{:S(2)}) collective-permute-start(f32[3,26,5,256]{3,1,2,0:T(8,128)} %copy.63), channel_id=1, source_target_pairs={{0,2},{2,4},{4,6},{6,8},{8,10},{10,12},{12,14},{14,16},{16,18},{18... | collective-permute-start | bytes 1198088 | tf_op jit(solution)/shard_map/ppermute | solution.py:74
  48.5 3.8 %collective-permute-done.3 = f32[3,26,5,256]{3,1,2,0:T(8,128)} collective-permute-done((f32[3,26,5,256]{3,1,2,0:T(8,128)}, f32[3,26,5,256]{3,1,2,0:T(8,128)}, u32[]{:S(2)}, u32[]{:S(2)}) %collective-permute-start.3) | collective-permute-done | bytes 399392 | tf_op jit(solution)/shard_map/ppermute | solution.py:76
  56.7 3.6 %fusion.113 = (f32[3,26,74,5]{3,2,1,0:T(8,128)}, f32[3,26,74,5]{3,2,1,0:T(8,128)}) fusion(f32[3,26,74,256]{3,2,1,0:T(8,128)S(1)} %pad_maximum_fusion.1), kind=kLoop, calls=%fused_computation.269 | loop fusion | bytes 461760 | tf_op jit(solution)/shard_map/slice | solution.py:71
  60.4 3.6 %copy.67 = f32[3,26,74,5]{2,1,3,0:T(8,128)} copy(f32[3,26,74,5]{3,2,1,0:T(8,128)} %get-tuple-element.21) | data formatting | bytes 230880 | tf_op jit(solution)/shard_map/slice | solution.py:71
  64.0 5.2 %collective-permute-start.4 = (f32[3,26,74,5]{2,1,3,0:T(8,128)}, f32[3,26,74,5]{2,1,3,0:T(8,128)}, u32[]{:S(2)}, u32[]{:S(2)}) collective-permute-start(f32[3,26,74,5]{2,1,3,0:T(8,128)} %copy.67), channel_id=1, source_target_pairs={{0,1},{2,3},{4,5},{6,7},{8,9},{10,11},{12,13},{14,15},{16,17},{18,... | collective-permute-start | bytes 346328 | tf_op jit(solution)/shard_map/ppermute | solution.py:74
  84.9 15.3 %pad_maximum_fusion = f32[3,26,74,266]{3,2,1,0:T(8,128)} fusion(f32[3,26,74,5]{3,2,1,0:T(8,128)} %copy.70, f32[3,26,5,256]{3,2,1,0:T(8,128)} %copy-done.6, f32[3,5,64,256]{3,2,1,0:T(8,128)} %collective-permute-done.1, f32[1,16,64,256]{3,2,1,0:T(8,128)S(1)} %bitcast.58, f32[1,16,64,256]{3,2,1,0:T(8,128)S(1)} %bitcast.62, f32[1,16,64,256]{3,2,1,0:T(8,128)S(1)} %bitcast.66, ...), kind=kLoop, calls=%fused_computation | loop fusion | flops 12282816 | bytes 12282816 | tf_op jit(solution)/shard_map/concatenate | solution.py:72
  100.2 4.5 %fusion = (f32[26,74,266]{2,1,0:T(8,128)S(1)}, f32[26,74,266]{2,1,0:T(8,128)S(1)}, f32[26,74,266]{2,1,0:T(8,128)S(1)}) fusion(f32[3,26,74,266]{3,2,1,0:T(8,128)} %pad_maximum_fusion), kind=kLoop, calls=%fused_computation.3 | loop fusion | flops 511784 | bytes 12282816 | tf_op jit(solution)/shard_map/add | solution.py:121
  104.7 7.2 %fusion.6 = f32[24,72,264]{2,1,0:T(8,128)S(1)} fusion(f32[26,74,266]{2,1,0:T(8,128)S(1)} %get-tuple-element.20, f32[26,74,266]{2,1,0:T(8,128)S(1)} %get-tuple-element.19, f32[26,74,266]{2,1,0:T(8,128)S(1)} %get-tuple-element.18, pred[26,74,266]{2,1,0:T(8,128)(4,1)S(1)} %copy-done.4), kind=kLoop, calls=%fused_computation.12 | loop fusion | flops 5474304 | bytes 18703872 | tf_op jit(solution)/shard_map/jit(_where)/select_n | solution.py:102
  111.9 6.8 %fusion.12 = f32[22,70,262]{2,1,0:T(8,128)S(1)} fusion(f32[24,72,264]{2,1,0:T(8,128)S(1)} %fusion.6, f32[26,74,266]{2,1,0:T(8,128)S(1)} %get-tuple-element.19, f32[26,74,266]{2,1,0:T(8,128)S(1)} %get-tuple-element.18, pred[26,74,266]{2,1,0:T(8,128)(4,1)S(1)} %copy-done.4), kind=kLoop, calls=%fused_computation.23 | loop fusion | flops 4841760 | bytes 16542680 | tf_op jit(solution)/shard_map/jit(_where)/select_n | solution.py:102
  118.7 6.0 %fusion.18 = f32[20,68,260]{2,1,0:T(8,128)S(1)} fusion(f32[22,70,262]{2,1,0:T(8,128)S(1)} %fusion.12, f32[26,74,266]{2,1,0:T(8,128)S(1)} %get-tuple-element.19, f32[26,74,266]{2,1,0:T(8,128)S(1)} %get-tuple-element.18, pred[26,74,266]{2,1,0:T(8,128)(4,1)S(1)} %copy-done.4), kind=kLoop, calls=%fused_computation.34 | loop fusion | flops 4243200 | bytes 14497600 | tf_op jit(solution)/shard_map/jit(_where)/select_n | solution.py:102
  124.7 5.4 %fusion.24 = f32[18,66,258]{2,1,0:T(8,128)S(1)} fusion(f32[20,68,260]{2,1,0:T(8,128)S(1)} %fusion.18, f32[26,74,266]{2,1,0:T(8,128)S(1)} %get-tuple-element.19, f32[26,74,266]{2,1,0:T(8,128)S(1)} %get-tuple-element.18, pred[26,74,266]{2,1,0:T(8,128)(4,1)S(1)} %copy-done.4), kind=kLoop, calls=%fused_computation.45 | loop fusion | flops 3678048 | bytes 12566664 | tf_op jit(solution)/shard_map/jit(_where)/select_n | solution.py:102
  138.4 3.8 %collective-permute-done.7 = f32[2,4,32,128]{3,2,1,0:T(8,128)S(1)} collective-permute-done((f32[2,4,32,128]{3,2,1,0:T(8,128)S(1)}, f32[2,4,32,128]{3,2,1,0:T(8,128)S(1)}, u32[]{:S(2)}, u32[]{:S(2)}) %collective-permute-start.7) | collective-permute-done | bytes 131104 | tf_op jit(solution)/shard_map/ppermute | solution.py:76
  142.3 6.3 %collective-permute-start.8 = (f32[2,16,4,128]{3,2,1,0:T(4,128)S(1)}, f32[2,16,4,128]{3,2,1,0:T(4,128)S(1)}, u32[]{:S(2)}, u32[]{:S(2)}) collective-permute-start(f32[2,16,4,128]{3,2,1,0:T(4,128)S(1)} %get-tuple-element.31), channel_id=1, source_target_pairs={{0,2},{2,4},{4,6},{6,8},{8,10},{10,12},{12,14},{14,16},{16,18},{18... | collective-permute-start | bytes 196616 | tf_op jit(solution)/shard_map/ppermute | solution.py:74
  158.3 4.9 %collective-permute-done.11 = f32[2,16,40,4]{2,1,3,0:T(8,128)S(1)} collective-permute-done((f32[2,16,40,4]{2,1,3,0:T(8,128)S(1)}, f32[2,16,40,4]{2,1,3,0:T(8,128)S(1)}, u32[]{:S(2)}, u32[]{:S(2)}) %collective-permute-start.11) | collective-permute-done | bytes 20512 | tf_op jit(solution)/shard_map/ppermute | solution.py:76
  173.3 5.3 %collective-permute-done.13 = f32[2,4,16,4]{3,2,1,0:T(8,128)S(1)} collective-permute-done((f32[2,4,16,4]{3,2,1,0:T(8,128)S(1)}, f32[2,4,16,4]{3,2,1,0:T(8,128)S(1)}, u32[]{:S(2)}, u32[]{:S(2)}) %collective-permute-start.13) | collective-permute-done | bytes 2080 | tf_op jit(solution)/shard_map/ppermute | solution.py:76
  183.3 3.7 %collective-permute-done.15 = f32[2,4,16,72]{3,2,1,0:T(8,128)S(1)} collective-permute-done((f32[2,4,16,72]{3,2,1,0:T(8,128)S(1)}, f32[2,4,16,72]{3,2,1,0:T(8,128)S(1)}, u32[]{:S(2)}, u32[]{:S(2)}) %collective-permute-start.15) | collective-permute-done | bytes 36896 | tf_op jit(solution)/shard_map/ppermute | solution.py:76
  187.1 6.2 %collective-permute-start.16 = (f32[2,12,4,72]{3,2,1,0:T(4,128)S(1)}, f32[2,12,4,72]{3,2,1,0:T(4,128)S(1)}, u32[]{:S(2)}, u32[]{:S(2)}) collective-permute-start(f32[2,12,4,72]{3,2,1,0:T(4,128)S(1)} %get-tuple-element.33), channel_id=1, source_target_pairs={{0,2},{2,4},{4,6},{6,8},{8,10},{10,12},{12,14},{14,16},{16,18},{18... | collective-permute-start | bytes 82952 | tf_op jit(solution)/shard_map/ppermute | solution.py:74
  201.3 5.3 %psum.28 = f32[1024]{0:T(1024)S(1)} all-reduce(f32[1024]{0:T(1024)S(1)} %reshape.365), channel_id=1, replica_groups=mesh['gx'=4,'gy'=16,'gz'=2] {'gz'}, use_global_device_ids=true, to_apply=%region_0.1 | all-reduce | flops 1024 | bytes 8192 | tf_op jit(solution)/shard_map/psum | solution.py:141
  206.6 6.0 %psum.29 = f32[1024]{0:T(1024)S(1)} all-reduce(f32[1024]{0:T(1024)S(1)} %psum.28), channel_id=1, replica_groups=mesh['gx'=4,'gy'=16,'gz'=2] {'gx'}, use_global_device_ids=true, to_apply=%region_1.2 | all-reduce | flops 1024 | bytes 8192 | tf_op jit(solution)/shard_map/psum | solution.py:142
  212.5 8.2 %psum.30 = f32[1024]{0:T(1024)S(1)} all-reduce(f32[1024]{0:T(1024)S(1)} %psum.29), channel_id=1, replica_groups={{0,2,4,6},{8,10,12,14},{16,18,20,22},{24,26,28,30},{1,3,5,7},{9,11,13,1..., use_global_device_ids=true, to_apply=%region_2.3 | all-reduce | flops 1024 | bytes 8192 | tf_op jit(solution)/shard_map/psum | solution.py:150
  220.7 10.0 %psum.31 = f32[1024]{0:T(1024)S(1)} all-reduce(f32[1024]{0:T(1024)S(1)} %psum.30), channel_id=1, replica_groups={{0,8,16,24},{2,10,18,26},{4,12,20,28},{6,14,22,30},{1,9,17,25},{3,11,19..., use_global_device_ids=true, to_apply=%region_3.4 | all-reduce | flops 1024 | bytes 8192 | tf_op jit(solution)/shard_map/psum | solution.py:150
  (166 shorter events, 84.1 us)
Async XLA Ops:
  0.6 230.1 %copy-start = (f32[64,1024]{1,0:T(8,128)S(1)}, f32[64,1024]{1,0:T(8,128)}, u32[]{:S(2)}) copy-start(f32[64,1024]{1,0:T(8,128)} %param.9) | copy-start | bytes 786436
  3.7 30.1 %copy-start.2 = (f32[16,64,256]{2,1,0:T(8,128)S(1)}, f32[16,64,256]{2,1,0:T(8,128)}, u32[]{:S(2)}) copy-start(f32[16,64,256]{2,1,0:T(8,128)} %param.5) | copy-start | bytes 3145732
  3.7 30.1 %copy-start.3 = (f32[16,64,256]{2,1,0:T(8,128)S(1)}, f32[16,64,256]{2,1,0:T(8,128)}, u32[]{:S(2)}) copy-start(f32[16,64,256]{2,1,0:T(8,128)} %param.6) | copy-start | bytes 3145732
  3.7 25.2 %collective-permute-start = (f32[3,5,64,256]{3,2,1,0:T(8,128)}, f32[3,5,64,256]{3,2,1,0:T(8,128)}, u32[]{:S(2)}, u32[]{:S(2)}) collective-permute-start(f32[3,5,64,256]{3,2,1,0:T(8,128)} %get-tuple-element.25), channel_id=1, source_target_pairs={{0,32},{32,64},{64,96},{1,33},{33,65},{65,97},{2,34},{34,66},{66,9... | collective-permute-start | bytes 2949128 | tf_op jit(solution)/shard_map/ppermute | solution.py:74
  9.2 24.6 %collective-permute-start.1 = (f32[3,5,64,256]{3,2,1,0:T(8,128)}, f32[3,5,64,256]{3,2,1,0:T(8,128)}, u32[]{:S(2)}, u32[]{:S(2)}) collective-permute-start(f32[3,5,64,256]{3,2,1,0:T(8,128)} %get-tuple-element.26), channel_id=1, source_target_pairs={{32,0},{64,32},{96,64},{33,1},{65,33},{97,65},{34,2},{66,34},{98,6... | collective-permute-start | bytes 2949128 | tf_op jit(solution)/shard_map/ppermute | solution.py:76
  10.6 24.4 %copy-start.17 = (s32[256]{0:T(256)}, s32[256]{0:T(256)S(1)}, u32[]{:S(2)}) copy-start(s32[256]{0:T(256)S(1)} %get-tuple-element.49) | copy-start | bytes 3076
  19.1 24.6 %copy-start.31 = (pred[74]{0:T(512)(128)(4,1)S(1)}, pred[74]{0:T(512)(128)(4,1)}, u32[]{:S(2)}) copy-start(pred[74]{0:T(512)(128)(4,1)} %compare_and_fusion.8) | copy-start | bytes 226
  19.1 24.6 %copy-start.32 = (pred[26]{0:T(512)(128)(4,1)S(1)}, pred[26]{0:T(512)(128)(4,1)}, u32[]{:S(2)}) copy-start(pred[26]{0:T(512)(128)(4,1)} %compare_and_fusion.9) | copy-start | bytes 82
  36.0 11.2 %collective-permute-start.2 = (f32[3,26,5,256]{3,1,2,0:T(8,128)}, f32[3,26,5,256]{3,1,2,0:T(8,128)}, u32[]{:S(2)}, u32[]{:S(2)}) collective-permute-start(f32[3,26,5,256]{3,1,2,0:T(8,128)} %copy.63), channel_id=1, source_target_pairs={{0,2},{2,4},{4,6},{6,8},{8,10},{10,12},{12,14},{14,16},{16,18},{18... | collective-permute-start | bytes 1198088 | tf_op jit(solution)/shard_map/ppermute | solution.py:74
  41.8 10.5 %collective-permute-start.3 = (f32[3,26,5,256]{3,1,2,0:T(8,128)}, f32[3,26,5,256]{3,1,2,0:T(8,128)}, u32[]{:S(2)}, u32[]{:S(2)}) collective-permute-start(f32[3,26,5,256]{3,1,2,0:T(8,128)} %copy.64), channel_id=1, source_target_pairs={{2,0},{4,2},{6,4},{8,6},{10,8},{12,10},{14,12},{16,14},{18,16},{20... | collective-permute-start | bytes 1198088 | tf_op jit(solution)/shard_map/ppermute | solution.py:76
  64.0 11.9 %collective-permute-start.4 = (f32[3,26,74,5]{2,1,3,0:T(8,128)}, f32[3,26,74,5]{2,1,3,0:T(8,128)}, u32[]{:S(2)}, u32[]{:S(2)}) collective-permute-start(f32[3,26,74,5]{2,1,3,0:T(8,128)} %copy.67), channel_id=1, source_target_pairs={{0,1},{2,3},{4,5},{6,7},{8,9},{10,11},{12,13},{14,15},{16,17},{18,... | collective-permute-start | bytes 346328 | tf_op jit(solution)/shard_map/ppermute | solution.py:74
  72.8 8.8 %collective-permute-start.5 = (f32[3,26,74,5]{2,1,3,0:T(8,128)}, f32[3,26,74,5]{2,1,3,0:T(8,128)}, u32[]{:S(2)}, u32[]{:S(2)}) collective-permute-start(f32[3,26,74,5]{2,1,3,0:T(8,128)} %copy.68), channel_id=1, source_target_pairs={{1,0},{3,2},{5,4},{7,6},{9,8},{11,10},{13,12},{15,14},{17,16},{19,... | collective-permute-start | bytes 346328 | tf_op jit(solution)/shard_map/ppermute | solution.py:76
  134.0 4.5 %collective-permute-start.6 = (f32[2,4,32,128]{3,2,1,0:T(8,128)S(1)}, f32[2,4,32,128]{3,2,1,0:T(8,128)S(1)}, u32[]{:S(2)}, u32[]{:S(2)}) collective-permute-start(f32[2,4,32,128]{3,2,1,0:T(8,128)S(1)} %get-tuple-element.37), channel_id=1, source_target_pairs={{0,32},{32,64},{64,96},{1,33},{33,65},{65,97},{2,34},{34,66},{66,9... | collective-permute-start | bytes 393224 | tf_op jit(solution)/shard_map/ppermute | solution.py:74
  136.5 5.7 %collective-permute-start.7 = (f32[2,4,32,128]{3,2,1,0:T(8,128)S(1)}, f32[2,4,32,128]{3,2,1,0:T(8,128)S(1)}, u32[]{:S(2)}, u32[]{:S(2)}) collective-permute-start(f32[2,4,32,128]{3,2,1,0:T(8,128)S(1)} %get-tuple-element.38), channel_id=1, source_target_pairs={{32,0},{64,32},{96,64},{33,1},{65,33},{97,65},{34,2},{66,34},{98,6... | collective-permute-start | bytes 393224 | tf_op jit(solution)/shard_map/ppermute | solution.py:76
  142.3 8.5 %collective-permute-start.8 = (f32[2,16,4,128]{3,2,1,0:T(4,128)S(1)}, f32[2,16,4,128]{3,2,1,0:T(4,128)S(1)}, u32[]{:S(2)}, u32[]{:S(2)}) collective-permute-start(f32[2,16,4,128]{3,2,1,0:T(4,128)S(1)} %get-tuple-element.31), channel_id=1, source_target_pairs={{0,2},{2,4},{4,6},{6,8},{8,10},{10,12},{12,14},{14,16},{16,18},{18... | collective-permute-start | bytes 196616 | tf_op jit(solution)/shard_map/ppermute | solution.py:74
  148.5 5.6 %collective-permute-start.9 = (f32[2,16,4,128]{3,2,1,0:T(4,128)S(1)}, f32[2,16,4,128]{3,2,1,0:T(4,128)S(1)}, u32[]{:S(2)}, u32[]{:S(2)}) collective-permute-start(f32[2,16,4,128]{3,2,1,0:T(4,128)S(1)} %get-tuple-element.32), channel_id=1, source_target_pairs={{2,0},{4,2},{6,4},{8,6},{10,8},{12,10},{14,12},{16,14},{18,16},{20... | collective-permute-start | bytes 196616 | tf_op jit(solution)/shard_map/ppermute | solution.py:76
  154.7 3.2 %collective-permute-start.10 = (f32[2,16,40,4]{2,1,3,0:T(8,128)S(1)}, f32[2,16,40,4]{2,1,3,0:T(8,128)S(1)}, u32[]{:S(2)}, u32[]{:S(2)}) collective-permute-start(f32[2,16,40,4]{2,1,3,0:T(8,128)S(1)} %copy.71), channel_id=1, source_target_pairs={{0,1},{2,3},{4,5},{6,7},{8,9},{10,11},{12,13},{14,15},{16,17},{18,... | collective-permute-start | bytes 61448 | tf_op jit(solution)/shard_map/ppermute | solution.py:74
  156.6 6.5 %collective-permute-start.11 = (f32[2,16,40,4]{2,1,3,0:T(8,128)S(1)}, f32[2,16,40,4]{2,1,3,0:T(8,128)S(1)}, u32[]{:S(2)}, u32[]{:S(2)}) collective-permute-start(f32[2,16,40,4]{2,1,3,0:T(8,128)S(1)} %copy.72), channel_id=1, source_target_pairs={{1,0},{3,2},{5,4},{7,6},{9,8},{11,10},{13,12},{15,14},{17,16},{19,... | collective-permute-start | bytes 61448 | tf_op jit(solution)/shard_map/ppermute | solution.py:76
  170.4 3.0 %collective-permute-start.12 = (f32[2,4,16,4]{3,2,1,0:T(8,128)S(1)}, f32[2,4,16,4]{3,2,1,0:T(8,128)S(1)}, u32[]{:S(2)}, u32[]{:S(2)}) collective-permute-start(f32[2,4,16,4]{3,2,1,0:T(8,128)S(1)} %get-tuple-element.39), channel_id=1, source_target_pairs={{0,1},{2,3},{4,5},{6,7},{8,9},{10,11},{12,13},{14,15},{16,17},{18,... | collective-permute-start | bytes 6152 | tf_op jit(solution)/shard_map/ppermute | solution.py:74
  172.0 6.7 %collective-permute-start.13 = (f32[2,4,16,4]{3,2,1,0:T(8,128)S(1)}, f32[2,4,16,4]{3,2,1,0:T(8,128)S(1)}, u32[]{:S(2)}, u32[]{:S(2)}) collective-permute-start(f32[2,4,16,4]{3,2,1,0:T(8,128)S(1)} %get-tuple-element.40), channel_id=1, source_target_pairs={{1,0},{3,2},{5,4},{7,6},{9,8},{11,10},{13,12},{15,14},{17,16},{19,... | collective-permute-start | bytes 6152 | tf_op jit(solution)/shard_map/ppermute | solution.py:76
  178.7 4.6 %collective-permute-start.14 = (f32[2,4,16,72]{3,2,1,0:T(8,128)S(1)}, f32[2,4,16,72]{3,2,1,0:T(8,128)S(1)}, u32[]{:S(2)}, u32[]{:S(2)}) collective-permute-start(f32[2,4,16,72]{3,2,1,0:T(8,128)S(1)} %pad_maximum_fusion.19), channel_id=1, source_target_pairs={{0,32},{32,64},{64,96},{1,33},{33,65},{65,97},{2,34},{34,66},{66,9... | collective-permute-start | bytes 110600 | tf_op jit(solution)/shard_map/ppermute | solution.py:74
  182.0 5.0 %collective-permute-start.15 = (f32[2,4,16,72]{3,2,1,0:T(8,128)S(1)}, f32[2,4,16,72]{3,2,1,0:T(8,128)S(1)}, u32[]{:S(2)}, u32[]{:S(2)}) collective-permute-start(f32[2,4,16,72]{3,2,1,0:T(8,128)S(1)} %pad_maximum_fusion.19), channel_id=1, source_target_pairs={{32,0},{64,32},{96,64},{33,1},{65,33},{97,65},{34,2},{66,34},{98,6... | collective-permute-start | bytes 110600 | tf_op jit(solution)/shard_map/ppermute | solution.py:76
  187.1 8.3 %collective-permute-start.16 = (f32[2,12,4,72]{3,2,1,0:T(4,128)S(1)}, f32[2,12,4,72]{3,2,1,0:T(4,128)S(1)}, u32[]{:S(2)}, u32[]{:S(2)}) collective-permute-start(f32[2,12,4,72]{3,2,1,0:T(4,128)S(1)} %get-tuple-element.33), channel_id=1, source_target_pairs={{0,2},{2,4},{4,6},{6,8},{8,10},{10,12},{12,14},{14,16},{16,18},{18... | collective-permute-start | bytes 82952 | tf_op jit(solution)/shard_map/ppermute | solution.py:74
  193.4 5.4 %collective-permute-start.17 = (f32[2,12,4,72]{3,2,1,0:T(4,128)S(1)}, f32[2,12,4,72]{3,2,1,0:T(4,128)S(1)}, u32[]{:S(2)}, u32[]{:S(2)}) collective-permute-start(f32[2,12,4,72]{3,2,1,0:T(4,128)S(1)} %get-tuple-element.34), channel_id=1, source_target_pairs={{2,0},{4,2},{6,4},{8,6},{10,8},{12,10},{14,12},{16,14},{18,16},{20... | collective-permute-start | bytes 82952 | tf_op jit(solution)/shard_map/ppermute | solution.py:76
  (27 other events, 181.4 us)
